TPU v7x, 1024 devices: a whole 4x4x32 slice. The times are simulated.
1024 devices in a mesh: space: 64 (over y, z_lo), chan: 16 (over z_hi, x, core).
Axes of the slice: x: 4, y: 4, z: 32 (z_hi: 2, z_lo: 16; z = z_hi * 16 + z_lo), core: 2. Of those that a mesh axis runs over, the one named last changes fastest.
Arguments:
- latent: bfloat16 [2, 64, 32, 1024], P(None, 'space', None, 'chan'), may hold values from -6 to 6
- conv_one: bfloat16 [27, 1024, 1024], P(None, None, 'chan'), may hold values from -0.0390625 to 0.0390625
- bias_one: float32 [1024], P('chan'), may hold values from -3 to 3
- conv_two: bfloat16 [27, 1024, 1024], P(None, 'chan'), may hold values from -0.0546875 to 0.0546875
- bias_two: float32 [1024], P('chan'), may hold values from -3 to 3
Outputs:
- block_out: bfloat16 [2, 64, 32, 1024], P(None, 'space', None, 'chan')
All inputs are finite; a program needn't handle non-finite values.
Results may differ from a plain program's by a relative error of at most 0.0034.
Values may be sent and summed in bfloat16 or wider, within the bound.
No kernel may reach another device: no remote copies, remote signals or barrier semaphores. Data moves between devices by JAX's collectives and lax.ppermute only.
A program may use at most 32 MiB of HBM per device.

v0:
```python
import jax
import jax.numpy as jnp
from jax import lax
from jax.sharding import PartitionSpec as P


def padded_2(cells, sides, width):
    for axis, dim in sides:
        count = lax.axis_size(axis)
        ends = count - 1
        head = lax.slice_in_dim(cells, 0, width, axis=dim)
        tail = lax.slice_in_dim(cells, cells.shape[dim] - width, cells.shape[dim], axis=dim)
        cells = jnp.concatenate(
            [
                lax.ppermute(tail, axis, [(i, (i + 1) % count) for i in range(ends)]),
                cells,
                lax.ppermute(head, axis, [((i + 1) % count, i) for i in range(ends)]),
            ],
            axis=dim,
        )
    return cells


def pad_sides(values):
    return jnp.pad(values, ((1, 1), (0, 0), (1, 1), (0, 0)))


def tap_windows(padded, frame_count, row_count, col_count):
    windows = []
    for depth_off in range(3):
        for row_off in range(3):
            for col_off in range(3):
                window = padded[
                    depth_off : depth_off + frame_count,
                    row_off : row_off + row_count,
                    col_off : col_off + col_count,
                ]
                windows.append(window.reshape(frame_count * row_count * col_count, padded.shape[3]))
    return windows


def tap_sum(padded, kernel, frame_count, row_count, col_count):
    accum = None
    for tap_index, flat in enumerate(tap_windows(padded, frame_count, row_count, col_count)):
        term = jnp.dot(flat, kernel[tap_index], preferred_element_type=jnp.float32)
        accum = term if accum is None else accum + term
    return accum


def local(latent, conv_one, bias_one, conv_two, bias_two):
    frame_count, row_count, col_count, own_chan = latent.shape
    gathered = lax.all_gather(latent, "chan", axis=3, tiled=True)
    extended = padded_2(gathered, (("space", 1),), 1)
    first = tap_sum(pad_sides(extended), conv_one, frame_count, row_count, col_count)
    hidden = jax.nn.relu(first + bias_one).astype(jnp.bfloat16)
    hidden = hidden.reshape(frame_count, row_count, col_count, own_chan)
    hidden_ext = padded_2(hidden, (("space", 1),), 1)
    columns = jnp.concatenate(
        tap_windows(pad_sides(hidden_ext), frame_count, row_count, col_count), axis=1
    )
    flat_two = conv_two.reshape(27 * own_chan, conv_two.shape[2])
    mine = lax.psum_scatter(
        lax.dot_general(
            flat_two, columns, (((0,), (1,)), ((), ())), preferred_element_type=jnp.float32
        ),
        "chan",
        scatter_dimension=0,
        tiled=True,
    )
    second = mine.T.reshape(frame_count, row_count, col_count, own_chan)
    summed = latent.astype(jnp.float32) + second + bias_two
    return summed.astype(jnp.bfloat16)


def solution(mesh):
    in_specs = (
        P(None, "space", None, "chan"),
        P(None, None, "chan"),
        P("chan"),
        P(None, "chan", None),
        P("chan"),
    )
    out_specs = P(None, "space", None, "chan")
    return jax.shard_map(local, mesh=mesh, in_specs=in_specs, out_specs=out_specs, check_vma=False)
```

profile of v0, /device:TPU:24, one launch (start us, length us, event | category | flops | bytes accessed | tf_op | source)
XLA Modules:
  0.0 314.5 jit_solution(10981507040637839587)
XLA Ops:
  6.5 1.6 copy.9
  8.1 91.8 %all_gather.3 = bf16[2,1,32,1024]{2,0,1,3:T(2,128)(2,1)} all-gather(bf16[2,1,32,64]{2,0,1,3:T(2,128)(2,1)} %copy.9), channel_id=1, replica_groups=mesh['space'=64,'chan'=16] {'chan'}, dimensions={3}, use_global_device_ids=true | all-gather | bytes 139264 | tf_op jit(solution)/shard_map/all_gather | solution.py:52
  99.9 1.9 copy.10
  101.7 4.8 %collective-permute-start.1 = (bf16[2,1,32,1024]{3,2,0,1:T(8,128)(2,1)}, bf16[2,1,32,1024]{3,2,0,1:T(8,128)(2,1)S(1)}, u32[]{:S(2)}, u32[]{:S(2)}) collective-permute-start(bf16[2,1,32,1024]{3,2,0,1:T(8,128)(2,1)} %copy.10), channel_id=1, source_target_pairs={{16,0},{32,16},{48,32},{64,48},{80,64},{96,80},{112,96},{128,112},... | collective-permute-start | bytes 393224 | tf_op jit(solution)/shard_map/ppermute | solution.py:17
  106.5 1.9 collective-permute-start
  108.4 2.3 collective-permute-done.1
  110.7 20.7 %collective-permute-done = bf16[2,1,32,1024]{3,2,0,1:T(8,128)(2,1)S(1)} collective-permute-done((bf16[2,1,32,1024]{3,2,0,1:T(8,128)(2,1)}, bf16[2,1,32,1024]{3,2,0,1:T(8,128)(2,1)S(1)}, u32[]{:S(2)}, u32[]{:S(2)}) %collective-permute-start) | collective-permute-done | bytes 131104 | tf_op jit(solution)/shard_map/ppermute | solution.py:15
  131.4 1.1 select_maximum_fusion
  132.6 0.5 fusion.74
  133.8 0.2 convolution_add_fusion.22
  134.0 0.2 convolution_add_fusion.21
  134.4 0.2 convolution_add_fusion.19
  134.7 0.2 convolution_add_fusion.17
  135.1 0.2 convolution_add_fusion.15
  135.3 0.2 fusion.5
  136.0 0.2 convolution_add_fusion.10
  136.2 0.2 fusion.4
  136.4 0.2 convolution_add_fusion.8
  136.6 0.2 convolution_add_fusion.7
  136.9 0.2 convolution_add_fusion.5
  137.8 0.2 fusion.7
  138.0 1.9 collective-permute-start.3
  140.0 3.9 %collective-permute-start.2 = (bf16[2,1,32,64]{3,2,0,1:T(8,128)(2,1)S(1)}, bf16[2,1,32,64]{3,2,0,1:T(8,128)(2,1)S(1)}, u32[]{:S(2)}, u32[]{:S(2)}) collective-permute-start(bf16[2,1,32,64]{3,2,0,1:T(8,128)(2,1)S(1)} %bitcast.202), channel_id=1, source_target_pairs={{0,16},{16,32},{32,48},{48,64},{64,80},{80,96},{96,112},{112,128},... | collective-permute-start | bytes 24584 | tf_op jit(solution)/shard_map/ppermute | solution.py:15
  143.9 18.8 %collective-permute-done.2 = bf16[2,1,32,64]{3,2,0,1:T(8,128)(2,1)S(1)} collective-permute-done((bf16[2,1,32,64]{3,2,0,1:T(8,128)(2,1)S(1)}, bf16[2,1,32,64]{3,2,0,1:T(8,128)(2,1)S(1)}, u32[]{:S(2)}, u32[]{:S(2)}) %collective-permute-start.2) | collective-permute-done | bytes 8224 | tf_op jit(solution)/shard_map/ppermute | solution.py:15
  162.7 0.6 fusion.77
  163.4 0.7 fusion.76
  164.2 1.8 concatenate.11
  166.0 2.4 convolution_bitcast_fusion
  168.4 1.9 copy.15
  170.3 134.5 %reduce-scatter.4.cloned.1.call-done = f32[64,64]{1,0:T(8,128)} async-done(((f32[1024,64]{1,0:T(8,128)}), f32[64,64]{1,0:T(8,128)}) %reduce-scatter.4.cloned.1.call-update) | async-done | bytes 16400
  304.8 1.4 copy.16
  306.2 1.4 add_convert_fusion
  (34 shorter events, 2.8 us)
Async XLA Ops:
  6.5 159.4 %copy-start = (bf16[27,64,1024]{2,1,0:T(8,128)(2,1)S(1)}, bf16[27,64,1024]{2,1,0:T(8,128)(2,1)}, u32[]{:S(2)}) copy-start(bf16[27,64,1024]{2,1,0:T(8,128)(2,1)} %param.8) | copy-start | bytes 10616836
  6.5 298.3 %reduce-scatter.4.cloned.1.call-start = ((), (), s32[]{:S(2)}) async-start(), calls=%async_computation.1 | async-start | bytes 557056
  101.7 31.4 %copy-start.1 = (bf16[27,1024,64]{1,2,0:T(8,128)(2,1)S(1)}, bf16[27,1024,64]{1,2,0:T(8,128)(2,1)}, u32[]{:S(2)}) copy-start(bf16[27,1024,64]{1,2,0:T(8,128)(2,1)} %param.6) | copy-start | bytes 10616836
  101.7 9.0 %collective-permute-start.1 = (bf16[2,1,32,1024]{3,2,0,1:T(8,128)(2,1)}, bf16[2,1,32,1024]{3,2,0,1:T(8,128)(2,1)S(1)}, u32[]{:S(2)}, u32[]{:S(2)}) collective-permute-start(bf16[2,1,32,1024]{3,2,0,1:T(8,128)(2,1)} %copy.10), channel_id=1, source_target_pairs={{16,0},{32,16},{48,32},{64,48},{80,64},{96,80},{112,96},{128,112},... | collective-permute-start | bytes 393224 | tf_op jit(solution)/shard_map/ppermute | solution.py:17
  106.5 24.9 %collective-permute-start = (bf16[2,1,32,1024]{3,2,0,1:T(8,128)(2,1)}, bf16[2,1,32,1024]{3,2,0,1:T(8,128)(2,1)S(1)}, u32[]{:S(2)}, u32[]{:S(2)}) collective-permute-start(bf16[2,1,32,1024]{3,2,0,1:T(8,128)(2,1)} %copy.10), channel_id=1, source_target_pairs={{0,16},{16,32},{32,48},{48,64},{64,80},{80,96},{96,112},{112,128},... | collective-permute-start | bytes 393224 | tf_op jit(solution)/shard_map/ppermute | solution.py:15
  132.6 3.1 copy-start.2
  134.0 3.8 %copy-start.6 = (f32[64]{0:T(128)S(1)}, f32[64]{0:T(128)}, u32[]{:S(2)}) copy-start(f32[64]{0:T(128)} %param.7) | copy-start | bytes 772
  138.0 5.9 %collective-permute-start.3 = (bf16[2,1,32,64]{3,2,0,1:T(8,128)(2,1)S(1)}, bf16[2,1,32,64]{3,2,0,1:T(8,128)(2,1)S(1)}, u32[]{:S(2)}, u32[]{:S(2)}) collective-permute-start(bf16[2,1,32,64]{3,2,0,1:T(8,128)(2,1)S(1)} %bitcast.201), channel_id=1, source_target_pairs={{16,0},{32,16},{48,32},{64,48},{80,64},{96,80},{112,96},{128,112},... | collective-permute-start | bytes 24584 | tf_op jit(solution)/shard_map/ppermute | solution.py:17
  140.0 22.7 %collective-permute-start.2 = (bf16[2,1,32,64]{3,2,0,1:T(8,128)(2,1)S(1)}, bf16[2,1,32,64]{3,2,0,1:T(8,128)(2,1)S(1)}, u32[]{:S(2)}, u32[]{:S(2)}) collective-permute-start(bf16[2,1,32,64]{3,2,0,1:T(8,128)(2,1)S(1)} %bitcast.202), channel_id=1, source_target_pairs={{0,16},{16,32},{32,48},{48,64},{64,80},{80,96},{96,112},{112,128},... | collective-permute-start | bytes 24584 | tf_op jit(solution)/shard_map/ppermute | solution.py:15
  143.9 20.2 %copy-start.4 = (bf16[2,1,32,64]{3,2,0,1:T(8,128)(2,1)}, bf16[2,1,32,64]{3,2,0,1:T(8,128)(2,1)S(1)}, u32[]{:S(2)}) copy-start(bf16[2,1,32,64]{3,2,0,1:T(8,128)(2,1)S(1)} %collective-permute-done.3) | copy-start | bytes 24580
  162.7 1.4 copy-start.5
  166.0 140.3 %copy-start.3 = (bf16[2,1,32,64]{3,2,1,0:T(8,128)(2,1)S(1)}, bf16[2,1,32,64]{3,2,1,0:T(8,128)(2,1)}, u32[]{:S(2)}) copy-start(bf16[2,1,32,64]{3,2,1,0:T(8,128)(2,1)} %param.5) | copy-start | bytes 24580
Sparse Core Ops, SparseCore 0:
  170.5 134.2 reduce-scatter.3
where the time goes:
time: 315 us; the launch traced here: 314 us
  waiting for transfers between devices  176 us (56%)
  blocking collectives  91.8 us (29%)
  between operations  13.7 us (4%)
  starting transfers between devices  12.5 us (4%)
  local copies, waits for them, and re-layouts  10.6 us (3%)
  matrix products  7.1 us (2%)
    unnamed x2, waiting for transfers between devices  134 us
    all_gather x1, blocking collectives, local(): gathered = lax.all_gather(latent, 'chan', axis=3, tiled=True)  91.8 us
    ppermute x2, waiting for transfers between devices, padded_2(): lax.ppermute(tail, axis, [(i, (i + 1) % count) for i in range(ends)])  39.5 us
    ppermute x2, starting transfers between devices, padded_2(): lax.ppermute(head, axis, [((i + 1) % count, i) for i in range(ends)])  6.69 us
  transfers between devices with their start and end apart: 5, of which 4 were waited for; matrix products, arithmetic and copies ran while one was open for 0% of the time, Pallas kernels for 0%

commit v1 on v0

v1 whole, which is shorter than its diff:
```python
import jax
import jax.numpy as jnp
from jax import lax
from jax.sharding import Mesh
from jax.sharding import PartitionSpec as P

CHAN = ("zh", "inner")
HALVES = 2


def halo_rows(cells, dim):
    count = lax.axis_size("space")
    ends = count - 1
    head = lax.slice_in_dim(cells, 0, 1, axis=dim)
    tail = lax.slice_in_dim(cells, cells.shape[dim] - 1, cells.shape[dim], axis=dim)
    return jnp.concatenate(
        [
            lax.ppermute(tail, "space", [(i, (i + 1) % count) for i in range(ends)]),
            cells,
            lax.ppermute(head, "space", [((i + 1) % count, i) for i in range(ends)]),
        ],
        axis=dim,
    )


def swap_halves(v):
    return lax.ppermute(v, "zh", [(0, 1), (1, 0)])


def pad_sides(values):
    return jnp.pad(values, ((1, 1), (0, 0), (1, 1), (0, 0)))


def tap_windows(padded, frame_count, row_count, col_count):
    windows = []
    for depth_off in range(3):
        for row_off in range(3):
            for col_off in range(3):
                window = padded[
                    depth_off : depth_off + frame_count,
                    row_off : row_off + row_count,
                    col_off : col_off + col_count,
                ]
                windows.append(window.reshape(frame_count * row_count * col_count, padded.shape[3]))
    return windows


def tap_sum(padded, kernel, frame_count, row_count, col_count):
    accum = None
    for tap_index, flat in enumerate(tap_windows(padded, frame_count, row_count, col_count)):
        term = jnp.dot(flat, kernel[tap_index], preferred_element_type=jnp.float32)
        accum = term if accum is None else accum + term
    return accum


def gather_channels(latent):
    other = swap_halves(latent)
    half = lax.axis_index("zh")
    pair = jnp.where(half == 0, jnp.stack([latent, other]), jnp.stack([other, latent]))
    inner = lax.all_gather(pair, "inner", axis=0, tiled=False)
    frame_count, row_count, col_count, own_chan = latent.shape
    total = inner.shape[0] * HALVES * own_chan
    return jnp.transpose(inner, (2, 3, 4, 1, 0, 5)).reshape(frame_count, row_count, col_count, total)


def reduce_channels(partial, own_chan):
    inner_count = lax.axis_size("inner")
    cells = partial.shape[1]
    cur = partial.reshape(HALVES, inner_count, own_chan, cells).transpose(1, 0, 2, 3)
    idx = lax.axis_index("inner")
    step = inner_count // 2
    while step >= 1:
        size = cur.shape[0] // 2
        low, high = cur[:size], cur[size:]
        upper = (idx // step) % 2 == 1
        keep = jnp.where(upper, high, low)
        send = jnp.where(upper, low, high)
        cur = keep + lax.ppermute(send, "inner", [(i, i ^ step) for i in range(inner_count)])
        step //= 2
    sums = cur[0]
    half = lax.axis_index("zh")
    mine = jnp.where(half == 0, sums[0], sums[1])
    theirs = jnp.where(half == 0, sums[1], sums[0])
    return mine + swap_halves(theirs)


def local(latent, conv_one, bias_one, conv_two, bias_two):
    frame_count, row_count, col_count, own_chan = latent.shape
    gathered = gather_channels(latent)
    extended = halo_rows(gathered, 1)
    first = tap_sum(pad_sides(extended), conv_one, frame_count, row_count, col_count)
    hidden = jax.nn.relu(first + bias_one).astype(jnp.bfloat16)
    hidden = hidden.reshape(frame_count, row_count, col_count, own_chan)
    hidden_ext = halo_rows(hidden, 1)
    columns = jnp.concatenate(
        tap_windows(pad_sides(hidden_ext), frame_count, row_count, col_count), axis=1
    )
    flat_two = conv_two.reshape(27 * own_chan, conv_two.shape[2])
    partial = lax.dot_general(
        flat_two, columns, (((0,), (1,)), ((), ())), preferred_element_type=jnp.float32
    )
    mine = reduce_channels(partial, own_chan)
    second = mine.T.reshape(frame_count, row_count, col_count, own_chan)
    summed = latent.astype(jnp.float32) + second + bias_two
    return summed.astype(jnp.bfloat16)


def solution(mesh):
    space, chan = mesh.shape["space"], mesh.shape["chan"]
    split = Mesh(mesh.devices.reshape(space, HALVES, chan // HALVES), ("space",) + CHAN)
    in_specs = (
        P(None, "space", None, CHAN),
        P(None, None, CHAN),
        P(CHAN),
        P(None, CHAN, None),
        P(CHAN),
    )
    out_specs = P(None, "space", None, CHAN)
    return jax.shard_map(local, mesh=split, in_specs=in_specs, out_specs=out_specs, check_vma=False)
```

time: 315 us -> 187 us (0.59)
  waiting for transfers between devices: 176 us -> 66.1 us
  blocking collectives: 91.8 us -> 13.2 us
  starting transfers between devices: 12.5 us -> 77.1 us
  between operations: 13.7 us -> 0.47 us
  other arithmetic: 2.48 us -> 9.59 us
    unnamed x2 -> x0, waiting for transfers between devices: 134 us -> none
    all_gather x1, blocking collectives: 91.8 us -> 13.2 us  [gather_channels(): inner = lax.all_gather(pair, 'inner', axis=0, tiled=False)]
    ppermute x4 -> x9, starting transfers between devices: 12.5 us -> 77.1 us  [the longest x2 41.1 us: swap_halves(): return lax.ppermute(v, 'zh', [(0, 1), (1, 0)])]
    ppermute x4 -> x9, waiting for transfers between devices: 41.8 us -> 66.1 us  [the longest x2 39.6 us: halo_rows(): lax.ppermute(tail, 'space', [(i, (i + 1) % count) for i in range(ends)])]
    reshape x0 -> x3, local copies, waits for them, and re-layouts: none -> 5.49 us  [the longest x1 1.89 us: reduce_channels(): partial.reshape(HALVES, inner_count, own_chan, cells).transpose(1, 0, 2, 3)]
    unnamed x17 -> x12, local copies, waits for them, and re-layouts: 4.98 us -> 0.71 us
    select_n x0 -> x4, other arithmetic: none -> 3.58 us  [the longest x3 2.77 us: reduce_channels(): send = jnp.where(upper, low, high)]
  transfers between devices with their start and end apart: 5 -> 9, of which waited for: 4 -> 8; matrix products, arithmetic and copies ran while one was open for 0% -> 1% of each run, Pallas kernels for 0% -> 0%
where the time goes in v1:
time: 187 us; the launch traced here: 186 us
  starting transfers between devices  77.1 us (41%)
  waiting for transfers between devices  66.1 us (35%)
  blocking collectives  13.2 us (7%)
  local copies, waits for them, and re-layouts  10.8 us (6%)
  other arithmetic  9.59 us (5%)
  matrix products  8.9 us (5%)
    ppermute x2, starting transfers between devices, swap_halves(): return lax.ppermute(v, 'zh', [(0, 1), (1, 0)])  41.1 us
    ppermute x2, waiting for transfers between devices, halo_rows(): lax.ppermute(tail, 'space', [(i, (i + 1) % count) for i in range(ends)])  39.6 us
    ppermute x2, starting transfers between devices, halo_rows(): lax.ppermute(head, 'space', [((i + 1) % count, i) for i in range(ends)])  21.8 us
    ppermute x2, waiting for transfers between devices, swap_halves(): return lax.ppermute(v, 'zh', [(0, 1), (1, 0)])  14.1 us
    all_gather x1, blocking collectives, gather_channels(): inner = lax.all_gather(pair, 'inner', axis=0, tiled=False)  13.2 us
    ppermute x3, waiting for transfers between devices, reduce_channels(): lax.ppermute(send, 'inner', [(i, i ^ step) for i in range(inner_count)])  12 us
    ppermute x3, starting transfers between devices, reduce_channels(): lax.ppermute(send, 'inner', [(i, i ^ step) for i in range(inner_count)])  8.37 us
    dot_general x27, matrix products, tap_sum(): term = jnp.dot(flat, kernel[tap_index], preferred_element_type=jnp.float32)  6.53 us
  transfers between devices with their start and end apart: 9, of which 8 were waited for; matrix products, arithmetic and copies ran while one was open for 1% of the time, Pallas kernels for 0%

profile of v1, /device:TPU:24, one launch (start us, length us, event | category | flops | bytes accessed | tf_op | source)
XLA Modules:
  0.0 186.2 jit_solution(9994540108755686467)
XLA Ops:
  0.0 29.2 %collective-permute-start = (bf16[2,1,32,64]{3,2,0,1:T(8,128)(2,1)}, bf16[2,1,32,64]{3,2,0,1:T(8,128)(2,1)S(1)}, u32[]{:S(2)}, u32[]{:S(2)}) collective-permute-start(bf16[2,1,32,64]{3,2,0,1:T(8,128)(2,1)} %bitcast.225), channel_id=1, source_target_pairs={{0,8},{8,0},{1,9},{9,1},{2,10},{10,2},{3,11},{11,3},{4,12},{12,4},... | collective-permute-start | bytes 24584 | tf_op jit(solution)/shard_map/ppermute | solution.py:27
  29.2 1.9 %collective-permute-done = bf16[2,1,32,64]{3,2,0,1:T(8,128)(2,1)S(1)} collective-permute-done((bf16[2,1,32,64]{3,2,0,1:T(8,128)(2,1)}, bf16[2,1,32,64]{3,2,0,1:T(8,128)(2,1)S(1)}, u32[]{:S(2)}, u32[]{:S(2)}) %collective-permute-start) | collective-permute-done | bytes 8224 | tf_op jit(solution)/shard_map/ppermute | solution.py:27
  31.2 0.8 maximum_select_fusion
  32.0 13.2 %all_gather.4 = bf16[8,2,2,1,32,64]{5,4,3,2,1,0:T(8,128)(2,1)S(1)} all-gather(bf16[1,2,2,1,32,64]{5,4,3,2,1,0:T(8,128)(2,1)S(1)} %maximum_select_fusion), channel_id=1, replica_groups=mesh['space'=64,'zh'=2,'inner'=8] {'inner'}, dimensions={0}, use_global_device_ids=true | all-gather | bytes 147456 | tf_op jit(solution)/shard_map/all_gather | solution.py:60
  45.1 0.9 copy.17
  46.0 1.8 reshape.265
  47.8 19.9 %collective-permute-start.2 = (bf16[2,1,32,1024]{3,2,0,1:T(8,128)(2,1)}, bf16[2,1,32,1024]{3,2,0,1:T(8,128)(2,1)}, u32[]{:S(2)}, u32[]{:S(2)}) collective-permute-start(bf16[2,1,32,1024]{3,2,0,1:T(8,128)(2,1)} %reshape.265), channel_id=1, source_target_pairs={{16,0},{32,16},{48,32},{64,48},{80,64},{96,80},{112,96},{128,112},... | collective-permute-start | bytes 393224 | tf_op jit(solution)/shard_map/ppermute | solution.py:20
  67.7 1.9 %collective-permute-start.1 = (bf16[2,1,32,1024]{3,2,0,1:T(8,128)(2,1)}, bf16[2,1,32,1024]{3,2,0,1:T(8,128)(2,1)}, u32[]{:S(2)}, u32[]{:S(2)}) collective-permute-start(bf16[2,1,32,1024]{3,2,0,1:T(8,128)(2,1)} %reshape.265), channel_id=1, source_target_pairs={{0,16},{16,32},{32,48},{48,64},{64,80},{80,96},{96,112},{112,128},... | collective-permute-start | bytes 393224 | tf_op jit(solution)/shard_map/ppermute | solution.py:18
  69.6 1.8 reshape.279
  71.8 20.7 %collective-permute-done.1 = bf16[2,1,32,1024]{3,2,0,1:T(8,128)(2,1)} collective-permute-done((bf16[2,1,32,1024]{3,2,0,1:T(8,128)(2,1)}, bf16[2,1,32,1024]{3,2,0,1:T(8,128)(2,1)}, u32[]{:S(2)}, u32[]{:S(2)}) %collective-permute-start.1) | collective-permute-done | bytes 131104 | tf_op jit(solution)/shard_map/ppermute | solution.py:18
  92.6 1.2 select_maximum_fusion
  96.6 1.1 fusion.5
  98.4 1.1 fusion.4
  101.1 1.9 %collective-permute-start.4 = (bf16[2,1,32,64]{3,2,0,1:T(8,128)(2,1)S(1)}, bf16[2,1,32,64]{3,2,0,1:T(8,128)(2,1)}, u32[]{:S(2)}, u32[]{:S(2)}) collective-permute-start(bf16[2,1,32,64]{3,2,0,1:T(8,128)(2,1)S(1)} %bitcast.219), channel_id=1, source_target_pairs={{16,0},{32,16},{48,32},{64,48},{80,64},{96,80},{112,96},{128,112},... | collective-permute-start | bytes 24584 | tf_op jit(solution)/shard_map/ppermute | solution.py:20
  103.1 3.9 %collective-permute-start.3 = (bf16[2,1,32,64]{3,2,0,1:T(8,128)(2,1)S(1)}, bf16[2,1,32,64]{3,2,0,1:T(8,128)(2,1)}, u32[]{:S(2)}, u32[]{:S(2)}) collective-permute-start(bf16[2,1,32,64]{3,2,0,1:T(8,128)(2,1)S(1)} %bitcast.220), channel_id=1, source_target_pairs={{0,16},{16,32},{32,48},{48,64},{64,80},{80,96},{96,112},{112,128},... | collective-permute-start | bytes 24584 | tf_op jit(solution)/shard_map/ppermute | solution.py:18
  107.0 18.9 %collective-permute-done.3 = bf16[2,1,32,64]{3,2,0,1:T(8,128)(2,1)} collective-permute-done((bf16[2,1,32,64]{3,2,0,1:T(8,128)(2,1)S(1)}, bf16[2,1,32,64]{3,2,0,1:T(8,128)(2,1)}, u32[]{:S(2)}, u32[]{:S(2)}) %collective-permute-start.3) | collective-permute-done | bytes 8224 | tf_op jit(solution)/shard_map/ppermute | solution.py:18
  125.9 0.8 select_maximum_fusion.2
  128.1 1.8 concatenate.29
  129.9 2.4 %convolution_bitcast_fusion = f32[1024,64]{0,1:T(8,128)} fusion(bf16[64,1728]{1,0:T(8,128)(2,1)} %concatenate.29, bf16[1728,1024]{1,0:T(8,128)(2,1)S(1)} %bitcast.191), kind=kOutput, calls=%fused_computation.7 | convolution fusion | flops 226492416 | bytes 4022272 | tf_op jit(solution)/shard_map/dot_general | solution.py:99
  132.2 1.9 %reshape.321 = f32[2,8,64,64]{2,1,0,3:T(8,128)} reshape(f32[1024,64]{0,1:T(8,128)} %convolution_bitcast_fusion) | data formatting | bytes 524288 | tf_op jit(solution)/shard_map/reshape | solution.py:69
  134.1 2.0 %slice_select_fusion = f32[4,2,64,64]{2,0,1,3:T(4,128)} fusion(f32[8,2,64,64]{2,0,1,3:T(8,128)} %bitcast.192, pred[]{:T(512)S(6)} %eq.21), kind=kLoop, calls=%fused_computation.50 | loop fusion | flops 32768 | bytes 393217 | tf_op jit(solution)/shard_map/jit(_where)/select_n | solution.py:77
  136.1 3.4 %collective-permute-start.5 = (f32[4,2,64,64]{2,0,1,3:T(4,128)}, f32[4,2,64,64]{2,0,1,3:T(4,128)}, u32[]{:S(2)}, u32[]{:S(2)}) collective-permute-start(f32[4,2,64,64]{2,0,1,3:T(4,128)} %slice_select_fusion), channel_id=1, source_target_pairs={{0,4},{1,5},{2,6},{3,7},{4,0},{5,1},{6,2},{7,3},{8,12},{9,13},{10,... | collective-permute-start | bytes 393224 | tf_op jit(solution)/shard_map/ppermute | solution.py:78
  139.5 6.7 %collective-permute-done.5 = f32[4,2,64,64]{2,0,1,3:T(4,128)} collective-permute-done((f32[4,2,64,64]{2,0,1,3:T(4,128)}, f32[4,2,64,64]{2,0,1,3:T(4,128)}, u32[]{:S(2)}, u32[]{:S(2)}) %collective-permute-start.5) | collective-permute-done | bytes 131104 | tf_op jit(solution)/shard_map/ppermute | solution.py:78
  146.2 1.4 select_add_fusion
  149.0 3.1 %collective-permute-start.6 = (f32[2,2,64,64]{2,0,1,3:T(2,128)}, f32[2,2,64,64]{2,0,1,3:T(2,128)}, u32[]{:S(2)}, u32[]{:S(2)}) collective-permute-start(f32[2,2,64,64]{2,0,1,3:T(2,128)} %broadcast_select_fusion), channel_id=1, source_target_pairs={{0,2},{1,3},{2,0},{3,1},{4,6},{5,7},{6,4},{7,5},{8,10},{9,11},{10,... | collective-permute-start | bytes 196616 | tf_op jit(solution)/shard_map/ppermute | solution.py:78
  152.1 4.1 %collective-permute-done.6 = f32[2,2,64,64]{2,0,1,3:T(2,128)} collective-permute-done((f32[2,2,64,64]{2,0,1,3:T(2,128)}, f32[2,2,64,64]{2,0,1,3:T(2,128)}, u32[]{:S(2)}, u32[]{:S(2)}) %collective-permute-start.6) | collective-permute-done | bytes 65568 | tf_op jit(solution)/shard_map/ppermute | solution.py:78
  156.2 1.2 select_add_fusion.1
  157.5 1.9 %collective-permute-start.7 = (f32[1,2,64,64]{2,0,1,3:T(1,128)S(1)}, f32[1,2,64,64]{2,0,1,3:T(1,128)S(1)}, u32[]{:S(2)}, u32[]{:S(2)}) collective-permute-start(f32[1,2,64,64]{2,0,1,3:T(1,128)S(1)} %broadcast_select_fusion.1), channel_id=1, source_target_pairs={{0,1},{1,0},{2,3},{3,2},{4,5},{5,4},{6,7},{7,6},{8,9},{9,8},{10,11... | collective-permute-start | bytes 98312 | tf_op jit(solution)/shard_map/ppermute | solution.py:78
  159.4 1.2 collective-permute-done.7
  160.8 11.9 %collective-permute-start.8 = (f32[64,64]{0,1:T(8,128)S(1)}, f32[64,64]{0,1:T(8,128)S(1)}, u32[]{:S(2)}, u32[]{:S(2)}) collective-permute-start(f32[64,64]{0,1:T(8,128)S(1)} %bitcast.251), channel_id=1, source_target_pairs={{0,8},{8,0},{1,9},{9,1},{2,10},{10,2},{3,11},{11,3},{4,12},{12,4},... | collective-permute-start | bytes 49160 | tf_op jit(solution)/shard_map/ppermute | solution.py:27
  172.7 12.2 %collective-permute-done.8 = f32[64,64]{0,1:T(8,128)S(1)} collective-permute-done((f32[64,64]{0,1:T(8,128)S(1)}, f32[64,64]{0,1:T(8,128)S(1)}, u32[]{:S(2)}, u32[]{:S(2)}) %collective-permute-start.8) | collective-permute-done | bytes 16416 | tf_op jit(solution)/shard_map/ppermute | solution.py:27
  184.9 1.3 add_convert_fusion
  (48 shorter events, 8.4 us)
Async XLA Ops:
  0.0 129.9 %copy-start = (bf16[27,64,1024]{2,1,0:T(8,128)(2,1)S(1)}, bf16[27,64,1024]{2,1,0:T(8,128)(2,1)}, u32[]{:S(2)}) copy-start(bf16[27,64,1024]{2,1,0:T(8,128)(2,1)} %param.8) | copy-start | bytes 10616836
  0.0 31.1 %collective-permute-start = (bf16[2,1,32,64]{3,2,0,1:T(8,128)(2,1)}, bf16[2,1,32,64]{3,2,0,1:T(8,128)(2,1)S(1)}, u32[]{:S(2)}, u32[]{:S(2)}) collective-permute-start(bf16[2,1,32,64]{3,2,0,1:T(8,128)(2,1)} %bitcast.225), channel_id=1, source_target_pairs={{0,8},{8,0},{1,9},{9,1},{2,10},{10,2},{3,11},{11,3},{4,12},{12,4},... | collective-permute-start | bytes 24584 | tf_op jit(solution)/shard_map/ppermute | solution.py:27
  47.8 24.0 %collective-permute-start.2 = (bf16[2,1,32,1024]{3,2,0,1:T(8,128)(2,1)}, bf16[2,1,32,1024]{3,2,0,1:T(8,128)(2,1)}, u32[]{:S(2)}, u32[]{:S(2)}) collective-permute-start(bf16[2,1,32,1024]{3,2,0,1:T(8,128)(2,1)} %reshape.265), channel_id=1, source_target_pairs={{16,0},{32,16},{48,32},{64,48},{80,64},{96,80},{112,96},{128,112},... | collective-permute-start | bytes 393224 | tf_op jit(solution)/shard_map/ppermute | solution.py:20
  67.7 24.9 %collective-permute-start.1 = (bf16[2,1,32,1024]{3,2,0,1:T(8,128)(2,1)}, bf16[2,1,32,1024]{3,2,0,1:T(8,128)(2,1)}, u32[]{:S(2)}, u32[]{:S(2)}) collective-permute-start(bf16[2,1,32,1024]{3,2,0,1:T(8,128)(2,1)} %reshape.265), channel_id=1, source_target_pairs={{0,16},{16,32},{32,48},{48,64},{64,80},{80,96},{96,112},{112,128},... | collective-permute-start | bytes 393224 | tf_op jit(solution)/shard_map/ppermute | solution.py:18
  71.4 23.0 %copy-start.1 = (bf16[27,1024,64]{1,2,0:T(8,128)(2,1)S(1)}, bf16[27,1024,64]{1,2,0:T(8,128)(2,1)}, u32[]{:S(2)}) copy-start(bf16[27,1024,64]{1,2,0:T(8,128)(2,1)} %param.6) | copy-start | bytes 10616836
  93.9 4.0 %copy-start.3 = (bf16[64,1024]{1,0:T(8,128)(2,1)S(1)}, bf16[64,1024]{1,0:T(8,128)(2,1)}, u32[]{:S(2)}) copy-start(bf16[64,1024]{1,0:T(8,128)(2,1)} %reshape.279) | copy-start | bytes 393220
  95.3 5.7 %copy-start.5 = (f32[64]{0:T(128)S(1)}, f32[64]{0:T(128)}, u32[]{:S(2)}) copy-start(f32[64]{0:T(128)} %param.7) | copy-start | bytes 772
  101.1 5.9 %collective-permute-start.4 = (bf16[2,1,32,64]{3,2,0,1:T(8,128)(2,1)S(1)}, bf16[2,1,32,64]{3,2,0,1:T(8,128)(2,1)}, u32[]{:S(2)}, u32[]{:S(2)}) collective-permute-start(bf16[2,1,32,64]{3,2,0,1:T(8,128)(2,1)S(1)} %bitcast.219), channel_id=1, source_target_pairs={{16,0},{32,16},{48,32},{64,48},{80,64},{96,80},{112,96},{128,112},... | collective-permute-start | bytes 24584 | tf_op jit(solution)/shard_map/ppermute | solution.py:20
  103.1 22.9 %collective-permute-start.3 = (bf16[2,1,32,64]{3,2,0,1:T(8,128)(2,1)S(1)}, bf16[2,1,32,64]{3,2,0,1:T(8,128)(2,1)}, u32[]{:S(2)}, u32[]{:S(2)}) collective-permute-start(bf16[2,1,32,64]{3,2,0,1:T(8,128)(2,1)S(1)} %bitcast.220), channel_id=1, source_target_pairs={{0,16},{16,32},{32,48},{48,64},{64,80},{80,96},{96,112},{112,128},... | collective-permute-start | bytes 24584 | tf_op jit(solution)/shard_map/ppermute | solution.py:18
  129.9 55.1 %copy-start.4 = (bf16[2,1,32,64]{3,2,1,0:T(8,128)(2,1)S(1)}, bf16[2,1,32,64]{3,2,1,0:T(8,128)(2,1)}, u32[]{:S(2)}) copy-start(bf16[2,1,32,64]{3,2,1,0:T(8,128)(2,1)} %param.5) | copy-start | bytes 24580
  136.1 10.1 %collective-permute-start.5 = (f32[4,2,64,64]{2,0,1,3:T(4,128)}, f32[4,2,64,64]{2,0,1,3:T(4,128)}, u32[]{:S(2)}, u32[]{:S(2)}) collective-permute-start(f32[4,2,64,64]{2,0,1,3:T(4,128)} %slice_select_fusion), channel_id=1, source_target_pairs={{0,4},{1,5},{2,6},{3,7},{4,0},{5,1},{6,2},{7,3},{8,12},{9,13},{10,... | collective-permute-start | bytes 393224 | tf_op jit(solution)/shard_map/ppermute | solution.py:78
  147.6 0.7 copy-start.2
  149.0 7.2 %collective-permute-start.6 = (f32[2,2,64,64]{2,0,1,3:T(2,128)}, f32[2,2,64,64]{2,0,1,3:T(2,128)}, u32[]{:S(2)}, u32[]{:S(2)}) collective-permute-start(f32[2,2,64,64]{2,0,1,3:T(2,128)} %broadcast_select_fusion), channel_id=1, source_target_pairs={{0,2},{1,3},{2,0},{3,1},{4,6},{5,7},{6,4},{7,5},{8,10},{9,11},{10,... | collective-permute-start | bytes 196616 | tf_op jit(solution)/shard_map/ppermute | solution.py:78
  157.5 3.1 %collective-permute-start.7 = (f32[1,2,64,64]{2,0,1,3:T(1,128)S(1)}, f32[1,2,64,64]{2,0,1,3:T(1,128)S(1)}, u32[]{:S(2)}, u32[]{:S(2)}) collective-permute-start(f32[1,2,64,64]{2,0,1,3:T(1,128)S(1)} %broadcast_select_fusion.1), channel_id=1, source_target_pairs={{0,1},{1,0},{2,3},{3,2},{4,5},{5,4},{6,7},{7,6},{8,9},{9,8},{10,11... | collective-permute-start | bytes 98312 | tf_op jit(solution)/shard_map/ppermute | solution.py:78
  160.8 24.1 %collective-permute-start.8 = (f32[64,64]{0,1:T(8,128)S(1)}, f32[64,64]{0,1:T(8,128)S(1)}, u32[]{:S(2)}, u32[]{:S(2)}) collective-permute-start(f32[64,64]{0,1:T(8,128)S(1)} %bitcast.251), channel_id=1, source_target_pairs={{0,8},{8,0},{1,9},{9,1},{2,10},{10,2},{3,11},{11,3},{4,12},{12,4},... | collective-permute-start | bytes 49160 | tf_op jit(solution)/shard_map/ppermute | solution.py:27

commit v2 on v1

--- a/solution.py
+++ b/solution.py
@@ -6,21 +6,26 @@
 
 CHAN = ("zh", "inner")
 HALVES = 2
+RUN = 16
 
 
-def halo_rows(cells, dim):
-    count = lax.axis_size("space")
-    ends = count - 1
-    head = lax.slice_in_dim(cells, 0, 1, axis=dim)
-    tail = lax.slice_in_dim(cells, cells.shape[dim] - 1, cells.shape[dim], axis=dim)
-    return jnp.concatenate(
-        [
-            lax.ppermute(tail, "space", [(i, (i + 1) % count) for i in range(ends)]),
-            cells,
-            lax.ppermute(head, "space", [((i + 1) % count, i) for i in range(ends)]),
-        ],
-        axis=dim,
-    )
+def row_from(cells, shift):
+    rows = lax.axis_size("space")
+    pairs = []
+    for target in range(rows):
+        source = target + shift
+        if 0 <= source < rows:
+            cross = source // RUN != target // RUN
+            for half in range(HALVES):
+                other = (HALVES - 1 - half) if cross else half
+                pairs.append((source * HALVES + other, target * HALVES + half))
+    return lax.ppermute(cells, ("space", "zh"), pairs)
+
+
+def halo_rows(cells, width):
+    parts = [row_from(cells, -d) for d in range(width, 0, -1)]
+    parts += [cells] + [row_from(cells, d) for d in range(1, width + 1)]
+    return jnp.concatenate(parts, axis=1)
 
 
 def swap_halves(v):
@@ -57,7 +62,9 @@
     other = swap_halves(latent)
     half = lax.axis_index("zh")
     pair = jnp.where(half == 0, jnp.stack([latent, other]), jnp.stack([other, latent]))
-    inner = lax.all_gather(pair, "inner", axis=0, tiled=False)
+    inner_count = lax.axis_size("inner")
+    copies = jnp.broadcast_to(pair[None], (inner_count,) + pair.shape)
+    inner = lax.all_to_all(copies, "inner", 0, 0, tiled=True)
     frame_count, row_count, col_count, own_chan = latent.shape
     total = inner.shape[0] * HALVES * own_chan
     return jnp.transpose(inner, (2, 3, 4, 1, 0, 5)).reshape(frame_count, row_count, col_count, total)
@@ -66,18 +73,8 @@
 def reduce_channels(partial, own_chan):
     inner_count = lax.axis_size("inner")
     cells = partial.shape[1]
-    cur = partial.reshape(HALVES, inner_count, own_chan, cells).transpose(1, 0, 2, 3)
-    idx = lax.axis_index("inner")
-    step = inner_count // 2
-    while step >= 1:
-        size = cur.shape[0] // 2
-        low, high = cur[:size], cur[size:]
-        upper = (idx // step) % 2 == 1
-        keep = jnp.where(upper, high, low)
-        send = jnp.where(upper, low, high)
-        cur = keep + lax.ppermute(send, "inner", [(i, i ^ step) for i in range(inner_count)])
-        step //= 2
-    sums = cur[0]
+    blocks = partial.reshape(HALVES, inner_count, own_chan, cells).transpose(1, 0, 2, 3)
+    sums = lax.all_to_all(blocks, "inner", 0, 0, tiled=True).sum(0)
     half = lax.axis_index("zh")
     mine = jnp.where(half == 0, sums[0], sums[1])
     theirs = jnp.where(half == 0, sums[1], sums[0])
@@ -87,11 +84,13 @@
 def local(latent, conv_one, bias_one, conv_two, bias_two):
     frame_count, row_count, col_count, own_chan = latent.shape
     gathered = gather_channels(latent)
-    extended = halo_rows(gathered, 1)
-    first = tap_sum(pad_sides(extended), conv_one, frame_count, row_count, col_count)
+    extended = halo_rows(gathered, 2)
+    first = tap_sum(pad_sides(extended), conv_one, frame_count, row_count + 2, col_count)
     hidden = jax.nn.relu(first + bias_one).astype(jnp.bfloat16)
-    hidden = hidden.reshape(frame_count, row_count, col_count, own_chan)
-    hidden_ext = halo_rows(hidden, 1)
+    hidden = hidden.reshape(frame_count, row_count + 2, col_count, own_chan)
+    row = lax.axis_index("space") * row_count + jnp.arange(-1, row_count + 1)
+    inside = (row >= 0) & (row < lax.axis_size("space") * row_count)
+    hidden_ext = jnp.where(inside[None, :, None, None], hidden, jnp.zeros_like(hidden))
     columns = jnp.concatenate(
         tap_windows(pad_sides(hidden_ext), frame_count, row_count, col_count), axis=1
     )

time: 187 us -> 151 us (0.81)
  waiting for transfers between devices: 66.1 us -> 13.7 us
  local copies, waits for them, and re-layouts: 10.8 us -> 29.7 us
  starting transfers between devices: 77.1 us -> 66.2 us
  blocking collectives: 13.2 us -> 22 us
    ppermute x7 -> x4, waiting for transfers between devices: 52 us -> 3.52 us  [row_from(): return lax.ppermute(cells, ('space', 'zh'), pairs)]
    all_to_all x0 -> x2, blocking collectives: none -> 22 us  [the longest x1 11.5 us: reduce_channels(): sums = lax.all_to_all(blocks, 'inner', 0, 0, tiled=True).sum(0)]
    ppermute x7 -> x4, starting transfers between devices: 36 us -> 20.8 us  [row_from(): return lax.ppermute(cells, ('space', 'zh'), pairs)]
    all_gather x1 -> x0, blocking collectives: 13.2 us -> none  [gather_channels(): inner = lax.all_gather(pair, 'inner', axis=0, tiled=False)]
    unnamed x12 -> x19, local copies, waits for them, and re-layouts: 0.71 us -> 13.1 us
    ppermute x2, starting transfers between devices: 41.1 us -> 45.4 us  [swap_halves(): return lax.ppermute(v, 'zh', [(0, 1), (1, 0)])]
    ppermute x2, waiting for transfers between devices: 14.1 us -> 10.2 us  [swap_halves(): return lax.ppermute(v, 'zh', [(0, 1), (1, 0)])]
    all_to_all x0 -> x1, other arithmetic: none -> 2.92 us  [reduce_channels(): sums = lax.all_to_all(blocks, 'inner', 0, 0, tiled=True).sum(0)]
  transfers between devices with their start and end apart: 9 -> 6, of which waited for: 8 -> 3; matrix products, arithmetic and copies ran while one was open for 1% -> 1% of each run, Pallas kernels for 0% -> 0%
where the time goes in v2:
time: 151 us; the launch traced here: 150 us
  starting transfers between devices  66.2 us (44%)
  local copies, waits for them, and re-layouts  29.7 us (20%)
  blocking collectives  22 us (15%)
  waiting for transfers between devices  13.7 us (9%)
  matrix products  9.88 us (7%)
  other arithmetic  8.21 us (5%)
    ppermute x2, starting transfers between devices, swap_halves(): return lax.ppermute(v, 'zh', [(0, 1), (1, 0)])  45.4 us
    ppermute x4, starting transfers between devices, row_from(): return lax.ppermute(cells, ('space', 'zh'), pairs)  20.8 us
    unnamed x19, local copies, waits for them, and re-layouts  13.1 us
    all_to_all x1, blocking collectives, reduce_channels(): sums = lax.all_to_all(blocks, 'inner', 0, 0, tiled=True).sum(0)  11.5 us
    all_to_all x1, blocking collectives, gather_channels(): inner = lax.all_to_all(copies, 'inner', 0, 0, tiled=True)  10.5 us
    ppermute x2, waiting for transfers between devices, swap_halves(): return lax.ppermute(v, 'zh', [(0, 1), (1, 0)])  10.2 us
    dot_general x27, matrix products, tap_sum(): term = jnp.dot(flat, kernel[tap_index], preferred_element_type=jnp.float32)  7.51 us
    slice x28, local copies, waits for them, and re-layouts, tap_windows(): padded[depth_off:depth_off + frame_count, row_off:row_off + row_count, co...  4.75 us
  transfers between devices with their start and end apart: 6, of which 3 were waited for; matrix products, arithmetic and copies ran while one was open for 1% of the time, Pallas kernels for 0%

profile of v2, /device:TPU:24, one launch (start us, length us, event | category | flops | bytes accessed | tf_op | source)
XLA Modules:
  0.0 150.2 jit_solution(6807020223735101954)
XLA Ops:
  0.0 29.2 %collective-permute-start = (bf16[2,1,32,64]{3,2,1,0:T(8,128)(2,1)}, bf16[2,1,32,64]{3,2,1,0:T(8,128)(2,1)S(1)}, u32[]{:S(2)}, u32[]{:S(2)}) collective-permute-start(bf16[2,1,32,64]{3,2,1,0:T(8,128)(2,1)} %param.5), channel_id=1, source_target_pairs={{0,8},{8,0},{1,9},{9,1},{2,10},{10,2},{3,11},{11,3},{4,12},{12,4},... | collective-permute-start | bytes 24584 | tf_op jit(solution)/shard_map/ppermute | solution.py:32
  29.2 1.9 %collective-permute-done = bf16[2,1,32,64]{3,2,1,0:T(8,128)(2,1)S(1)} collective-permute-done((bf16[2,1,32,64]{3,2,1,0:T(8,128)(2,1)}, bf16[2,1,32,64]{3,2,1,0:T(8,128)(2,1)S(1)}, u32[]{:S(2)}, u32[]{:S(2)}) %collective-permute-start) | collective-permute-done | bytes 8224 | tf_op jit(solution)/shard_map/ppermute | solution.py:32
  32.0 0.9 broadcast_bitcast_fusion
  32.9 1.8 %reshape.304 = bf16[8,2,4096]{2,1,0:T(2,128)(2,1)} reshape(bf16[8,1,2,32,2,64]{5,4,3,2,1,0:T(2,128)(2,1)} %broadcast_bitcast_fusion) | data formatting | bytes 262144
  34.8 10.5 %all_to_all.10 = bf16[8,2,4096]{2,1,0:T(2,128)(2,1)} all-to-all(bf16[8,2,4096]{2,1,0:T(2,128)(2,1)} %reshape.304), channel_id=1, replica_groups=mesh['space'=64,'zh'=2,'inner'=8] {'inner'}, dimensions={0} | all-to-all | bytes 262144 | tf_op jit(solution)/shard_map/all_to_all | solution.py:67
  45.3 1.8 %reshape.305 = bf16[8,1,2,32,2,64]{5,4,3,2,1,0:T(2,128)(2,1)} reshape(bf16[8,2,4096]{2,1,0:T(2,128)(2,1)} %all_to_all.10) | data formatting | bytes 262144
  47.1 1.1 bitcast_bitcast_fusion
  48.2 1.0 copy.38
  49.3 1.8 %reshape.245 = bf16[2,1,32,1024]{3,2,0,1:T(8,128)(2,1)} reshape(bf16[2,1,32,2,8,64]{5,4,3,2,0,1:T(8,128)(2,1)} %copy.38) | data formatting | bytes 262144 | tf_op jit(solution)/shard_map/reshape | solution.py:70
  51.1 3.6 %collective-permute-start.1 = (bf16[2,1,32,1024]{3,2,0,1:T(8,128)(2,1)}, bf16[2,1,32,1024]{3,2,0,1:T(8,128)(2,1)}, u32[]{:S(2)}, u32[]{:S(2)}) collective-permute-start(bf16[2,1,32,1024]{3,2,0,1:T(8,128)(2,1)} %reshape.245), channel_id=1, source_target_pairs={{0,32},{8,40},{16,48},{24,56},{32,64},{40,72},{48,80},{56,88},{64,... | collective-permute-start | bytes 393224 | tf_op jit(solution)/shard_map/ppermute | solution.py:22
  54.7 2.9 %collective-permute-start.2 = (bf16[2,1,32,1024]{3,2,0,1:T(8,128)(2,1)}, bf16[2,1,32,1024]{3,2,0,1:T(8,128)(2,1)S(1)}, u32[]{:S(2)}, u32[]{:S(2)}) collective-permute-start(bf16[2,1,32,1024]{3,2,0,1:T(8,128)(2,1)} %reshape.245), channel_id=1, source_target_pairs={{0,16},{8,24},{16,32},{24,40},{32,48},{40,56},{48,64},{56,72},{64,... | collective-permute-start | bytes 393224 | tf_op jit(solution)/shard_map/ppermute | solution.py:22
  57.7 9.4 %collective-permute-start.3 = (bf16[2,1,32,1024]{3,2,0,1:T(8,128)(2,1)}, bf16[2,1,32,1024]{3,2,0,1:T(8,128)(2,1)S(1)}, u32[]{:S(2)}, u32[]{:S(2)}) collective-permute-start(bf16[2,1,32,1024]{3,2,0,1:T(8,128)(2,1)} %reshape.245), channel_id=1, source_target_pairs={{16,0},{24,8},{32,16},{40,24},{48,32},{56,40},{64,48},{72,56},{80,... | collective-permute-start | bytes 393224 | tf_op jit(solution)/shard_map/ppermute | solution.py:22
  67.1 4.8 %collective-permute-start.4 = (bf16[2,1,32,1024]{3,2,0,1:T(8,128)(2,1)}, bf16[2,1,32,1024]{3,2,0,1:T(8,128)(2,1)S(1)}, u32[]{:S(2)}, u32[]{:S(2)}) collective-permute-start(bf16[2,1,32,1024]{3,2,0,1:T(8,128)(2,1)} %reshape.245), channel_id=1, source_target_pairs={{32,0},{40,8},{48,16},{56,24},{64,32},{72,40},{80,48},{88,56},{96,... | collective-permute-start | bytes 393224 | tf_op jit(solution)/shard_map/ppermute | solution.py:22
  71.9 0.9 constant_dynamic-update-slice_fusion.4
  72.8 0.9 constant_dynamic-update-slice_fusion.2
  73.8 3.5 %collective-permute-done.4 = bf16[2,1,32,1024]{3,2,0,1:T(8,128)(2,1)S(1)} collective-permute-done((bf16[2,1,32,1024]{3,2,0,1:T(8,128)(2,1)}, bf16[2,1,32,1024]{3,2,0,1:T(8,128)(2,1)S(1)}, u32[]{:S(2)}, u32[]{:S(2)}) %collective-permute-start.4) | collective-permute-done | bytes 131104 | tf_op jit(solution)/shard_map/ppermute | solution.py:22
  77.3 2.5 %pad_slice_fusion = (bf16[2,3,32,1024]{3,2,0,1:T(8,128)(2,1)S(1)}, bf16[2,3,32,1024]{3,2,0,1:T(8,128)(2,1)S(1)}, bf16[2,3,32,1024]{3,2,0,1:T(8,128)(2,1)S(1)}, b...) fusion(bf16[2,5,32,1024]{3,2,0,1:T(8,128)(2,1)S(1)} %constant_d, ...), kind=kLoop, calls=%fused_computation | loop fusion | bytes 8126464 | tf_op jit(solution)/shard_map/slice | solution.py:44
  81.0 1.0 pad_maximum_fusion.2
  82.6 1.7 %copy-done.1 = bf16[27,1024,64]{1,2,0:T(8,128)(2,1)S(1)} copy-done((bf16[27,1024,64]{1,2,0:T(8,128)(2,1)S(1)}, bf16[27,1024,64]{1,2,0:T(8,128)(2,1)}, u32[]{:S(2)}) %copy-start.1) | copy-done | bytes 3538968
  91.8 1.5 copy.66
  95.6 1.8 %concatenate.31 = bf16[64,1728]{1,0:T(8,128)(2,1)} concatenate(bf16[64,64]{1,0:T(8,128)(2,1)} %bitcast.245, bf16[64,64]{1,0:T(8,128)(2,1)} %bitcast.247, bf16[64,64]{1,0:T(8,128)(2,1)} %bitcast.248, bf16[64,64]{1,0:T(8,128)(2,1)} %bitcast.249, bf16[64,64]{1,0:T(8,128)(2,1)} %bitcast.250, bf16[64,64]{1,0:T(8,128)(2,1)} %bitcast.251, bf16[64,64]{1,0:T(8,128)(2,1)} %bitcast.252, ...), dimensions={1} | concatenate | bytes 442368 | tf_op jit(solution)/shard_map/concatenate | solution.py:94
  97.4 2.4 %convolution_bitcast_fusion = f32[1024,64]{0,1:T(8,128)} fusion(bf16[64,1728]{1,0:T(8,128)(2,1)} %concatenate.31, bf16[1728,1024]{1,0:T(8,128)(2,1)S(1)} %bitcast.204), kind=kOutput, calls=%fused_computation.24 | convolution fusion | flops 226492416 | bytes 4022272 | tf_op jit(solution)/shard_map/dot_general | solution.py:98
  99.8 1.9 %reshape.302 = f32[2,8,64,64]{2,1,0,3:T(8,128)} reshape(f32[1024,64]{0,1:T(8,128)} %convolution_bitcast_fusion) | data formatting | bytes 524288 | tf_op jit(solution)/shard_map/reshape | solution.py:76
  101.7 2.1 %copy.79 = f32[2,8,64,64]{2,0,3,1:T(2,128)} copy(f32[2,8,64,64]{2,1,0,3:T(8,128)} %reshape.302) | data formatting | bytes 524288 | tf_op jit(solution)/shard_map/reshape | solution.py:76
  103.8 2.3 %reshape.306 = f32[8,1,8192]{2,1,0:T(1,128)} reshape(f32[8,64,2,64]{3,2,1,0:T(2,128)} %bitcast.205) | data formatting | bytes 524288
  106.1 11.5 %all_to_all.11 = f32[8,1,8192]{2,1,0:T(1,128)} all-to-all(f32[8,1,8192]{2,1,0:T(1,128)} %reshape.306), channel_id=1, replica_groups=mesh['space'=64,'zh'=2,'inner'=8] {'inner'}, dimensions={0} | all-to-all | bytes 524288 | tf_op jit(solution)/shard_map/all_to_all | solution.py:77
  118.1 2.9 %reduce = f32[8,8192]{1,0:T(8,128)} reduce(f32[8,1,8192]{2,1,0:T(1,128)} %all_to_all.11, f32[]{:T(128)} %broadcast.48), dimensions={1}, to_apply=%all_to_all.7.reduce_sub_computation | reduce | bytes 524292 | tf_op jit(solution)/shard_map/all_to_all | solution.py:77
  121.0 2.1 %reshape.307 = f32[8,64,2,64]{3,2,1,0:T(2,128)} reshape(f32[8,8192]{1,0:T(8,128)} %reduce) | data formatting | bytes 524288
  123.1 1.2 bitcast_reduce_fusion
  124.5 16.2 %collective-permute-start.5 = (f32[64,64]{0,1:T(8,128)S(1)}, f32[64,64]{0,1:T(8,128)S(1)}, u32[]{:S(2)}, u32[]{:S(2)}) collective-permute-start(f32[64,64]{0,1:T(8,128)S(1)} %bitcast.265), channel_id=1, source_target_pairs={{0,8},{8,0},{1,9},{9,1},{2,10},{10,2},{3,11},{11,3},{4,12},{12,4},... | collective-permute-start | bytes 49160 | tf_op jit(solution)/shard_map/ppermute | solution.py:32
  140.7 8.3 %collective-permute-done.5 = f32[64,64]{0,1:T(8,128)S(1)} collective-permute-done((f32[64,64]{0,1:T(8,128)S(1)}, f32[64,64]{0,1:T(8,128)S(1)}, u32[]{:S(2)}, u32[]{:S(2)}) %collective-permute-start.5) | collective-permute-done | bytes 16416 | tf_op jit(solution)/shard_map/ppermute | solution.py:32
  149.0 1.3 add_convert_fusion
  (79 shorter events, 12.8 us)
Async XLA Ops:
  0.0 97.4 %copy-start = (bf16[27,64,1024]{2,1,0:T(8,128)(2,1)S(1)}, bf16[27,64,1024]{2,1,0:T(8,128)(2,1)}, u32[]{:S(2)}) copy-start(bf16[27,64,1024]{2,1,0:T(8,128)(2,1)} %param.8) | copy-start | bytes 10616836
  0.0 31.1 %collective-permute-start = (bf16[2,1,32,64]{3,2,1,0:T(8,128)(2,1)}, bf16[2,1,32,64]{3,2,1,0:T(8,128)(2,1)S(1)}, u32[]{:S(2)}, u32[]{:S(2)}) collective-permute-start(bf16[2,1,32,64]{3,2,1,0:T(8,128)(2,1)} %param.5), channel_id=1, source_target_pairs={{0,8},{8,0},{1,9},{9,1},{2,10},{10,2},{3,11},{11,3},{4,12},{12,4},... | collective-permute-start | bytes 24584 | tf_op jit(solution)/shard_map/ppermute | solution.py:32
  51.1 20.8 %collective-permute-start.1 = (bf16[2,1,32,1024]{3,2,0,1:T(8,128)(2,1)}, bf16[2,1,32,1024]{3,2,0,1:T(8,128)(2,1)}, u32[]{:S(2)}, u32[]{:S(2)}) collective-permute-start(bf16[2,1,32,1024]{3,2,0,1:T(8,128)(2,1)} %reshape.245), channel_id=1, source_target_pairs={{0,32},{8,40},{16,48},{24,56},{32,64},{40,72},{48,80},{56,88},{64,... | collective-permute-start | bytes 393224 | tf_op jit(solution)/shard_map/ppermute | solution.py:22
  54.7 18.1 %collective-permute-start.2 = (bf16[2,1,32,1024]{3,2,0,1:T(8,128)(2,1)}, bf16[2,1,32,1024]{3,2,0,1:T(8,128)(2,1)S(1)}, u32[]{:S(2)}, u32[]{:S(2)}) collective-permute-start(bf16[2,1,32,1024]{3,2,0,1:T(8,128)(2,1)} %reshape.245), channel_id=1, source_target_pairs={{0,16},{8,24},{16,32},{24,40},{32,48},{40,56},{48,64},{56,72},{64,... | collective-permute-start | bytes 393224 | tf_op jit(solution)/shard_map/ppermute | solution.py:22
  57.7 16.1 %collective-permute-start.3 = (bf16[2,1,32,1024]{3,2,0,1:T(8,128)(2,1)}, bf16[2,1,32,1024]{3,2,0,1:T(8,128)(2,1)S(1)}, u32[]{:S(2)}, u32[]{:S(2)}) collective-permute-start(bf16[2,1,32,1024]{3,2,0,1:T(8,128)(2,1)} %reshape.245), channel_id=1, source_target_pairs={{16,0},{24,8},{32,16},{40,24},{48,32},{56,40},{64,48},{72,56},{80,... | collective-permute-start | bytes 393224 | tf_op jit(solution)/shard_map/ppermute | solution.py:22
  67.1 10.2 %collective-permute-start.4 = (bf16[2,1,32,1024]{3,2,0,1:T(8,128)(2,1)}, bf16[2,1,32,1024]{3,2,0,1:T(8,128)(2,1)S(1)}, u32[]{:S(2)}, u32[]{:S(2)}) collective-permute-start(bf16[2,1,32,1024]{3,2,0,1:T(8,128)(2,1)} %reshape.245), channel_id=1, source_target_pairs={{32,0},{40,8},{48,16},{56,24},{64,32},{72,40},{80,48},{88,56},{96,... | collective-permute-start | bytes 393224 | tf_op jit(solution)/shard_map/ppermute | solution.py:22
  80.1 0.9 copy-start.2
  82.3 2.0 %copy-start.1 = (bf16[27,1024,64]{1,2,0:T(8,128)(2,1)S(1)}, bf16[27,1024,64]{1,2,0:T(8,128)(2,1)}, u32[]{:S(2)}) copy-start(bf16[27,1024,64]{1,2,0:T(8,128)(2,1)} %param.6) | copy-start | bytes 10616836
  88.1 2.8 %copy-start.4 = (f32[64]{0:T(128)S(1)}, f32[64]{0:T(128)}, u32[]{:S(2)}) copy-start(f32[64]{0:T(128)} %param.7) | copy-start | bytes 772
  99.8 49.2 %copy-start.3 = (bf16[2,1,32,64]{3,2,1,0:T(8,128)(2,1)S(1)}, bf16[2,1,32,64]{3,2,1,0:T(8,128)(2,1)}, u32[]{:S(2)}) copy-start(bf16[2,1,32,64]{3,2,1,0:T(8,128)(2,1)} %param.5) | copy-start | bytes 24580
  124.5 24.5 %collective-permute-start.5 = (f32[64,64]{0,1:T(8,128)S(1)}, f32[64,64]{0,1:T(8,128)S(1)}, u32[]{:S(2)}, u32[]{:S(2)}) collective-permute-start(f32[64,64]{0,1:T(8,128)S(1)} %bitcast.265), channel_id=1, source_target_pairs={{0,8},{8,0},{1,9},{9,1},{2,10},{10,2},{3,11},{11,3},{4,12},{12,4},... | collective-permute-start | bytes 49160 | tf_op jit(solution)/shard_map/ppermute | solution.py:32

commit v3 on v2

--- a/solution.py
+++ b/solution.py
@@ -58,6 +58,19 @@
     return accum
 
 
+def conv3(padded, kernel):
+    taps = kernel.reshape(3, 3, 3, kernel.shape[1], kernel.shape[2])
+    out = lax.conv_general_dilated(
+        padded[None],
+        taps,
+        (1, 1, 1),
+        "VALID",
+        dimension_numbers=("NDHWC", "DHWIO", "NDHWC"),
+        preferred_element_type=jnp.float32,
+    )
+    return out[0]
+
+
 def gather_channels(latent):
     other = swap_halves(latent)
     half = lax.axis_index("zh")
@@ -85,19 +98,13 @@
     frame_count, row_count, col_count, own_chan = latent.shape
     gathered = gather_channels(latent)
     extended = halo_rows(gathered, 2)
-    first = tap_sum(pad_sides(extended), conv_one, frame_count, row_count + 2, col_count)
+    first = conv3(pad_sides(extended), conv_one)
     hidden = jax.nn.relu(first + bias_one).astype(jnp.bfloat16)
-    hidden = hidden.reshape(frame_count, row_count + 2, col_count, own_chan)
     row = lax.axis_index("space") * row_count + jnp.arange(-1, row_count + 1)
     inside = (row >= 0) & (row < lax.axis_size("space") * row_count)
     hidden_ext = jnp.where(inside[None, :, None, None], hidden, jnp.zeros_like(hidden))
-    columns = jnp.concatenate(
-        tap_windows(pad_sides(hidden_ext), frame_count, row_count, col_count), axis=1
-    )
-    flat_two = conv_two.reshape(27 * own_chan, conv_two.shape[2])
-    partial = lax.dot_general(
-        flat_two, columns, (((0,), (1,)), ((), ())), preferred_element_type=jnp.float32
-    )
+    partial = conv3(pad_sides(hidden_ext), conv_two)
+    partial = partial.reshape(frame_count * row_count * col_count, -1).T
     mine = reduce_channels(partial, own_chan)
     second = mine.T.reshape(frame_count, row_count, col_count, own_chan)
     summed = latent.astype(jnp.float32) + second + bias_two

time: 151 us -> 139 us (0.921)
  matrix products: 9.88 us -> 4.42 us
  local copies, waits for them, and re-layouts: 29.7 us -> 24.7 us
  other arithmetic: 8.21 us -> 6.42 us
    dot_general x28 -> x0, matrix products: 9.88 us -> none  [the longest x27 7.51 us: tap_sum(): term = jnp.dot(flat, kernel[tap_index], preferred_element_type=jnp.float32)]
    slice x28 -> x0, local copies, waits for them, and re-layouts: 4.75 us -> none  [tap_windows(): padded[depth_off:depth_off + frame_count, row_off:row_off + row_count, co...]
    conv_general_dilated x0 -> x2, matrix products: none -> 4.42 us  [conv3(): lax.conv_general_dilated(padded[None], taps, (1, 1, 1), 'VALID', dimensio...]
    concatenate x1 -> x0, local copies, waits for them, and re-layouts: 1.81 us -> none  [local(): jnp.concatenate(tap_windows(pad_sides(hidden_ext), frame_count, row_count...]
    conv_general_dilated x0 -> x8, local copies, waits for them, and re-layouts: none -> 1.79 us  [conv3(): lax.conv_general_dilated(padded[None], taps, (1, 1, 1), 'VALID', dimensio...]
    unnamed x19 -> x20, local copies, waits for them, and re-layouts: 13.1 us -> 13.3 us
where the time goes in v3:
time: 139 us; the launch traced here: 138 us
  starting transfers between devices  66.2 us (48%)
  local copies, waits for them, and re-layouts  24.7 us (18%)
  blocking collectives  22 us (16%)
  waiting for transfers between devices  13.7 us (10%)
  other arithmetic  6.42 us (5%)
  matrix products  4.42 us (3%)
    ppermute x2, starting transfers between devices, swap_halves(): return lax.ppermute(v, 'zh', [(0, 1), (1, 0)])  45.4 us
    ppermute x4, starting transfers between devices, row_from(): return lax.ppermute(cells, ('space', 'zh'), pairs)  20.8 us
    unnamed x20, local copies, waits for them, and re-layouts  13.3 us
    all_to_all x1, blocking collectives, reduce_channels(): sums = lax.all_to_all(blocks, 'inner', 0, 0, tiled=True).sum(0)  11.5 us
    all_to_all x1, blocking collectives, gather_channels(): inner = lax.all_to_all(copies, 'inner', 0, 0, tiled=True)  10.5 us
    ppermute x2, waiting for transfers between devices, swap_halves(): return lax.ppermute(v, 'zh', [(0, 1), (1, 0)])  10.2 us
    conv_general_dilated x2, matrix products, conv3(): lax.conv_general_dilated(padded[None], taps, (1, 1, 1), 'VALID', dimensio...  4.42 us
    reshape x2, local copies, waits for them, and re-layouts, reduce_channels(): partial.reshape(HALVES, inner_count, own_chan, cells).transpose(1, 0, 2, 3)  4 us
  transfers between devices with their start and end apart: 6, of which 3 were waited for; matrix products, arithmetic and copies ran while one was open for 1% of the time, Pallas kernels for 0%

profile of v3, /device:TPU:24, one launch (start us, length us, event | category | flops | bytes accessed | tf_op | source)
XLA Modules:
  0.0 137.8 jit_solution(3794800319665913664)
XLA Ops:
  0.0 29.2 %collective-permute-start = (bf16[2,1,32,64]{3,2,1,0:T(8,128)(2,1)}, bf16[2,1,32,64]{3,2,1,0:T(8,128)(2,1)S(1)}, u32[]{:S(2)}, u32[]{:S(2)}) collective-permute-start(bf16[2,1,32,64]{3,2,1,0:T(8,128)(2,1)} %param.5), channel_id=1, source_target_pairs={{0,8},{8,0},{1,9},{9,1},{2,10},{10,2},{3,11},{11,3},{4,12},{12,4},... | collective-permute-start | bytes 24584 | tf_op jit(solution)/shard_map/ppermute | solution.py:32
  29.2 1.9 %collective-permute-done = bf16[2,1,32,64]{3,2,1,0:T(8,128)(2,1)S(1)} collective-permute-done((bf16[2,1,32,64]{3,2,1,0:T(8,128)(2,1)}, bf16[2,1,32,64]{3,2,1,0:T(8,128)(2,1)S(1)}, u32[]{:S(2)}, u32[]{:S(2)}) %collective-permute-start) | collective-permute-done | bytes 8224 | tf_op jit(solution)/shard_map/ppermute | solution.py:32
  31.2 0.8 maximum_select_fusion
  32.0 0.9 broadcast_bitcast_fusion
  32.9 1.8 %reshape.116 = bf16[8,2,4096]{2,1,0:T(2,128)(2,1)} reshape(bf16[8,1,2,32,2,64]{5,4,3,2,1,0:T(2,128)(2,1)} %broadcast_bitcast_fusion) | data formatting | bytes 262144
  34.8 10.5 %all_to_all.10 = bf16[8,2,4096]{2,1,0:T(2,128)(2,1)} all-to-all(bf16[8,2,4096]{2,1,0:T(2,128)(2,1)} %reshape.116), channel_id=1, replica_groups=mesh['space'=64,'zh'=2,'inner'=8] {'inner'}, dimensions={0} | all-to-all | bytes 262144 | tf_op jit(solution)/shard_map/all_to_all | solution.py:80
  45.3 1.8 %reshape.117 = bf16[8,1,2,32,2,64]{5,4,3,2,1,0:T(2,128)(2,1)} reshape(bf16[8,2,4096]{2,1,0:T(2,128)(2,1)} %all_to_all.10) | data formatting | bytes 262144
  47.1 1.1 bitcast_bitcast_fusion
  48.2 1.0 copy.24
  49.2 1.8 %reshape.83 = bf16[2,1,32,1024]{3,2,0,1:T(8,128)(2,1)} reshape(bf16[2,1,32,2,8,64]{5,4,3,2,0,1:T(8,128)(2,1)} %copy.24) | data formatting | bytes 262144 | tf_op jit(solution)/shard_map/reshape | solution.py:83
  51.0 3.6 %collective-permute-start.1 = (bf16[2,1,32,1024]{3,2,0,1:T(8,128)(2,1)}, bf16[2,1,32,1024]{3,2,0,1:T(8,128)(2,1)}, u32[]{:S(2)}, u32[]{:S(2)}) collective-permute-start(bf16[2,1,32,1024]{3,2,0,1:T(8,128)(2,1)} %reshape.83), channel_id=1, source_target_pairs={{0,32},{8,40},{16,48},{24,56},{32,64},{40,72},{48,80},{56,88},{64,... | collective-permute-start | bytes 393224 | tf_op jit(solution)/shard_map/ppermute | solution.py:22
  54.7 2.9 %collective-permute-start.2 = (bf16[2,1,32,1024]{3,2,0,1:T(8,128)(2,1)}, bf16[2,1,32,1024]{3,2,0,1:T(8,128)(2,1)S(1)}, u32[]{:S(2)}, u32[]{:S(2)}) collective-permute-start(bf16[2,1,32,1024]{3,2,0,1:T(8,128)(2,1)} %reshape.83), channel_id=1, source_target_pairs={{0,16},{8,24},{16,32},{24,40},{32,48},{40,56},{48,64},{56,72},{64,... | collective-permute-start | bytes 393224 | tf_op jit(solution)/shard_map/ppermute | solution.py:22
  57.7 9.4 %collective-permute-start.3 = (bf16[2,1,32,1024]{3,2,0,1:T(8,128)(2,1)}, bf16[2,1,32,1024]{3,2,0,1:T(8,128)(2,1)S(1)}, u32[]{:S(2)}, u32[]{:S(2)}) collective-permute-start(bf16[2,1,32,1024]{3,2,0,1:T(8,128)(2,1)} %reshape.83), channel_id=1, source_target_pairs={{16,0},{24,8},{32,16},{40,24},{48,32},{56,40},{64,48},{72,56},{80,... | collective-permute-start | bytes 393224 | tf_op jit(solution)/shard_map/ppermute | solution.py:22
  67.0 4.8 %collective-permute-start.4 = (bf16[2,1,32,1024]{3,2,0,1:T(8,128)(2,1)}, bf16[2,1,32,1024]{3,2,0,1:T(8,128)(2,1)S(1)}, u32[]{:S(2)}, u32[]{:S(2)}) collective-permute-start(bf16[2,1,32,1024]{3,2,0,1:T(8,128)(2,1)} %reshape.83), channel_id=1, source_target_pairs={{32,0},{40,8},{48,16},{56,24},{64,32},{72,40},{80,48},{88,56},{96,... | collective-permute-start | bytes 393224 | tf_op jit(solution)/shard_map/ppermute | solution.py:22
  71.9 0.9 constant_dynamic-update-slice_fusion.4
  72.8 0.9 constant_dynamic-update-slice_fusion.2
  73.8 3.5 %collective-permute-done.4 = bf16[2,1,32,1024]{3,2,0,1:T(8,128)(2,1)S(1)} collective-permute-done((bf16[2,1,32,1024]{3,2,0,1:T(8,128)(2,1)}, bf16[2,1,32,1024]{3,2,0,1:T(8,128)(2,1)S(1)}, u32[]{:S(2)}, u32[]{:S(2)}) %collective-permute-start.4) | collective-permute-done | bytes 131104 | tf_op jit(solution)/shard_map/ppermute | solution.py:22
  77.6 1.1 copy.42
  80.0 1.3 copy-done.3
  81.3 3.7 %fusion.9 = f32[2,3,8,5,64]{4,2,3,1,0:T(8,128)S(1)} fusion(bf16[3,3,3,1024,64]{3,4,2,1,0:T(8,128)(2,1)S(1)} %bitcast.82, bf16[4,5,1,7,2,1024]{5,3,4,1,0,2:T(8,128)(2,1)S(1)} %slice.14, bf16[4,5,1,8,5,1024]{5,3,4,1,0,2:T(8,128)(2,1)S(1)} %copy.27, pred[8,5]{0,1:T(8,128)(4,1)S(1)} %copy-done.4), kind=kOutput, calls=%fused_computation.11 | convolution fusion | flops 856243200 | bytes 5812264 | tf_op jit(solution)/shard_map/conv_general_dilated | solution.py:63
  85.4 0.8 convolution_select_fusion
  86.5 0.8 copy.32
  87.3 1.9 %reshape.86 = f32[2,8,64,64]{2,1,0,3:T(8,128)} reshape(f32[1024,64]{0,1:T(8,128)} %bitcast.73) | data formatting | bytes 524288 | tf_op jit(solution)/shard_map/reshape | solution.py:89
  89.2 2.1 %copy.46 = f32[2,8,64,64]{2,0,3,1:T(2,128)} copy(f32[2,8,64,64]{2,1,0,3:T(8,128)} %reshape.86) | data formatting | bytes 524288 | tf_op jit(solution)/shard_map/reshape | solution.py:89
  91.3 2.3 %reshape.118 = f32[8,1,8192]{2,1,0:T(1,128)} reshape(f32[8,64,2,64]{3,2,1,0:T(2,128)} %bitcast.71) | data formatting | bytes 524288
  93.6 11.5 %all_to_all.11 = f32[8,1,8192]{2,1,0:T(1,128)} all-to-all(f32[8,1,8192]{2,1,0:T(1,128)} %reshape.118), channel_id=1, replica_groups=mesh['space'=64,'zh'=2,'inner'=8] {'inner'}, dimensions={0} | all-to-all | bytes 524288 | tf_op jit(solution)/shard_map/all_to_all | solution.py:90
  105.6 2.9 %reduce = f32[8,8192]{1,0:T(8,128)} reduce(f32[8,1,8192]{2,1,0:T(1,128)} %all_to_all.11, f32[]{:T(128)} %broadcast.80), dimensions={1}, to_apply=%all_to_all.7.reduce_sub_computation | reduce | bytes 524292 | tf_op jit(solution)/shard_map/all_to_all | solution.py:90
  108.5 2.1 %reshape.119 = f32[8,64,2,64]{3,2,1,0:T(2,128)} reshape(f32[8,8192]{1,0:T(8,128)} %reduce) | data formatting | bytes 524288
  110.7 1.2 bitcast_reduce_fusion
  112.0 16.2 %collective-permute-start.5 = (f32[64,64]{0,1:T(8,128)S(1)}, f32[64,64]{0,1:T(8,128)S(1)}, u32[]{:S(2)}, u32[]{:S(2)}) collective-permute-start(f32[64,64]{0,1:T(8,128)S(1)} %bitcast.80), channel_id=1, source_target_pairs={{0,8},{8,0},{1,9},{9,1},{2,10},{10,2},{3,11},{11,3},{4,12},{12,4},... | collective-permute-start | bytes 49160 | tf_op jit(solution)/shard_map/ppermute | solution.py:32
  128.2 8.3 %collective-permute-done.5 = f32[64,64]{0,1:T(8,128)S(1)} collective-permute-done((f32[64,64]{0,1:T(8,128)S(1)}, f32[64,64]{0,1:T(8,128)S(1)}, u32[]{:S(2)}, u32[]{:S(2)}) %collective-permute-start.5) | collective-permute-done | bytes 16416 | tf_op jit(solution)/shard_map/ppermute | solution.py:32
  136.5 1.3 add_convert_fusion
  (32 shorter events, 2.9 us)
Async XLA Ops:
  0.0 85.4 %copy-start = (bf16[27,64,1024]{2,1,0:T(8,128)(2,1)S(1)}, bf16[27,64,1024]{2,1,0:T(8,128)(2,1)}, u32[]{:S(2)}) copy-start(bf16[27,64,1024]{2,1,0:T(8,128)(2,1)} %param.8) | copy-start | bytes 10616836
  0.0 31.1 %collective-permute-start = (bf16[2,1,32,64]{3,2,1,0:T(8,128)(2,1)}, bf16[2,1,32,64]{3,2,1,0:T(8,128)(2,1)S(1)}, u32[]{:S(2)}, u32[]{:S(2)}) collective-permute-start(bf16[2,1,32,64]{3,2,1,0:T(8,128)(2,1)} %param.5), channel_id=1, source_target_pairs={{0,8},{8,0},{1,9},{9,1},{2,10},{10,2},{3,11},{11,3},{4,12},{12,4},... | collective-permute-start | bytes 24584 | tf_op jit(solution)/shard_map/ppermute | solution.py:32
  51.0 20.8 %collective-permute-start.1 = (bf16[2,1,32,1024]{3,2,0,1:T(8,128)(2,1)}, bf16[2,1,32,1024]{3,2,0,1:T(8,128)(2,1)}, u32[]{:S(2)}, u32[]{:S(2)}) collective-permute-start(bf16[2,1,32,1024]{3,2,0,1:T(8,128)(2,1)} %reshape.83), channel_id=1, source_target_pairs={{0,32},{8,40},{16,48},{24,56},{32,64},{40,72},{48,80},{56,88},{64,... | collective-permute-start | bytes 393224 | tf_op jit(solution)/shard_map/ppermute | solution.py:22
  54.7 18.1 %collective-permute-start.2 = (bf16[2,1,32,1024]{3,2,0,1:T(8,128)(2,1)}, bf16[2,1,32,1024]{3,2,0,1:T(8,128)(2,1)S(1)}, u32[]{:S(2)}, u32[]{:S(2)}) collective-permute-start(bf16[2,1,32,1024]{3,2,0,1:T(8,128)(2,1)} %reshape.83), channel_id=1, source_target_pairs={{0,16},{8,24},{16,32},{24,40},{32,48},{40,56},{48,64},{56,72},{64,... | collective-permute-start | bytes 393224 | tf_op jit(solution)/shard_map/ppermute | solution.py:22
  57.7 16.1 %collective-permute-start.3 = (bf16[2,1,32,1024]{3,2,0,1:T(8,128)(2,1)}, bf16[2,1,32,1024]{3,2,0,1:T(8,128)(2,1)S(1)}, u32[]{:S(2)}, u32[]{:S(2)}) collective-permute-start(bf16[2,1,32,1024]{3,2,0,1:T(8,128)(2,1)} %reshape.83), channel_id=1, source_target_pairs={{16,0},{24,8},{32,16},{40,24},{48,32},{56,40},{64,48},{72,56},{80,... | collective-permute-start | bytes 393224 | tf_op jit(solution)/shard_map/ppermute | solution.py:22
  67.0 10.2 %collective-permute-start.4 = (bf16[2,1,32,1024]{3,2,0,1:T(8,128)(2,1)}, bf16[2,1,32,1024]{3,2,0,1:T(8,128)(2,1)S(1)}, u32[]{:S(2)}, u32[]{:S(2)}) collective-permute-start(bf16[2,1,32,1024]{3,2,0,1:T(8,128)(2,1)} %reshape.83), channel_id=1, source_target_pairs={{32,0},{40,8},{48,16},{56,24},{64,32},{72,40},{80,48},{88,56},{96,... | collective-permute-start | bytes 393224 | tf_op jit(solution)/shard_map/ppermute | solution.py:22
  79.3 2.0 %copy-start.3 = (bf16[27,1024,64]{1,2,0:T(8,128)(2,1)S(1)}, bf16[27,1024,64]{1,2,0:T(8,128)(2,1)}, u32[]{:S(2)}) copy-start(bf16[27,1024,64]{1,2,0:T(8,128)(2,1)} %param.6) | copy-start | bytes 10616836
  79.4 2.0 %copy-start.4 = (pred[8,5]{0,1:T(8,128)(4,1)S(1)}, pred[8,5]{0,1:T(8,128)(4,1)}, u32[]{:S(2)}) copy-start(pred[8,5]{0,1:T(8,128)(4,1)} %constant.39) | copy-start | bytes 124
  81.3 3.7 %copy-start.2 = (f32[64]{0:T(128)S(1)}, f32[64]{0:T(128)}, u32[]{:S(2)}) copy-start(f32[64]{0:T(128)} %param.7) | copy-start | bytes 772
  89.2 47.3 %copy-start.1 = (bf16[2,1,32,64]{3,2,1,0:T(8,128)(2,1)S(1)}, bf16[2,1,32,64]{3,2,1,0:T(8,128)(2,1)}, u32[]{:S(2)}) copy-start(bf16[2,1,32,64]{3,2,1,0:T(8,128)(2,1)} %param.5) | copy-start | bytes 24580
  112.0 24.5 %collective-permute-start.5 = (f32[64,64]{0,1:T(8,128)S(1)}, f32[64,64]{0,1:T(8,128)S(1)}, u32[]{:S(2)}, u32[]{:S(2)}) collective-permute-start(f32[64,64]{0,1:T(8,128)S(1)} %bitcast.80), channel_id=1, source_target_pairs={{0,8},{8,0},{1,9},{9,1},{2,10},{10,2},{3,11},{11,3},{4,12},{12,4},... | collective-permute-start | bytes 49160 | tf_op jit(solution)/shard_map/ppermute | solution.py:32

commit v4 on v3

--- a/solution.py
+++ b/solution.py
@@ -74,23 +74,20 @@
 def gather_channels(latent):
     other = swap_halves(latent)
     half = lax.axis_index("zh")
-    pair = jnp.where(half == 0, jnp.stack([latent, other]), jnp.stack([other, latent]))
+    pair = jnp.where(half == 0, jnp.stack([latent, other], 3), jnp.stack([other, latent], 3))
     inner_count = lax.axis_size("inner")
-    copies = jnp.broadcast_to(pair[None], (inner_count,) + pair.shape)
-    inner = lax.all_to_all(copies, "inner", 0, 0, tiled=True)
-    frame_count, row_count, col_count, own_chan = latent.shape
-    total = inner.shape[0] * HALVES * own_chan
-    return jnp.transpose(inner, (2, 3, 4, 1, 0, 5)).reshape(frame_count, row_count, col_count, total)
+    copies = jnp.broadcast_to(pair[:, :, :, :, None], pair.shape[:4] + (inner_count,) + pair.shape[4:])
+    inner = lax.all_to_all(copies, "inner", 4, 4, tiled=True)
+    return inner.reshape(inner.shape[:3] + (-1,))
 
 
 def reduce_channels(partial, own_chan):
     inner_count = lax.axis_size("inner")
-    cells = partial.shape[1]
-    blocks = partial.reshape(HALVES, inner_count, own_chan, cells).transpose(1, 0, 2, 3)
-    sums = lax.all_to_all(blocks, "inner", 0, 0, tiled=True).sum(0)
+    blocks = partial.reshape(partial.shape[0], HALVES, inner_count, own_chan)
+    sums = lax.all_to_all(blocks, "inner", 2, 2, tiled=True).sum(2)
     half = lax.axis_index("zh")
-    mine = jnp.where(half == 0, sums[0], sums[1])
-    theirs = jnp.where(half == 0, sums[1], sums[0])
+    mine = jnp.where(half == 0, sums[:, 0], sums[:, 1])
+    theirs = jnp.where(half == 0, sums[:, 1], sums[:, 0])
     return mine + swap_halves(theirs)
 
 
@@ -104,9 +101,9 @@
     inside = (row >= 0) & (row < lax.axis_size("space") * row_count)
     hidden_ext = jnp.where(inside[None, :, None, None], hidden, jnp.zeros_like(hidden))
     partial = conv3(pad_sides(hidden_ext), conv_two)
-    partial = partial.reshape(frame_count * row_count * col_count, -1).T
+    partial = partial.reshape(frame_count * row_count * col_count, -1)
     mine = reduce_channels(partial, own_chan)
-    second = mine.T.reshape(frame_count, row_count, col_count, own_chan)
+    second = mine.reshape(frame_count, row_count, col_count, own_chan)
     summed = latent.astype(jnp.float32) + second + bias_two
     return summed.astype(jnp.bfloat16)
 

time: 139 us -> 138 us (level)
    reshape x3 -> x1, local copies, waits for them, and re-layouts: 5.8 us -> 1.8 us  [gather_channels(): return inner.reshape(inner.shape[:3] + (-1,))]
    another operation x0 -> x2, local copies, waits for them, and re-layouts: none -> 4 us  [reduce_channels(): blocks = partial.reshape(partial.shape[0], HALVES, inner_count, own_chan)]
    transpose x2 -> x0, local copies, waits for them, and re-layouts: 2.15 us -> none  [gather_channels(): jnp.transpose(inner, (2, 3, 4, 1, 0, 5))]
    all_to_all x1 -> x2, local copies, waits for them, and re-layouts: 0.51 us -> 2.47 us  [the longest x1 1.96 us: gather_channels(): inner = lax.all_to_all(copies, 'inner', 4, 4, tiled=True)]
where the time goes in v4:
time: 138 us; the launch traced here: 137 us
  starting transfers between devices  66.2 us (48%)
  local copies, waits for them, and re-layouts  24.4 us (18%)
  blocking collectives  22 us (16%)
  waiting for transfers between devices  13.7 us (10%)
  other arithmetic  6.42 us (5%)
  matrix products  4.43 us (3%)
    ppermute x2, starting transfers between devices, swap_halves(): return lax.ppermute(v, 'zh', [(0, 1), (1, 0)])  45.4 us
    ppermute x4, starting transfers between devices, row_from(): return lax.ppermute(cells, ('space', 'zh'), pairs)  20.8 us
    unnamed x20, local copies, waits for them, and re-layouts  13.2 us
    all_to_all x1, blocking collectives, reduce_channels(): sums = lax.all_to_all(blocks, 'inner', 2, 2, tiled=True).sum(2)  11.5 us
    all_to_all x1, blocking collectives, gather_channels(): inner = lax.all_to_all(copies, 'inner', 4, 4, tiled=True)  10.5 us
    ppermute x2, waiting for transfers between devices, swap_halves(): return lax.ppermute(v, 'zh', [(0, 1), (1, 0)])  10.2 us
    conv_general_dilated x2, matrix products, conv3(): lax.conv_general_dilated(padded[None], taps, (1, 1, 1), 'VALID', dimensio...  4.43 us
    another operation x2, local copies, waits for them, and re-layouts, reduce_channels(): blocks = partial.reshape(partial.shape[0], HALVES, inner_count, own_chan)  4 us
  transfers between devices with their start and end apart: 6, of which 3 were waited for; matrix products, arithmetic and copies ran while one was open for 1% of the time, Pallas kernels for 0%

profile of v4, /device:TPU:24, one launch (start us, length us, event | category | flops | bytes accessed | tf_op | source)
XLA Modules:
  0.0 137.5 jit_solution(1564298965300642088)
XLA Ops:
  0.0 29.2 %collective-permute-start = (bf16[2,1,32,64]{3,2,1,0:T(8,128)(2,1)}, bf16[2,1,32,64]{3,2,1,0:T(8,128)(2,1)S(1)}, u32[]{:S(2)}, u32[]{:S(2)}) collective-permute-start(bf16[2,1,32,64]{3,2,1,0:T(8,128)(2,1)} %param.5), channel_id=1, source_target_pairs={{0,8},{8,0},{1,9},{9,1},{2,10},{10,2},{3,11},{11,3},{4,12},{12,4},... | collective-permute-start | bytes 24584 | tf_op jit(solution)/shard_map/ppermute | solution.py:32
  29.2 1.9 %collective-permute-done = bf16[2,1,32,64]{3,2,1,0:T(8,128)(2,1)S(1)} collective-permute-done((bf16[2,1,32,64]{3,2,1,0:T(8,128)(2,1)}, bf16[2,1,32,64]{3,2,1,0:T(8,128)(2,1)S(1)}, u32[]{:S(2)}, u32[]{:S(2)}) %collective-permute-start) | collective-permute-done | bytes 8224 | tf_op jit(solution)/shard_map/ppermute | solution.py:32
  31.2 0.8 maximum_select_fusion
  32.0 0.8 broadcast_bitcast_fusion
  32.8 1.8 %reshape.112 = bf16[8,2,4096]{2,1,0:T(2,128)(2,1)} reshape(bf16[8,1,32,2,2,64]{5,4,3,2,1,0:T(2,128)(2,1)} %broadcast_bitcast_fusion) | data formatting | bytes 262144
  34.7 10.5 %all_to_all.10 = bf16[8,2,4096]{2,1,0:T(2,128)(2,1)} all-to-all(bf16[8,2,4096]{2,1,0:T(2,128)(2,1)} %reshape.112), channel_id=1, replica_groups=mesh['space'=64,'zh'=2,'inner'=8] {'inner'}, dimensions={0} | all-to-all | bytes 262144 | tf_op jit(solution)/shard_map/all_to_all | solution.py:80
  45.2 1.8 %reshape.113 = bf16[8,1,32,2,2,64]{5,4,3,2,1,0:T(2,128)(2,1)} reshape(bf16[8,2,4096]{2,1,0:T(2,128)(2,1)} %all_to_all.10) | data formatting | bytes 262144
  47.0 2.0 %copy.38 = bf16[2,1,32,2,8,64]{5,4,3,2,0,1:T(8,128)(2,1)} copy(bf16[2,1,32,2,8,64]{5,3,0,2,1,4:T(2,128)(2,1)} %bitcast.62) | data formatting | bytes 262144 | tf_op jit(solution)/shard_map/all_to_all | solution.py:80
  49.0 1.8 %reshape.80 = bf16[2,1,32,1024]{3,2,0,1:T(8,128)(2,1)} reshape(bf16[2,1,32,2,8,64]{5,4,3,2,0,1:T(8,128)(2,1)} %copy.38) | data formatting | bytes 262144 | tf_op jit(solution)/shard_map/reshape | solution.py:81
  50.8 3.6 %collective-permute-start.1 = (bf16[2,1,32,1024]{3,2,0,1:T(8,128)(2,1)}, bf16[2,1,32,1024]{3,2,0,1:T(8,128)(2,1)}, u32[]{:S(2)}, u32[]{:S(2)}) collective-permute-start(bf16[2,1,32,1024]{3,2,0,1:T(8,128)(2,1)} %reshape.80), channel_id=1, source_target_pairs={{0,32},{8,40},{16,48},{24,56},{32,64},{40,72},{48,80},{56,88},{64,... | collective-permute-start | bytes 393224 | tf_op jit(solution)/shard_map/ppermute | solution.py:22
  54.4 2.9 %collective-permute-start.2 = (bf16[2,1,32,1024]{3,2,0,1:T(8,128)(2,1)}, bf16[2,1,32,1024]{3,2,0,1:T(8,128)(2,1)S(1)}, u32[]{:S(2)}, u32[]{:S(2)}) collective-permute-start(bf16[2,1,32,1024]{3,2,0,1:T(8,128)(2,1)} %reshape.80), channel_id=1, source_target_pairs={{0,16},{8,24},{16,32},{24,40},{32,48},{40,56},{48,64},{56,72},{64,... | collective-permute-start | bytes 393224 | tf_op jit(solution)/shard_map/ppermute | solution.py:22
  57.4 9.4 %collective-permute-start.3 = (bf16[2,1,32,1024]{3,2,0,1:T(8,128)(2,1)}, bf16[2,1,32,1024]{3,2,0,1:T(8,128)(2,1)S(1)}, u32[]{:S(2)}, u32[]{:S(2)}) collective-permute-start(bf16[2,1,32,1024]{3,2,0,1:T(8,128)(2,1)} %reshape.80), channel_id=1, source_target_pairs={{16,0},{24,8},{32,16},{40,24},{48,32},{56,40},{64,48},{72,56},{80,... | collective-permute-start | bytes 393224 | tf_op jit(solution)/shard_map/ppermute | solution.py:22
  66.8 4.8 %collective-permute-start.4 = (bf16[2,1,32,1024]{3,2,0,1:T(8,128)(2,1)}, bf16[2,1,32,1024]{3,2,0,1:T(8,128)(2,1)S(1)}, u32[]{:S(2)}, u32[]{:S(2)}) collective-permute-start(bf16[2,1,32,1024]{3,2,0,1:T(8,128)(2,1)} %reshape.80), channel_id=1, source_target_pairs={{32,0},{40,8},{48,16},{56,24},{64,32},{72,40},{80,48},{88,56},{96,... | collective-permute-start | bytes 393224 | tf_op jit(solution)/shard_map/ppermute | solution.py:22
  71.6 0.9 constant_dynamic-update-slice_fusion.4
  72.6 0.9 constant_dynamic-update-slice_fusion.2
  73.5 3.5 %collective-permute-done.4 = bf16[2,1,32,1024]{3,2,0,1:T(8,128)(2,1)S(1)} collective-permute-done((bf16[2,1,32,1024]{3,2,0,1:T(8,128)(2,1)}, bf16[2,1,32,1024]{3,2,0,1:T(8,128)(2,1)S(1)}, u32[]{:S(2)}, u32[]{:S(2)}) %collective-permute-start.4) | collective-permute-done | bytes 131104 | tf_op jit(solution)/shard_map/ppermute | solution.py:22
  77.3 1.1 copy.56
  78.4 0.7 pad.10.clone
  79.7 1.3 copy-done.3
  81.1 3.7 %fusion.9 = f32[2,3,8,5,64]{4,2,3,1,0:T(8,128)S(1)} fusion(bf16[3,3,3,1024,64]{3,4,2,1,0:T(8,128)(2,1)S(1)} %bitcast.71, bf16[4,5,1,7,2,1024]{5,3,4,1,0,2:T(8,128)(2,1)S(1)} %slice.14, bf16[4,5,1,8,5,1024]{5,3,4,1,0,2:T(8,128)(2,1)S(1)} %copy.41, pred[8,5]{0,1:T(8,128)(4,1)S(1)} %copy-done.4), kind=kOutput, calls=%fused_computation.11 | convolution fusion | flops 856243200 | bytes 5812264 | tf_op jit(solution)/shard_map/conv_general_dilated | solution.py:63
  85.2 0.8 convolution_select_fusion
  86.2 0.8 copy.46
  87.0 1.9 %reshape_reshape_squeeze.3 = f32[64,2,8,64]{3,2,1,0:T(8,128)} reshape(f32[2,1,1,32,1024]{4,3,0,2,1:T(8,128)} %copy.46) | data formatting | bytes 524288 | tf_op jit(solution)/shard_map/reshape;reshape;squeeze | solution.py:86
  88.9 2.1 %copy.58 = f32[64,2,8,64]{3,1,0,2:T(2,128)} copy(f32[64,2,8,64]{3,2,1,0:T(8,128)} %reshape_reshape_squeeze.3) | data formatting | bytes 524288 | tf_op jit(solution)/shard_map/reshape;reshape;squeeze | solution.py:86
  91.0 2.3 %reshape.114 = f32[8,1,8192]{2,1,0:T(1,128)} reshape(f32[8,64,2,64]{3,2,1,0:T(2,128)} %bitcast.60) | data formatting | bytes 524288
  93.3 11.5 %all_to_all.11 = f32[8,1,8192]{2,1,0:T(1,128)} all-to-all(f32[8,1,8192]{2,1,0:T(1,128)} %reshape.114), channel_id=1, replica_groups=mesh['space'=64,'zh'=2,'inner'=8] {'inner'}, dimensions={0} | all-to-all | bytes 524288 | tf_op jit(solution)/shard_map/all_to_all | solution.py:87
  105.4 2.9 %reduce = f32[8,8192]{1,0:T(8,128)} reduce(f32[8,1,8192]{2,1,0:T(1,128)} %all_to_all.11, f32[]{:T(128)} %broadcast.80), dimensions={1}, to_apply=%all_to_all.7.reduce_sub_computation | reduce | bytes 524292 | tf_op jit(solution)/shard_map/all_to_all | solution.py:87
  108.3 2.1 %reshape.115 = f32[8,64,2,64]{3,2,1,0:T(2,128)} reshape(f32[8,8192]{1,0:T(8,128)} %reduce) | data formatting | bytes 524288
  110.4 1.2 bitcast_reduce_fusion
  111.7 16.2 %collective-permute-start.5 = (f32[64,64]{1,0:T(8,128)S(1)}, f32[64,64]{1,0:T(8,128)S(1)}, u32[]{:S(2)}, u32[]{:S(2)}) collective-permute-start(f32[64,64]{1,0:T(8,128)S(1)} %bitcast.69), channel_id=1, source_target_pairs={{0,8},{8,0},{1,9},{9,1},{2,10},{10,2},{3,11},{11,3},{4,12},{12,4},... | collective-permute-start | bytes 49160 | tf_op jit(solution)/shard_map/ppermute | solution.py:32
  127.9 8.3 %collective-permute-done.5 = f32[64,64]{1,0:T(8,128)S(1)} collective-permute-done((f32[64,64]{1,0:T(8,128)S(1)}, f32[64,64]{1,0:T(8,128)S(1)}, u32[]{:S(2)}, u32[]{:S(2)}) %collective-permute-start.5) | collective-permute-done | bytes 16416 | tf_op jit(solution)/shard_map/ppermute | solution.py:32
  136.2 1.3 add_convert_fusion
  (31 shorter events, 2.2 us)
Async XLA Ops:
  0.0 85.1 %copy-start = (bf16[27,64,1024]{2,1,0:T(8,128)(2,1)S(1)}, bf16[27,64,1024]{2,1,0:T(8,128)(2,1)}, u32[]{:S(2)}) copy-start(bf16[27,64,1024]{2,1,0:T(8,128)(2,1)} %param.8) | copy-start | bytes 10616836
  0.0 31.1 %collective-permute-start = (bf16[2,1,32,64]{3,2,1,0:T(8,128)(2,1)}, bf16[2,1,32,64]{3,2,1,0:T(8,128)(2,1)S(1)}, u32[]{:S(2)}, u32[]{:S(2)}) collective-permute-start(bf16[2,1,32,64]{3,2,1,0:T(8,128)(2,1)} %param.5), channel_id=1, source_target_pairs={{0,8},{8,0},{1,9},{9,1},{2,10},{10,2},{3,11},{11,3},{4,12},{12,4},... | collective-permute-start | bytes 24584 | tf_op jit(solution)/shard_map/ppermute | solution.py:32
  50.8 20.8 %collective-permute-start.1 = (bf16[2,1,32,1024]{3,2,0,1:T(8,128)(2,1)}, bf16[2,1,32,1024]{3,2,0,1:T(8,128)(2,1)}, u32[]{:S(2)}, u32[]{:S(2)}) collective-permute-start(bf16[2,1,32,1024]{3,2,0,1:T(8,128)(2,1)} %reshape.80), channel_id=1, source_target_pairs={{0,32},{8,40},{16,48},{24,56},{32,64},{40,72},{48,80},{56,88},{64,... | collective-permute-start | bytes 393224 | tf_op jit(solution)/shard_map/ppermute | solution.py:22
  54.4 18.1 %collective-permute-start.2 = (bf16[2,1,32,1024]{3,2,0,1:T(8,128)(2,1)}, bf16[2,1,32,1024]{3,2,0,1:T(8,128)(2,1)S(1)}, u32[]{:S(2)}, u32[]{:S(2)}) collective-permute-start(bf16[2,1,32,1024]{3,2,0,1:T(8,128)(2,1)} %reshape.80), channel_id=1, source_target_pairs={{0,16},{8,24},{16,32},{24,40},{32,48},{40,56},{48,64},{56,72},{64,... | collective-permute-start | bytes 393224 | tf_op jit(solution)/shard_map/ppermute | solution.py:22
  57.4 16.1 %collective-permute-start.3 = (bf16[2,1,32,1024]{3,2,0,1:T(8,128)(2,1)}, bf16[2,1,32,1024]{3,2,0,1:T(8,128)(2,1)S(1)}, u32[]{:S(2)}, u32[]{:S(2)}) collective-permute-start(bf16[2,1,32,1024]{3,2,0,1:T(8,128)(2,1)} %reshape.80), channel_id=1, source_target_pairs={{16,0},{24,8},{32,16},{40,24},{48,32},{56,40},{64,48},{72,56},{80,... | collective-permute-start | bytes 393224 | tf_op jit(solution)/shard_map/ppermute | solution.py:22
  66.8 10.2 %collective-permute-start.4 = (bf16[2,1,32,1024]{3,2,0,1:T(8,128)(2,1)}, bf16[2,1,32,1024]{3,2,0,1:T(8,128)(2,1)S(1)}, u32[]{:S(2)}, u32[]{:S(2)}) collective-permute-start(bf16[2,1,32,1024]{3,2,0,1:T(8,128)(2,1)} %reshape.80), channel_id=1, source_target_pairs={{32,0},{40,8},{48,16},{56,24},{64,32},{72,40},{80,48},{88,56},{96,... | collective-permute-start | bytes 393224 | tf_op jit(solution)/shard_map/ppermute | solution.py:22
  79.1 2.0 %copy-start.3 = (bf16[27,1024,64]{1,2,0:T(8,128)(2,1)S(1)}, bf16[27,1024,64]{1,2,0:T(8,128)(2,1)}, u32[]{:S(2)}) copy-start(bf16[27,1024,64]{1,2,0:T(8,128)(2,1)} %param.6) | copy-start | bytes 10616836
  79.1 2.0 %copy-start.4 = (pred[8,5]{0,1:T(8,128)(4,1)S(1)}, pred[8,5]{0,1:T(8,128)(4,1)}, u32[]{:S(2)}) copy-start(pred[8,5]{0,1:T(8,128)(4,1)} %constant.39) | copy-start | bytes 124
  81.1 3.7 %copy-start.2 = (f32[64]{0:T(128)S(1)}, f32[64]{0:T(128)}, u32[]{:S(2)}) copy-start(f32[64]{0:T(128)} %param.7) | copy-start | bytes 772
  88.9 47.3 %copy-start.1 = (bf16[2,1,32,64]{3,2,1,0:T(8,128)(2,1)S(1)}, bf16[2,1,32,64]{3,2,1,0:T(8,128)(2,1)}, u32[]{:S(2)}) copy-start(bf16[2,1,32,64]{3,2,1,0:T(8,128)(2,1)} %param.5) | copy-start | bytes 24580
  111.7 24.5 %collective-permute-start.5 = (f32[64,64]{1,0:T(8,128)S(1)}, f32[64,64]{1,0:T(8,128)S(1)}, u32[]{:S(2)}, u32[]{:S(2)}) collective-permute-start(f32[64,64]{1,0:T(8,128)S(1)} %bitcast.69), channel_id=1, source_target_pairs={{0,8},{8,0},{1,9},{9,1},{2,10},{10,2},{3,11},{11,3},{4,12},{12,4},... | collective-permute-start | bytes 49160 | tf_op jit(solution)/shard_map/ppermute | solution.py:32

commit v5 on v4

--- a/solution.py
+++ b/solution.py
@@ -83,11 +83,19 @@
 
 def reduce_channels(partial, own_chan):
     inner_count = lax.axis_size("inner")
-    blocks = partial.reshape(partial.shape[0], HALVES, inner_count, own_chan)
-    sums = lax.all_to_all(blocks, "inner", 2, 2, tiled=True).sum(2)
+    idx = lax.axis_index("inner")
+    cur = partial.reshape(partial.shape[0], HALVES, -1)
+    step = inner_count // 2
+    while step >= 1:
+        split = cur.reshape(cur.shape[0], HALVES, 2, -1)
+        upper = (idx // step) % 2 == 1
+        keep = jnp.where(upper, split[:, :, 1], split[:, :, 0])
+        send = jnp.where(upper, split[:, :, 0], split[:, :, 1])
+        cur = keep + lax.ppermute(send, "inner", [(i, i ^ step) for i in range(inner_count)])
+        step //= 2
     half = lax.axis_index("zh")
-    mine = jnp.where(half == 0, sums[:, 0], sums[:, 1])
-    theirs = jnp.where(half == 0, sums[:, 1], sums[:, 0])
+    mine = jnp.where(half == 0, cur[:, 0], cur[:, 1])
+    theirs = jnp.where(half == 0, cur[:, 1], cur[:, 0])
     return mine + swap_halves(theirs)
 
 

time: 138 us -> 147 us (1.065)
  blocking collectives: 22 us -> 10.5 us
  waiting for transfers between devices: 13.7 us -> 23.5 us
  starting transfers between devices: 66.2 us -> 73.4 us
  other arithmetic: 6.42 us -> 9.42 us
    all_to_all x1 -> x0, blocking collectives: 11.5 us -> none  [reduce_channels(): sums = lax.all_to_all(blocks, 'inner', 2, 2, tiled=True).sum(2)]
    ppermute x0 -> x3, waiting for transfers between devices: none -> 11 us  [reduce_channels(): lax.ppermute(send, 'inner', [(i, i ^ step) for i in range(inner_count)])]
    ppermute x0 -> x3, starting transfers between devices: none -> 7.2 us  [reduce_channels(): lax.ppermute(send, 'inner', [(i, i ^ step) for i in range(inner_count)])]
    reshape x0 -> x2, local copies, waits for them, and re-layouts: none -> 3.36 us  [reduce_channels(): split = cur.reshape(cur.shape[0], HALVES, 2, -1)]
    add x0 -> x3, other arithmetic: none -> 3.36 us  [reduce_channels(): keep + lax.ppermute(send, 'inner', [(i, i ^ step) for i in range(inner_co...]
    slice x1 -> x2, other arithmetic: 0.06 us -> 3.11 us  [reduce_channels(): keep = jnp.where(upper, split[:, :, 1], split[:, :, 0])]
    all_to_all x1 -> x0, other arithmetic: 2.92 us -> none  [reduce_channels(): sums = lax.all_to_all(blocks, 'inner', 2, 2, tiled=True).sum(2)]
    unnamed x20 -> x22, local copies, waits for them, and re-layouts: 13.2 us -> 11.1 us
  transfers between devices with their start and end apart: 6 -> 9, of which waited for: 3 -> 6; matrix products, arithmetic and copies ran while one was open for 1% -> 2% of each run, Pallas kernels for 0% -> 0%
where the time goes in v5:
time: 147 us; the launch traced here: 146 us
  starting transfers between devices  73.4 us (50%)
  local copies, waits for them, and re-layouts  24.1 us (16%)
  waiting for transfers between devices  23.5 us (16%)
  blocking collectives  10.5 us (7%)
  other arithmetic  9.42 us (6%)
  matrix products  4.44 us (3%)
    ppermute x2, starting transfers between devices, swap_halves(): return lax.ppermute(v, 'zh', [(0, 1), (1, 0)])  45.4 us
    ppermute x4, starting transfers between devices, row_from(): return lax.ppermute(cells, ('space', 'zh'), pairs)  20.8 us
    unnamed x22, local copies, waits for them, and re-layouts  11.1 us
    ppermute x3, waiting for transfers between devices, reduce_channels(): lax.ppermute(send, 'inner', [(i, i ^ step) for i in range(inner_count)])  11 us
    all_to_all x1, blocking collectives, gather_channels(): inner = lax.all_to_all(copies, 'inner', 4, 4, tiled=True)  10.5 us
    ppermute x2, waiting for transfers between devices, swap_halves(): return lax.ppermute(v, 'zh', [(0, 1), (1, 0)])  9.85 us
    ppermute x3, starting transfers between devices, reduce_channels(): lax.ppermute(send, 'inner', [(i, i ^ step) for i in range(inner_count)])  7.2 us
    conv_general_dilated x2, matrix products, conv3(): lax.conv_general_dilated(padded[None], taps, (1, 1, 1), 'VALID', dimensio...  4.44 us
  transfers between devices with their start and end apart: 9, of which 6 were waited for; matrix products, arithmetic and copies ran while one was open for 2% of the time, Pallas kernels for 0%

profile of v5, /device:TPU:24, one launch (start us, length us, event | category | flops | bytes accessed | tf_op | source)
XLA Modules:
  0.0 145.7 jit_solution(9556638001592392845)
XLA Ops:
  0.0 29.2 %collective-permute-start = (bf16[2,1,32,64]{3,2,1,0:T(8,128)(2,1)}, bf16[2,1,32,64]{3,2,1,0:T(8,128)(2,1)S(1)}, u32[]{:S(2)}, u32[]{:S(2)}) collective-permute-start(bf16[2,1,32,64]{3,2,1,0:T(8,128)(2,1)} %param.5), channel_id=1, source_target_pairs={{0,8},{8,0},{1,9},{9,1},{2,10},{10,2},{3,11},{11,3},{4,12},{12,4},... | collective-permute-start | bytes 24584 | tf_op jit(solution)/shard_map/ppermute | solution.py:32
  29.2 1.9 %collective-permute-done = bf16[2,1,32,64]{3,2,1,0:T(8,128)(2,1)S(1)} collective-permute-done((bf16[2,1,32,64]{3,2,1,0:T(8,128)(2,1)}, bf16[2,1,32,64]{3,2,1,0:T(8,128)(2,1)S(1)}, u32[]{:S(2)}, u32[]{:S(2)}) %collective-permute-start) | collective-permute-done | bytes 8224 | tf_op jit(solution)/shard_map/ppermute | solution.py:32
  32.9 1.8 %reshape.133 = bf16[8,2,4096]{2,1,0:T(2,128)(2,1)} reshape(bf16[8,1,32,2,2,64]{5,4,3,2,1,0:T(2,128)(2,1)} %broadcast_bitcast_fusion) | data formatting | bytes 262144
  34.7 10.5 %all_to_all.5 = bf16[8,2,4096]{2,1,0:T(2,128)(2,1)} all-to-all(bf16[8,2,4096]{2,1,0:T(2,128)(2,1)} %reshape.133), channel_id=1, replica_groups=mesh['space'=64,'zh'=2,'inner'=8] {'inner'}, dimensions={0} | all-to-all | bytes 262144 | tf_op jit(solution)/shard_map/all_to_all | solution.py:80
  45.2 1.8 %reshape.134 = bf16[8,1,32,2,2,64]{5,4,3,2,1,0:T(2,128)(2,1)} reshape(bf16[8,2,4096]{2,1,0:T(2,128)(2,1)} %all_to_all.5) | data formatting | bytes 262144
  47.0 2.0 %copy.58 = bf16[2,1,32,2,8,64]{5,4,3,2,0,1:T(8,128)(2,1)} copy(bf16[2,1,32,2,8,64]{5,3,0,2,1,4:T(2,128)(2,1)} %bitcast.74) | data formatting | bytes 262144 | tf_op jit(solution)/shard_map/all_to_all | solution.py:80
  49.0 1.8 %reshape.98 = bf16[2,1,32,1024]{3,2,0,1:T(8,128)(2,1)} reshape(bf16[2,1,32,2,8,64]{5,4,3,2,0,1:T(8,128)(2,1)} %copy.58) | data formatting | bytes 262144 | tf_op jit(solution)/shard_map/reshape | solution.py:81
  50.8 3.6 %collective-permute-start.1 = (bf16[2,1,32,1024]{3,2,0,1:T(8,128)(2,1)}, bf16[2,1,32,1024]{3,2,0,1:T(8,128)(2,1)}, u32[]{:S(2)}, u32[]{:S(2)}) collective-permute-start(bf16[2,1,32,1024]{3,2,0,1:T(8,128)(2,1)} %reshape.98), channel_id=1, source_target_pairs={{0,32},{8,40},{16,48},{24,56},{32,64},{40,72},{48,80},{56,88},{64,... | collective-permute-start | bytes 393224 | tf_op jit(solution)/shard_map/ppermute | solution.py:22
  54.5 2.9 %collective-permute-start.2 = (bf16[2,1,32,1024]{3,2,0,1:T(8,128)(2,1)}, bf16[2,1,32,1024]{3,2,0,1:T(8,128)(2,1)}, u32[]{:S(2)}, u32[]{:S(2)}) collective-permute-start(bf16[2,1,32,1024]{3,2,0,1:T(8,128)(2,1)} %reshape.98), channel_id=1, source_target_pairs={{0,16},{8,24},{16,32},{24,40},{32,48},{40,56},{48,64},{56,72},{64,... | collective-permute-start | bytes 393224 | tf_op jit(solution)/shard_map/ppermute | solution.py:22
  57.4 9.4 %collective-permute-start.3 = (bf16[2,1,32,1024]{3,2,0,1:T(8,128)(2,1)}, bf16[2,1,32,1024]{3,2,0,1:T(8,128)(2,1)S(1)}, u32[]{:S(2)}, u32[]{:S(2)}) collective-permute-start(bf16[2,1,32,1024]{3,2,0,1:T(8,128)(2,1)} %reshape.98), channel_id=1, source_target_pairs={{16,0},{24,8},{32,16},{40,24},{48,32},{56,40},{64,48},{72,56},{80,... | collective-permute-start | bytes 393224 | tf_op jit(solution)/shard_map/ppermute | solution.py:22
  66.8 4.8 %collective-permute-start.4 = (bf16[2,1,32,1024]{3,2,0,1:T(8,128)(2,1)}, bf16[2,1,32,1024]{3,2,0,1:T(8,128)(2,1)S(1)}, u32[]{:S(2)}, u32[]{:S(2)}) collective-permute-start(bf16[2,1,32,1024]{3,2,0,1:T(8,128)(2,1)} %reshape.98), channel_id=1, source_target_pairs={{32,0},{40,8},{48,16},{56,24},{64,32},{72,40},{80,48},{88,56},{96,... | collective-permute-start | bytes 393224 | tf_op jit(solution)/shard_map/ppermute | solution.py:22
  74.5 2.6 %collective-permute-done.4 = bf16[2,1,32,1024]{3,2,0,1:T(8,128)(2,1)S(1)} collective-permute-done((bf16[2,1,32,1024]{3,2,0,1:T(8,128)(2,1)}, bf16[2,1,32,1024]{3,2,0,1:T(8,128)(2,1)S(1)}, u32[]{:S(2)}, u32[]{:S(2)}) %collective-permute-start.4) | collective-permute-done | bytes 131104 | tf_op jit(solution)/shard_map/ppermute | solution.py:22
  77.4 1.1 copy.88
  79.8 1.3 copy-done.4
  81.1 3.7 %fusion.9 = f32[2,3,8,5,64]{4,2,3,1,0:T(8,128)S(1)} fusion(bf16[3,3,3,1024,64]{3,4,2,1,0:T(8,128)(2,1)S(1)} %bitcast.85, bf16[4,5,1,7,2,1024]{5,3,4,1,0,2:T(8,128)(2,1)S(1)} %slice.44, bf16[4,5,1,8,5,1024]{5,3,4,1,0,2:T(8,128)(2,1)S(1)} %copy.61, pred[8,5]{0,1:T(8,128)(4,1)S(1)} %copy-done.5), kind=kOutput, calls=%fused_computation.11 | convolution fusion | flops 856243200 | bytes 5812264 | tf_op jit(solution)/shard_map/conv_general_dilated | solution.py:63
  87.1 1.9 %reshape_reshape_reshape_squeeze.3 = f32[64,2,2,256]{3,2,1,0:T(2,128)} reshape(f32[2,1,1,32,1024]{4,3,0,2,1:T(8,128)} %copy.66) | data formatting | bytes 524288 | tf_op jit(solution)/shard_map/reshape;reshape;reshape;squeeze | solution.py:90
  88.9 2.0 %fusion.31 = (f32[64,2,1,256]{3,2,1,0:T(1,128)}, f32[64,2,1,256]{3,2,1,0:T(1,128)S(1)}, f32[64,2,1,256]{3,2,1,0:T(1,128)}) fusion(f32[64,2,2,256]{3,2,1,0:T(2,128)} %reshape_reshape_reshape_squeeze.3, pred[]{:T(512)S(6)} %eq.21), kind=kLoop, calls=%fused_computation.51 | loop fusion | flops 32768 | bytes 655361 | tf_op jit(solution)/shard_map/slice | solution.py:92
  91.7 2.8 %collective-permute-start.5 = (f32[64,2,256]{2,1,0:T(2,128)}, f32[64,2,256]{2,1,0:T(2,128)}, u32[]{:S(2)}, u32[]{:S(2)}) collective-permute-start(f32[64,2,256]{2,1,0:T(2,128)} %bitcast.70), channel_id=1, source_target_pairs={{0,4},{1,5},{2,6},{3,7},{4,0},{5,1},{6,2},{7,3},{8,12},{9,13},{10,... | collective-permute-start | bytes 393224 | tf_op jit(solution)/shard_map/ppermute | solution.py:94
  94.5 5.8 %collective-permute-done.5 = f32[64,2,256]{2,1,0:T(2,128)} collective-permute-done((f32[64,2,256]{2,1,0:T(2,128)}, f32[64,2,256]{2,1,0:T(2,128)}, u32[]{:S(2)}, u32[]{:S(2)}) %collective-permute-start.5) | collective-permute-done | bytes 131104 | tf_op jit(solution)/shard_map/ppermute | solution.py:94
  100.3 1.8 %fusion.20 = f32[64,2,256]{2,1,0:T(2,128)} fusion(f32[64,2,256]{2,1,0:T(2,128)} %collective-permute-done.5, f32[64,2,1,256]{3,2,1,0:T(1,128)} %get-tuple-element.7, f32[64,2,1,256]{3,2,1,0:T(1,128)} %get-tuple-element.5, pred[]{:T(512)S(6)} %eq.21), kind=kLoop, calls=%fused_computation.22 | loop fusion | flops 65536 | bytes 524289 | tf_op jit(solution)/shard_map/add | solution.py:94
  102.1 1.7 %reshape.132 = f32[64,2,2,128]{3,2,1,0:T(2,128)} reshape(f32[64,2,256]{2,1,0:T(2,128)} %fusion.20) | data formatting | bytes 262144 | tf_op jit(solution)/shard_map/reshape | solution.py:90
  103.9 1.1 fusion.33
  106.3 2.5 %collective-permute-start.6 = (f32[64,2,128]{2,0,1:T(8,128)}, f32[64,2,128]{2,0,1:T(8,128)}, u32[]{:S(2)}, u32[]{:S(2)}) collective-permute-start(f32[64,2,128]{2,0,1:T(8,128)} %bitcast.17), channel_id=1, source_target_pairs={{0,2},{1,3},{2,0},{3,1},{4,6},{5,7},{6,4},{7,5},{8,10},{9,11},{10,... | collective-permute-start | bytes 196616 | tf_op jit(solution)/shard_map/ppermute | solution.py:94
  108.8 4.0 %collective-permute-done.6 = f32[64,2,128]{2,0,1:T(8,128)} collective-permute-done((f32[64,2,128]{2,0,1:T(8,128)}, f32[64,2,128]{2,0,1:T(8,128)}, u32[]{:S(2)}, u32[]{:S(2)}) %collective-permute-start.6) | collective-permute-done | bytes 65568 | tf_op jit(solution)/shard_map/ppermute | solution.py:94
  112.8 1.5 %bitcast_add_fusion.1 = f32[64,2,128]{2,0,1:T(8,128)} fusion(f32[64,2,128]{2,0,1:T(8,128)} %collective-permute-done.6, f32[64,2,1,128]{3,0,1,2:T(8,128)} %bitcast.80, pred[]{:T(512)S(6)} %eq.20, f32[64,2,1,128]{3,2,1,0:T(1,128)} %copy-done.1), kind=kLoop, calls=%fused_computation.34 | loop fusion | flops 32768 | bytes 262145 | tf_op jit(solution)/shard_map/add | solution.py:94
  114.3 1.6 %reshape.102 = f32[64,2,2,64]{3,2,0,1:T(2,128)} reshape(f32[64,2,128]{2,0,1:T(8,128)} %bitcast_add_fusion.1) | data formatting | bytes 131072 | tf_op jit(solution)/shard_map/reshape | solution.py:90
  116.0 1.1 fusion.32
  117.1 1.9 %collective-permute-start.7 = (f32[64,2,64]{2,0,1:T(8,128)S(1)}, f32[64,2,64]{2,0,1:T(8,128)S(1)}, u32[]{:S(2)}, u32[]{:S(2)}) collective-permute-start(f32[64,2,64]{2,0,1:T(8,128)S(1)} %bitcast.82), channel_id=1, source_target_pairs={{0,1},{1,0},{2,3},{3,2},{4,5},{5,4},{6,7},{7,6},{8,9},{9,8},{10,11... | collective-permute-start | bytes 98312 | tf_op jit(solution)/shard_map/ppermute | solution.py:94
  119.0 1.2 collective-permute-done.7
  120.3 16.2 %collective-permute-start.8 = (f32[64,64]{1,0:T(8,128)S(1)}, f32[64,64]{1,0:T(8,128)S(1)}, u32[]{:S(2)}, u32[]{:S(2)}) collective-permute-start(f32[64,64]{1,0:T(8,128)S(1)} %select_bitcast_fusion), channel_id=1, source_target_pairs={{0,8},{8,0},{1,9},{9,1},{2,10},{10,2},{3,11},{11,3},{4,12},{12,4},... | collective-permute-start | bytes 49160 | tf_op jit(solution)/shard_map/ppermute | solution.py:32
  136.5 7.9 %collective-permute-done.8 = f32[64,64]{1,0:T(8,128)S(1)} collective-permute-done((f32[64,64]{1,0:T(8,128)S(1)}, f32[64,64]{1,0:T(8,128)S(1)}, u32[]{:S(2)}, u32[]{:S(2)}) %collective-permute-start.8) | collective-permute-done | bytes 16416 | tf_op jit(solution)/shard_map/ppermute | solution.py:32
  144.4 1.3 add_convert_fusion
  (43 shorter events, 10.3 us)
Async XLA Ops:
  0.0 85.2 %copy-start = (bf16[27,64,1024]{2,1,0:T(8,128)(2,1)S(1)}, bf16[27,64,1024]{2,1,0:T(8,128)(2,1)}, u32[]{:S(2)}) copy-start(bf16[27,64,1024]{2,1,0:T(8,128)(2,1)} %param.8) | copy-start | bytes 10616836
  0.0 31.1 %collective-permute-start = (bf16[2,1,32,64]{3,2,1,0:T(8,128)(2,1)}, bf16[2,1,32,64]{3,2,1,0:T(8,128)(2,1)S(1)}, u32[]{:S(2)}, u32[]{:S(2)}) collective-permute-start(bf16[2,1,32,64]{3,2,1,0:T(8,128)(2,1)} %param.5), channel_id=1, source_target_pairs={{0,8},{8,0},{1,9},{9,1},{2,10},{10,2},{3,11},{11,3},{4,12},{12,4},... | collective-permute-start | bytes 24584 | tf_op jit(solution)/shard_map/ppermute | solution.py:32
  50.8 20.9 %collective-permute-start.1 = (bf16[2,1,32,1024]{3,2,0,1:T(8,128)(2,1)}, bf16[2,1,32,1024]{3,2,0,1:T(8,128)(2,1)}, u32[]{:S(2)}, u32[]{:S(2)}) collective-permute-start(bf16[2,1,32,1024]{3,2,0,1:T(8,128)(2,1)} %reshape.98), channel_id=1, source_target_pairs={{0,32},{8,40},{16,48},{24,56},{32,64},{40,72},{48,80},{56,88},{64,... | collective-permute-start | bytes 393224 | tf_op jit(solution)/shard_map/ppermute | solution.py:22
  54.5 18.1 %collective-permute-start.2 = (bf16[2,1,32,1024]{3,2,0,1:T(8,128)(2,1)}, bf16[2,1,32,1024]{3,2,0,1:T(8,128)(2,1)}, u32[]{:S(2)}, u32[]{:S(2)}) collective-permute-start(bf16[2,1,32,1024]{3,2,0,1:T(8,128)(2,1)} %reshape.98), channel_id=1, source_target_pairs={{0,16},{8,24},{16,32},{24,40},{32,48},{40,56},{48,64},{56,72},{64,... | collective-permute-start | bytes 393224 | tf_op jit(solution)/shard_map/ppermute | solution.py:22
  57.4 17.0 %collective-permute-start.3 = (bf16[2,1,32,1024]{3,2,0,1:T(8,128)(2,1)}, bf16[2,1,32,1024]{3,2,0,1:T(8,128)(2,1)S(1)}, u32[]{:S(2)}, u32[]{:S(2)}) collective-permute-start(bf16[2,1,32,1024]{3,2,0,1:T(8,128)(2,1)} %reshape.98), channel_id=1, source_target_pairs={{16,0},{24,8},{32,16},{40,24},{48,32},{56,40},{64,48},{72,56},{80,... | collective-permute-start | bytes 393224 | tf_op jit(solution)/shard_map/ppermute | solution.py:22
  66.8 10.2 %collective-permute-start.4 = (bf16[2,1,32,1024]{3,2,0,1:T(8,128)(2,1)}, bf16[2,1,32,1024]{3,2,0,1:T(8,128)(2,1)S(1)}, u32[]{:S(2)}, u32[]{:S(2)}) collective-permute-start(bf16[2,1,32,1024]{3,2,0,1:T(8,128)(2,1)} %reshape.98), channel_id=1, source_target_pairs={{32,0},{40,8},{48,16},{56,24},{64,32},{72,40},{80,48},{88,56},{96,... | collective-permute-start | bytes 393224 | tf_op jit(solution)/shard_map/ppermute | solution.py:22
  79.1 2.0 %copy-start.4 = (bf16[27,1024,64]{1,2,0:T(8,128)(2,1)S(1)}, bf16[27,1024,64]{1,2,0:T(8,128)(2,1)}, u32[]{:S(2)}) copy-start(bf16[27,1024,64]{1,2,0:T(8,128)(2,1)} %param.6) | copy-start | bytes 10616836
  79.1 2.0 %copy-start.5 = (pred[8,5]{0,1:T(8,128)(4,1)S(1)}, pred[8,5]{0,1:T(8,128)(4,1)}, u32[]{:S(2)}) copy-start(pred[8,5]{0,1:T(8,128)(4,1)} %constant.90) | copy-start | bytes 124
  81.1 3.8 %copy-start.3 = (f32[64]{0:T(128)S(1)}, f32[64]{0:T(128)}, u32[]{:S(2)}) copy-start(f32[64]{0:T(128)} %param.7) | copy-start | bytes 772
  86.3 58.1 %copy-start.2 = (bf16[2,1,32,64]{3,2,1,0:T(8,128)(2,1)S(1)}, bf16[2,1,32,64]{3,2,1,0:T(8,128)(2,1)}, u32[]{:S(2)}) copy-start(bf16[2,1,32,64]{3,2,1,0:T(8,128)(2,1)} %param.5) | copy-start | bytes 24580
  91.7 8.7 %collective-permute-start.5 = (f32[64,2,256]{2,1,0:T(2,128)}, f32[64,2,256]{2,1,0:T(2,128)}, u32[]{:S(2)}, u32[]{:S(2)}) collective-permute-start(f32[64,2,256]{2,1,0:T(2,128)} %bitcast.70), channel_id=1, source_target_pairs={{0,4},{1,5},{2,6},{3,7},{4,0},{5,1},{6,2},{7,3},{8,12},{9,13},{10,... | collective-permute-start | bytes 393224 | tf_op jit(solution)/shard_map/ppermute | solution.py:94
  105.0 0.6 copy-start.1
  106.3 6.5 %collective-permute-start.6 = (f32[64,2,128]{2,0,1:T(8,128)}, f32[64,2,128]{2,0,1:T(8,128)}, u32[]{:S(2)}, u32[]{:S(2)}) collective-permute-start(f32[64,2,128]{2,0,1:T(8,128)} %bitcast.17), channel_id=1, source_target_pairs={{0,2},{1,3},{2,0},{3,1},{4,6},{5,7},{6,4},{7,5},{8,10},{9,11},{10,... | collective-permute-start | bytes 196616 | tf_op jit(solution)/shard_map/ppermute | solution.py:94
  117.1 3.1 %collective-permute-start.7 = (f32[64,2,64]{2,0,1:T(8,128)S(1)}, f32[64,2,64]{2,0,1:T(8,128)S(1)}, u32[]{:S(2)}, u32[]{:S(2)}) collective-permute-start(f32[64,2,64]{2,0,1:T(8,128)S(1)} %bitcast.82), channel_id=1, source_target_pairs={{0,1},{1,0},{2,3},{3,2},{4,5},{5,4},{6,7},{7,6},{8,9},{9,8},{10,11... | collective-permute-start | bytes 98312 | tf_op jit(solution)/shard_map/ppermute | solution.py:94
  120.3 24.1 %collective-permute-start.8 = (f32[64,64]{1,0:T(8,128)S(1)}, f32[64,64]{1,0:T(8,128)S(1)}, u32[]{:S(2)}, u32[]{:S(2)}) collective-permute-start(f32[64,64]{1,0:T(8,128)S(1)} %select_bitcast_fusion), channel_id=1, source_target_pairs={{0,8},{8,0},{1,9},{9,1},{2,10},{10,2},{3,11},{11,3},{4,12},{12,4},... | collective-permute-start | bytes 49160 | tf_op jit(solution)/shard_map/ppermute | solution.py:32

commit v6 on v4

--- a/solution.py
+++ b/solution.py
@@ -74,11 +74,11 @@
 def gather_channels(latent):
     other = swap_halves(latent)
     half = lax.axis_index("zh")
-    pair = jnp.where(half == 0, jnp.stack([latent, other], 3), jnp.stack([other, latent], 3))
-    inner_count = lax.axis_size("inner")
-    copies = jnp.broadcast_to(pair[:, :, :, :, None], pair.shape[:4] + (inner_count,) + pair.shape[4:])
-    inner = lax.all_to_all(copies, "inner", 4, 4, tiled=True)
-    return inner.reshape(inner.shape[:3] + (-1,))
+    pair = jnp.where(half == 0, jnp.stack([latent, other]), jnp.stack([other, latent]))
+    inner = lax.all_gather(pair, "inner", axis=0, tiled=False)
+    frame_count, row_count, col_count, own_chan = latent.shape
+    total = inner.shape[0] * HALVES * own_chan
+    return jnp.transpose(inner, (2, 3, 4, 1, 0, 5)).reshape(frame_count, row_count, col_count, total)
 
 
 def reduce_channels(partial, own_chan):

time: 138 us -> 134 us (0.971)
  local copies, waits for them, and re-layouts: 24.4 us -> 18.8 us
  waiting for transfers between devices: 13.7 us -> 9.62 us
  blocking collectives: 22 us -> 24.7 us
  starting transfers between devices: 66.2 us -> 68.3 us
    all_gather x0 -> x1, blocking collectives: none -> 13.2 us  [gather_channels(): inner = lax.all_gather(pair, 'inner', axis=0, tiled=False)]
    all_to_all x1 -> x0, blocking collectives: 10.5 us -> none  [gather_channels(): inner = lax.all_to_all(copies, 'inner', 4, 4, tiled=True)]
    unnamed x20 -> x17, local copies, waits for them, and re-layouts: 13.2 us -> 8.71 us
    ppermute x2, waiting for transfers between devices: 10.2 us -> 7.77 us  [swap_halves(): return lax.ppermute(v, 'zh', [(0, 1), (1, 0)])]
    ppermute x2, starting transfers between devices: 45.4 us -> 47.5 us  [swap_halves(): return lax.ppermute(v, 'zh', [(0, 1), (1, 0)])]
    all_to_all x1 -> x0, local copies, waits for them, and re-layouts: 1.96 us -> none  [gather_channels(): inner = lax.all_to_all(copies, 'inner', 4, 4, tiled=True)]
    ppermute x4, waiting for transfers between devices: 3.52 us -> 1.86 us  [row_from(): return lax.ppermute(cells, ('space', 'zh'), pairs)]
  transfers between devices with their start and end apart: 6 -> 6, of which waited for: 3 -> 4; matrix products, arithmetic and copies ran while one was open for 1% -> 1% of each run, Pallas kernels for 0% -> 0%
where the time goes in v6:
time: 134 us; the launch traced here: 133 us
  starting transfers between devices  68.3 us (51%)
  blocking collectives  24.7 us (18%)
  local copies, waits for them, and re-layouts  18.8 us (14%)
  waiting for transfers between devices  9.62 us (7%)
  other arithmetic  6.42 us (5%)
  matrix products  4.43 us (3%)
    ppermute x2, starting transfers between devices, swap_halves(): return lax.ppermute(v, 'zh', [(0, 1), (1, 0)])  47.5 us
    ppermute x4, starting transfers between devices, row_from(): return lax.ppermute(cells, ('space', 'zh'), pairs)  20.8 us
    all_gather x1, blocking collectives, gather_channels(): inner = lax.all_gather(pair, 'inner', axis=0, tiled=False)  13.2 us
    all_to_all x1, blocking collectives, reduce_channels(): sums = lax.all_to_all(blocks, 'inner', 2, 2, tiled=True).sum(2)  11.5 us
    unnamed x17, local copies, waits for them, and re-layouts  8.71 us
    ppermute x2, waiting for transfers between devices, swap_halves(): return lax.ppermute(v, 'zh', [(0, 1), (1, 0)])  7.77 us
    conv_general_dilated x2, matrix products, conv3(): lax.conv_general_dilated(padded[None], taps, (1, 1, 1), 'VALID', dimensio...  4.43 us
    another operation x2, local copies, waits for them, and re-layouts, reduce_channels(): blocks = partial.reshape(partial.shape[0], HALVES, inner_count, own_chan)  4 us
  transfers between devices with their start and end apart: 6, of which 4 were waited for; matrix products, arithmetic and copies ran while one was open for 1% of the time, Pallas kernels for 0%

profile of v6, /device:TPU:24, one launch (start us, length us, event | category | flops | bytes accessed | tf_op | source)
XLA Modules:
  0.0 132.5 jit_solution(10036193122673043076)
XLA Ops:
  0.0 29.2 %collective-permute-start = (bf16[2,1,32,64]{3,2,0,1:T(8,128)(2,1)}, bf16[2,1,32,64]{3,2,0,1:T(8,128)(2,1)S(1)}, u32[]{:S(2)}, u32[]{:S(2)}) collective-permute-start(bf16[2,1,32,64]{3,2,0,1:T(8,128)(2,1)} %bitcast.67), channel_id=1, source_target_pairs={{0,8},{8,0},{1,9},{9,1},{2,10},{10,2},{3,11},{11,3},{4,12},{12,4},... | collective-permute-start | bytes 24584 | tf_op jit(solution)/shard_map/ppermute | solution.py:32
  29.2 1.9 %collective-permute-done = bf16[2,1,32,64]{3,2,0,1:T(8,128)(2,1)S(1)} collective-permute-done((bf16[2,1,32,64]{3,2,0,1:T(8,128)(2,1)}, bf16[2,1,32,64]{3,2,0,1:T(8,128)(2,1)S(1)}, u32[]{:S(2)}, u32[]{:S(2)}) %collective-permute-start) | collective-permute-done | bytes 8224 | tf_op jit(solution)/shard_map/ppermute | solution.py:32
  31.2 0.8 maximum_select_fusion
  32.0 13.2 %all_gather.4 = bf16[8,2,2,1,32,64]{5,4,3,2,1,0:T(8,128)(2,1)S(1)} all-gather(bf16[1,2,2,1,32,64]{5,4,3,2,1,0:T(8,128)(2,1)S(1)} %maximum_select_fusion), channel_id=1, replica_groups=mesh['space'=64,'zh'=2,'inner'=8] {'inner'}, dimensions={0}, use_global_device_ids=true | all-gather | bytes 147456 | tf_op jit(solution)/shard_map/all_gather | solution.py:78
  45.1 0.9 copy.24
  46.0 1.8 %reshape.104 = bf16[2,1,32,1024]{3,2,0,1:T(8,128)(2,1)} reshape(bf16[2,1,32,2,8,64]{5,4,3,2,0,1:T(8,128)(2,1)} %copy.24) | data formatting | bytes 262144 | tf_op jit(solution)/shard_map/reshape | solution.py:81
  47.8 3.6 %collective-permute-start.1 = (bf16[2,1,32,1024]{3,2,0,1:T(8,128)(2,1)}, bf16[2,1,32,1024]{3,2,0,1:T(8,128)(2,1)}, u32[]{:S(2)}, u32[]{:S(2)}) collective-permute-start(bf16[2,1,32,1024]{3,2,0,1:T(8,128)(2,1)} %reshape.104), channel_id=1, source_target_pairs={{0,32},{8,40},{16,48},{24,56},{32,64},{40,72},{48,80},{56,88},{64,... | collective-permute-start | bytes 393224 | tf_op jit(solution)/shard_map/ppermute | solution.py:22
  51.5 2.9 %collective-permute-start.2 = (bf16[2,1,32,1024]{3,2,0,1:T(8,128)(2,1)}, bf16[2,1,32,1024]{3,2,0,1:T(8,128)(2,1)S(1)}, u32[]{:S(2)}, u32[]{:S(2)}) collective-permute-start(bf16[2,1,32,1024]{3,2,0,1:T(8,128)(2,1)} %reshape.104), channel_id=1, source_target_pairs={{0,16},{8,24},{16,32},{24,40},{32,48},{40,56},{48,64},{56,72},{64,... | collective-permute-start | bytes 393224 | tf_op jit(solution)/shard_map/ppermute | solution.py:22
  54.4 9.4 %collective-permute-start.3 = (bf16[2,1,32,1024]{3,2,0,1:T(8,128)(2,1)}, bf16[2,1,32,1024]{3,2,0,1:T(8,128)(2,1)S(1)}, u32[]{:S(2)}, u32[]{:S(2)}) collective-permute-start(bf16[2,1,32,1024]{3,2,0,1:T(8,128)(2,1)} %reshape.104), channel_id=1, source_target_pairs={{16,0},{24,8},{32,16},{40,24},{48,32},{56,40},{64,48},{72,56},{80,... | collective-permute-start | bytes 393224 | tf_op jit(solution)/shard_map/ppermute | solution.py:22
  63.8 4.8 %collective-permute-start.4 = (bf16[2,1,32,1024]{3,2,0,1:T(8,128)(2,1)}, bf16[2,1,32,1024]{3,2,0,1:T(8,128)(2,1)S(1)}, u32[]{:S(2)}, u32[]{:S(2)}) collective-permute-start(bf16[2,1,32,1024]{3,2,0,1:T(8,128)(2,1)} %reshape.104), channel_id=1, source_target_pairs={{32,0},{40,8},{48,16},{56,24},{64,32},{72,40},{80,48},{88,56},{96,... | collective-permute-start | bytes 393224 | tf_op jit(solution)/shard_map/ppermute | solution.py:22
  68.7 0.9 constant_dynamic-update-slice_fusion.4
  69.8 0.9 constant_dynamic-update-slice_fusion.2
  70.7 1.7 %collective-permute-done.4 = bf16[2,1,32,1024]{3,2,0,1:T(8,128)(2,1)S(1)} collective-permute-done((bf16[2,1,32,1024]{3,2,0,1:T(8,128)(2,1)}, bf16[2,1,32,1024]{3,2,0,1:T(8,128)(2,1)S(1)}, u32[]{:S(2)}, u32[]{:S(2)}) %collective-permute-start.4) | collective-permute-done | bytes 131104 | tf_op jit(solution)/shard_map/ppermute | solution.py:22
  72.4 0.3 pad_bitcast_fusion
  72.7 1.1 copy.42
  73.8 0.7 pad.10.clone
  74.5 0.5 copy.27
  75.1 1.3 %copy-done.3 = bf16[27,1024,64]{1,2,0:T(8,128)(2,1)S(1)} copy-done((bf16[27,1024,64]{1,2,0:T(8,128)(2,1)S(1)}, bf16[27,1024,64]{1,2,0:T(8,128)(2,1)}, u32[]{:S(2)}) %copy-start.3) | copy-done | bytes 3538968
  76.5 3.7 %fusion.9 = f32[2,3,8,5,64]{4,2,3,1,0:T(8,128)S(1)} fusion(bf16[3,3,3,1024,64]{3,4,2,1,0:T(8,128)(2,1)S(1)} %bitcast.71, bf16[4,5,1,7,2,1024]{5,3,4,1,0,2:T(8,128)(2,1)S(1)} %slice.14, bf16[4,5,1,8,5,1024]{5,3,4,1,0,2:T(8,128)(2,1)S(1)} %copy.27, pred[8,5]{0,1:T(8,128)(4,1)S(1)} %copy-done.4), kind=kOutput, calls=%fused_computation.11 | convolution fusion | flops 856243200 | bytes 5812264 | tf_op jit(solution)/shard_map/conv_general_dilated | solution.py:63
  80.5 0.8 convolution_select_fusion
  81.6 0.8 copy.32
  82.4 1.9 %reshape_reshape_squeeze.3 = f32[64,2,8,64]{3,2,1,0:T(8,128)} reshape(f32[2,1,1,32,1024]{4,3,0,2,1:T(8,128)} %copy.32) | data formatting | bytes 524288 | tf_op jit(solution)/shard_map/reshape;reshape;squeeze | solution.py:86
  84.3 2.1 %copy.44 = f32[64,2,8,64]{3,1,0,2:T(2,128)} copy(f32[64,2,8,64]{3,2,1,0:T(8,128)} %reshape_reshape_squeeze.3) | data formatting | bytes 524288 | tf_op jit(solution)/shard_map/reshape;reshape;squeeze | solution.py:86
  86.4 2.3 %reshape.136 = f32[8,1,8192]{2,1,0:T(1,128)} reshape(f32[8,64,2,64]{3,2,1,0:T(2,128)} %bitcast.59) | data formatting | bytes 524288
  88.7 11.5 %all_to_all.5 = f32[8,1,8192]{2,1,0:T(1,128)} all-to-all(f32[8,1,8192]{2,1,0:T(1,128)} %reshape.136), channel_id=1, replica_groups=mesh['space'=64,'zh'=2,'inner'=8] {'inner'}, dimensions={0} | all-to-all | bytes 524288 | tf_op jit(solution)/shard_map/all_to_all | solution.py:87
  100.2 0.5 broadcast.82
  100.7 2.9 %reduce = f32[8,8192]{1,0:T(8,128)} reduce(f32[8,1,8192]{2,1,0:T(1,128)} %all_to_all.5, f32[]{:T(128)} %broadcast.82), dimensions={1}, to_apply=%all_to_all.3.reduce_sub_computation | reduce | bytes 524292 | tf_op jit(solution)/shard_map/all_to_all | solution.py:87
  103.6 2.1 %reshape.137 = f32[8,64,2,64]{3,2,1,0:T(2,128)} reshape(f32[8,8192]{1,0:T(8,128)} %reduce) | data formatting | bytes 524288
  105.8 1.2 bitcast_reduce_fusion
  107.1 18.3 %collective-permute-start.5 = (f32[64,64]{1,0:T(8,128)S(1)}, f32[64,64]{1,0:T(8,128)S(1)}, u32[]{:S(2)}, u32[]{:S(2)}) collective-permute-start(f32[64,64]{1,0:T(8,128)S(1)} %bitcast.69), channel_id=1, source_target_pairs={{0,8},{8,0},{1,9},{9,1},{2,10},{10,2},{3,11},{11,3},{4,12},{12,4},... | collective-permute-start | bytes 49160 | tf_op jit(solution)/shard_map/ppermute | solution.py:32
  125.4 5.9 %collective-permute-done.5 = f32[64,64]{1,0:T(8,128)S(1)} collective-permute-done((f32[64,64]{1,0:T(8,128)S(1)}, f32[64,64]{1,0:T(8,128)S(1)}, u32[]{:S(2)}, u32[]{:S(2)}) %collective-permute-start.5) | collective-permute-done | bytes 16416 | tf_op jit(solution)/shard_map/ppermute | solution.py:32
  131.2 1.3 add_convert_fusion
  (27 shorter events, 1.1 us)
Async XLA Ops:
  0.0 80.5 %copy-start = (bf16[27,64,1024]{2,1,0:T(8,128)(2,1)S(1)}, bf16[27,64,1024]{2,1,0:T(8,128)(2,1)}, u32[]{:S(2)}) copy-start(bf16[27,64,1024]{2,1,0:T(8,128)(2,1)} %param.8) | copy-start | bytes 10616836
  0.0 31.1 %collective-permute-start = (bf16[2,1,32,64]{3,2,0,1:T(8,128)(2,1)}, bf16[2,1,32,64]{3,2,0,1:T(8,128)(2,1)S(1)}, u32[]{:S(2)}, u32[]{:S(2)}) collective-permute-start(bf16[2,1,32,64]{3,2,0,1:T(8,128)(2,1)} %bitcast.67), channel_id=1, source_target_pairs={{0,8},{8,0},{1,9},{9,1},{2,10},{10,2},{3,11},{11,3},{4,12},{12,4},... | collective-permute-start | bytes 24584 | tf_op jit(solution)/shard_map/ppermute | solution.py:32
  47.8 20.8 %collective-permute-start.1 = (bf16[2,1,32,1024]{3,2,0,1:T(8,128)(2,1)}, bf16[2,1,32,1024]{3,2,0,1:T(8,128)(2,1)}, u32[]{:S(2)}, u32[]{:S(2)}) collective-permute-start(bf16[2,1,32,1024]{3,2,0,1:T(8,128)(2,1)} %reshape.104), channel_id=1, source_target_pairs={{0,32},{8,40},{16,48},{24,56},{32,64},{40,72},{48,80},{56,88},{64,... | collective-permute-start | bytes 393224 | tf_op jit(solution)/shard_map/ppermute | solution.py:22
  51.5 18.3 %collective-permute-start.2 = (bf16[2,1,32,1024]{3,2,0,1:T(8,128)(2,1)}, bf16[2,1,32,1024]{3,2,0,1:T(8,128)(2,1)S(1)}, u32[]{:S(2)}, u32[]{:S(2)}) collective-permute-start(bf16[2,1,32,1024]{3,2,0,1:T(8,128)(2,1)} %reshape.104), channel_id=1, source_target_pairs={{0,16},{8,24},{16,32},{24,40},{32,48},{40,56},{48,64},{56,72},{64,... | collective-permute-start | bytes 393224 | tf_op jit(solution)/shard_map/ppermute | solution.py:22
  54.4 16.3 %collective-permute-start.3 = (bf16[2,1,32,1024]{3,2,0,1:T(8,128)(2,1)}, bf16[2,1,32,1024]{3,2,0,1:T(8,128)(2,1)S(1)}, u32[]{:S(2)}, u32[]{:S(2)}) collective-permute-start(bf16[2,1,32,1024]{3,2,0,1:T(8,128)(2,1)} %reshape.104), channel_id=1, source_target_pairs={{16,0},{24,8},{32,16},{40,24},{48,32},{56,40},{64,48},{72,56},{80,... | collective-permute-start | bytes 393224 | tf_op jit(solution)/shard_map/ppermute | solution.py:22
  63.8 8.6 %collective-permute-start.4 = (bf16[2,1,32,1024]{3,2,0,1:T(8,128)(2,1)}, bf16[2,1,32,1024]{3,2,0,1:T(8,128)(2,1)S(1)}, u32[]{:S(2)}, u32[]{:S(2)}) collective-permute-start(bf16[2,1,32,1024]{3,2,0,1:T(8,128)(2,1)} %reshape.104), channel_id=1, source_target_pairs={{32,0},{40,8},{48,16},{56,24},{64,32},{72,40},{80,48},{88,56},{96,... | collective-permute-start | bytes 393224 | tf_op jit(solution)/shard_map/ppermute | solution.py:22
  74.4 2.0 %copy-start.3 = (bf16[27,1024,64]{1,2,0:T(8,128)(2,1)S(1)}, bf16[27,1024,64]{1,2,0:T(8,128)(2,1)}, u32[]{:S(2)}) copy-start(bf16[27,1024,64]{1,2,0:T(8,128)(2,1)} %param.6) | copy-start | bytes 10616836
  74.5 2.0 %copy-start.4 = (pred[8,5]{0,1:T(8,128)(4,1)S(1)}, pred[8,5]{0,1:T(8,128)(4,1)}, u32[]{:S(2)}) copy-start(pred[8,5]{0,1:T(8,128)(4,1)} %constant.39) | copy-start | bytes 124
  76.4 3.7 %copy-start.2 = (f32[64]{0:T(128)S(1)}, f32[64]{0:T(128)}, u32[]{:S(2)}) copy-start(f32[64]{0:T(128)} %param.7) | copy-start | bytes 772
  84.3 47.0 %copy-start.1 = (bf16[2,1,32,64]{3,2,1,0:T(8,128)(2,1)S(1)}, bf16[2,1,32,64]{3,2,1,0:T(8,128)(2,1)}, u32[]{:S(2)}) copy-start(bf16[2,1,32,64]{3,2,1,0:T(8,128)(2,1)} %param.5) | copy-start | bytes 24580
  107.1 24.1 %collective-permute-start.5 = (f32[64,64]{1,0:T(8,128)S(1)}, f32[64,64]{1,0:T(8,128)S(1)}, u32[]{:S(2)}, u32[]{:S(2)}) collective-permute-start(f32[64,64]{1,0:T(8,128)S(1)} %bitcast.69), channel_id=1, source_target_pairs={{0,8},{8,0},{1,9},{9,1},{2,10},{10,2},{3,11},{11,3},{4,12},{12,4},... | collective-permute-start | bytes 49160 | tf_op jit(solution)/shard_map/ppermute | solution.py:32

commit v7 on v6

--- a/solution.py
+++ b/solution.py
@@ -83,11 +83,14 @@
 
 def reduce_channels(partial, own_chan):
     inner_count = lax.axis_size("inner")
-    blocks = partial.reshape(partial.shape[0], HALVES, inner_count, own_chan)
-    sums = lax.all_to_all(blocks, "inner", 2, 2, tiled=True).sum(2)
+    cells = partial.shape[0]
+    blocks = partial.reshape(cells, HALVES, inner_count, own_chan).transpose(2, 0, 1, 3)
+    blocks = blocks.reshape(inner_count, cells, HALVES * own_chan)
+    sums = lax.all_to_all(blocks, "inner", 0, 0, tiled=True).sum(0)
     half = lax.axis_index("zh")
-    mine = jnp.where(half == 0, sums[:, 0], sums[:, 1])
-    theirs = jnp.where(half == 0, sums[:, 1], sums[:, 0])
+    low, high = sums[:, :own_chan], sums[:, own_chan:]
+    mine = jnp.where(half == 0, low, high)
+    theirs = jnp.where(half == 0, high, low)
     return mine + swap_halves(theirs)
 
 

time: 134 us -> 131 us (0.978)
  local copies, waits for them, and re-layouts: 18.8 us -> 15.9 us
  waiting for transfers between devices: 9.62 us -> 12.3 us
    unnamed x17 -> x15, local copies, waits for them, and re-layouts: 8.71 us -> 4.28 us
    all_to_all x1 -> x0, other arithmetic: 2.92 us -> none  [reduce_channels(): sums = lax.all_to_all(blocks, 'inner', 2, 2, tiled=True).sum(2)]
    transpose x0 -> x1, local copies, waits for them, and re-layouts: none -> 2.11 us  [reduce_channels(): partial.reshape(cells, HALVES, inner_count, own_chan).transpose(2, 0, 1, 3)]
    another operation x2 -> x1, local copies, waits for them, and re-layouts: 4 us -> 1.89 us  [reduce_channels(): partial.reshape(cells, HALVES, inner_count, own_chan).transpose(2, 0, 1, 3)]
    reshape x0 -> x1, local copies, waits for them, and re-layouts: none -> 2.03 us  [reduce_channels(): blocks = blocks.reshape(inner_count, cells, HALVES * own_chan)]
    ppermute x4, waiting for transfers between devices: 1.86 us -> 3.44 us  [row_from(): return lax.ppermute(cells, ('space', 'zh'), pairs)]
where the time goes in v7:
time: 131 us; the launch traced here: 130 us
  starting transfers between devices  67.2 us (51%)
  blocking collectives  24.7 us (19%)
  local copies, waits for them, and re-layouts  15.9 us (12%)
  waiting for transfers between devices  12.3 us (9%)
  other arithmetic  5.58 us (4%)
  matrix products  4.43 us (3%)
    ppermute x2, starting transfers between devices, swap_halves(): return lax.ppermute(v, 'zh', [(0, 1), (1, 0)])  46.4 us
    ppermute x4, starting transfers between devices, row_from(): return lax.ppermute(cells, ('space', 'zh'), pairs)  20.8 us
    all_gather x1, blocking collectives, gather_channels(): inner = lax.all_gather(pair, 'inner', axis=0, tiled=False)  13.2 us
    all_to_all x1, blocking collectives, reduce_channels(): sums = lax.all_to_all(blocks, 'inner', 0, 0, tiled=True).sum(0)  11.5 us
    ppermute x2, waiting for transfers between devices, swap_halves(): return lax.ppermute(v, 'zh', [(0, 1), (1, 0)])  8.87 us
    conv_general_dilated x2, matrix products, conv3(): lax.conv_general_dilated(padded[None], taps, (1, 1, 1), 'VALID', dimensio...  4.43 us
    unnamed x15, local copies, waits for them, and re-layouts  4.28 us
    ppermute x4, waiting for transfers between devices, row_from(): return lax.ppermute(cells, ('space', 'zh'), pairs)  3.44 us
  transfers between devices with their start and end apart: 6, of which 4 were waited for; matrix products, arithmetic and copies ran while one was open for 1% of the time, Pallas kernels for 0%

profile of v7, /device:TPU:24, one launch (start us, length us, event | category | flops | bytes accessed | tf_op | source)
XLA Modules:
  0.0 130.4 jit_solution(3576920197753405920)
XLA Ops:
  0.0 29.2 %collective-permute-start = (bf16[2,1,32,64]{3,2,0,1:T(8,128)(2,1)}, bf16[2,1,32,64]{3,2,0,1:T(8,128)(2,1)S(1)}, u32[]{:S(2)}, u32[]{:S(2)}) collective-permute-start(bf16[2,1,32,64]{3,2,0,1:T(8,128)(2,1)} %bitcast.52), channel_id=1, source_target_pairs={{0,8},{8,0},{1,9},{9,1},{2,10},{10,2},{3,11},{11,3},{4,12},{12,4},... | collective-permute-start | bytes 24584 | tf_op jit(solution)/shard_map/ppermute | solution.py:32
  29.2 1.9 %collective-permute-done = bf16[2,1,32,64]{3,2,0,1:T(8,128)(2,1)S(1)} collective-permute-done((bf16[2,1,32,64]{3,2,0,1:T(8,128)(2,1)}, bf16[2,1,32,64]{3,2,0,1:T(8,128)(2,1)S(1)}, u32[]{:S(2)}, u32[]{:S(2)}) %collective-permute-start) | collective-permute-done | bytes 8224 | tf_op jit(solution)/shard_map/ppermute | solution.py:32
  31.2 0.8 maximum_select_fusion
  32.0 13.2 %all_gather.4 = bf16[8,2,2,1,32,64]{5,4,3,2,1,0:T(8,128)(2,1)S(1)} all-gather(bf16[1,2,2,1,32,64]{5,4,3,2,1,0:T(8,128)(2,1)S(1)} %maximum_select_fusion), channel_id=1, replica_groups=mesh['space'=64,'zh'=2,'inner'=8] {'inner'}, dimensions={0}, use_global_device_ids=true | all-gather | bytes 147456 | tf_op jit(solution)/shard_map/all_gather | solution.py:78
  45.1 0.9 copy.25
  46.0 1.8 %reshape.103 = bf16[2,1,32,1024]{3,2,0,1:T(8,128)(2,1)} reshape(bf16[2,1,32,2,8,64]{5,4,3,2,0,1:T(8,128)(2,1)} %copy.25) | data formatting | bytes 262144 | tf_op jit(solution)/shard_map/reshape | solution.py:81
  47.8 3.6 %collective-permute-start.1 = (bf16[2,1,32,1024]{3,2,0,1:T(8,128)(2,1)}, bf16[2,1,32,1024]{3,2,0,1:T(8,128)(2,1)}, u32[]{:S(2)}, u32[]{:S(2)}) collective-permute-start(bf16[2,1,32,1024]{3,2,0,1:T(8,128)(2,1)} %reshape.103), channel_id=1, source_target_pairs={{0,32},{8,40},{16,48},{24,56},{32,64},{40,72},{48,80},{56,88},{64,... | collective-permute-start | bytes 393224 | tf_op jit(solution)/shard_map/ppermute | solution.py:22
  51.5 2.9 %collective-permute-start.2 = (bf16[2,1,32,1024]{3,2,0,1:T(8,128)(2,1)}, bf16[2,1,32,1024]{3,2,0,1:T(8,128)(2,1)S(1)}, u32[]{:S(2)}, u32[]{:S(2)}) collective-permute-start(bf16[2,1,32,1024]{3,2,0,1:T(8,128)(2,1)} %reshape.103), channel_id=1, source_target_pairs={{0,16},{8,24},{16,32},{24,40},{32,48},{40,56},{48,64},{56,72},{64,... | collective-permute-start | bytes 393224 | tf_op jit(solution)/shard_map/ppermute | solution.py:22
  54.4 10.8 %collective-permute-start.4 = (bf16[2,1,32,1024]{3,2,0,1:T(8,128)(2,1)}, bf16[2,1,32,1024]{3,2,0,1:T(8,128)(2,1)S(1)}, u32[]{:S(2)}, u32[]{:S(2)}) collective-permute-start(bf16[2,1,32,1024]{3,2,0,1:T(8,128)(2,1)} %reshape.103), channel_id=1, source_target_pairs={{32,0},{40,8},{48,16},{56,24},{64,32},{72,40},{80,48},{88,56},{96,... | collective-permute-start | bytes 393224 | tf_op jit(solution)/shard_map/ppermute | solution.py:22
  65.3 3.4 %collective-permute-start.3 = (bf16[2,1,32,1024]{3,2,0,1:T(8,128)(2,1)}, bf16[2,1,32,1024]{3,2,0,1:T(8,128)(2,1)S(1)}, u32[]{:S(2)}, u32[]{:S(2)}) collective-permute-start(bf16[2,1,32,1024]{3,2,0,1:T(8,128)(2,1)} %reshape.103), channel_id=1, source_target_pairs={{16,0},{24,8},{32,16},{40,24},{48,32},{56,40},{64,48},{72,56},{80,... | collective-permute-start | bytes 393224 | tf_op jit(solution)/shard_map/ppermute | solution.py:22
  68.7 0.9 constant_dynamic-update-slice_fusion.4
  69.8 0.9 constant_dynamic-update-slice_fusion.2
  70.7 3.2 %collective-permute-done.3 = bf16[2,1,32,1024]{3,2,0,1:T(8,128)(2,1)S(1)} collective-permute-done((bf16[2,1,32,1024]{3,2,0,1:T(8,128)(2,1)}, bf16[2,1,32,1024]{3,2,0,1:T(8,128)(2,1)S(1)}, u32[]{:S(2)}, u32[]{:S(2)}) %collective-permute-start.3) | collective-permute-done | bytes 131104 | tf_op jit(solution)/shard_map/ppermute | solution.py:22
  74.0 0.3 pad_bitcast_fusion
  74.3 1.1 copy.35
  75.3 0.7 pad.10.clone
  76.0 0.5 copy.28
  76.7 1.3 %copy-done.3 = bf16[27,1024,64]{1,2,0:T(8,128)(2,1)S(1)} copy-done((bf16[27,1024,64]{1,2,0:T(8,128)(2,1)S(1)}, bf16[27,1024,64]{1,2,0:T(8,128)(2,1)}, u32[]{:S(2)}) %copy-start.3) | copy-done | bytes 3538968
  78.0 3.7 %fusion.9 = f32[2,3,8,5,64]{4,2,3,1,0:T(8,128)S(1)} fusion(bf16[3,3,3,1024,64]{3,4,2,1,0:T(8,128)(2,1)S(1)} %bitcast.55, bf16[4,5,1,7,2,1024]{5,3,4,1,0,2:T(8,128)(2,1)S(1)} %slice.12, bf16[4,5,1,8,5,1024]{5,3,4,1,0,2:T(8,128)(2,1)S(1)} %copy.28, pred[8,5]{0,1:T(8,128)(4,1)S(1)} %copy-done.4), kind=kOutput, calls=%fused_computation.11 | convolution fusion | flops 856243200 | bytes 5812264 | tf_op jit(solution)/shard_map/conv_general_dilated | solution.py:63
  82.1 0.8 convolution_select_fusion
  82.9 0.3 copy.32
  83.2 0.8 copy.33
  84.0 1.9 %reshape_reshape_squeeze.3 = f32[64,2,8,64]{3,2,1,0:T(8,128)} reshape(f32[2,1,1,32,1024]{4,3,0,2,1:T(8,128)} %copy.33) | data formatting | bytes 524288 | tf_op jit(solution)/shard_map/reshape;reshape;squeeze | solution.py:87
  85.9 2.1 %copy.34 = f32[8,64,2,64]{3,2,1,0:T(2,128)} copy(f32[8,64,2,64]{3,0,2,1:T(8,128)} %bitcast.46) | data formatting | bytes 524288 | tf_op jit(solution)/shard_map/transpose | solution.py:87
  88.0 2.0 %reshape.106 = f32[8,64,128]{2,1,0:T(8,128)} reshape(f32[8,64,2,64]{3,2,1,0:T(2,128)} %copy.34) | data formatting | bytes 524288 | tf_op jit(solution)/shard_map/reshape | solution.py:88
  90.0 11.5 %all_to_all.5 = f32[8,64,128]{2,1,0:T(8,128)} all-to-all(f32[8,64,128]{2,1,0:T(8,128)} %reshape.106), channel_id=1, replica_groups=mesh['space'=64,'zh'=2,'inner'=8] {'inner'}, dimensions={0} | all-to-all | bytes 524288 | tf_op jit(solution)/shard_map/all_to_all | solution.py:89
  101.6 1.6 %reduce_sum.9 = f32[64,128]{1,0:T(8,128)} reduce(f32[8,64,128]{2,1,0:T(8,128)} %all_to_all.5, f32[]{:T(128)} %constant.25.clone.1), dimensions={0}, to_apply=%region_0.1 | reduce | flops 57344 | bytes 294916 | tf_op jit(solution)/shard_map/reduce_sum | solution.py:89
  103.1 0.9 slice_select_fusion
  104.0 17.2 %collective-permute-start.5 = (f32[64,64]{1,0:T(8,128)S(1)}, f32[64,64]{1,0:T(8,128)S(1)}, u32[]{:S(2)}, u32[]{:S(2)}) collective-permute-start(f32[64,64]{1,0:T(8,128)S(1)} %slice_select_fusion), channel_id=1, source_target_pairs={{0,8},{8,0},{1,9},{9,1},{2,10},{10,2},{3,11},{11,3},{4,12},{12,4},... | collective-permute-start | bytes 49160 | tf_op jit(solution)/shard_map/ppermute | solution.py:32
  121.2 7.0 %collective-permute-done.5 = f32[64,64]{1,0:T(8,128)S(1)} collective-permute-done((f32[64,64]{1,0:T(8,128)S(1)}, f32[64,64]{1,0:T(8,128)S(1)}, u32[]{:S(2)}, u32[]{:S(2)}) %collective-permute-start.5) | collective-permute-done | bytes 16416 | tf_op jit(solution)/shard_map/ppermute | solution.py:32
  128.2 0.9 select_add_fusion
  129.1 1.3 add_convert_fusion
  (24 shorter events, 0.8 us)
Async XLA Ops:
  0.0 82.1 %copy-start = (bf16[27,64,1024]{2,1,0:T(8,128)(2,1)S(1)}, bf16[27,64,1024]{2,1,0:T(8,128)(2,1)}, u32[]{:S(2)}) copy-start(bf16[27,64,1024]{2,1,0:T(8,128)(2,1)} %param.8) | copy-start | bytes 10616836
  0.0 31.1 %collective-permute-start = (bf16[2,1,32,64]{3,2,0,1:T(8,128)(2,1)}, bf16[2,1,32,64]{3,2,0,1:T(8,128)(2,1)S(1)}, u32[]{:S(2)}, u32[]{:S(2)}) collective-permute-start(bf16[2,1,32,64]{3,2,0,1:T(8,128)(2,1)} %bitcast.52), channel_id=1, source_target_pairs={{0,8},{8,0},{1,9},{9,1},{2,10},{10,2},{3,11},{11,3},{4,12},{12,4},... | collective-permute-start | bytes 24584 | tf_op jit(solution)/shard_map/ppermute | solution.py:32
  47.8 20.8 %collective-permute-start.1 = (bf16[2,1,32,1024]{3,2,0,1:T(8,128)(2,1)}, bf16[2,1,32,1024]{3,2,0,1:T(8,128)(2,1)}, u32[]{:S(2)}, u32[]{:S(2)}) collective-permute-start(bf16[2,1,32,1024]{3,2,0,1:T(8,128)(2,1)} %reshape.103), channel_id=1, source_target_pairs={{0,32},{8,40},{16,48},{24,56},{32,64},{40,72},{48,80},{56,88},{64,... | collective-permute-start | bytes 393224 | tf_op jit(solution)/shard_map/ppermute | solution.py:22
  51.5 18.3 %collective-permute-start.2 = (bf16[2,1,32,1024]{3,2,0,1:T(8,128)(2,1)}, bf16[2,1,32,1024]{3,2,0,1:T(8,128)(2,1)S(1)}, u32[]{:S(2)}, u32[]{:S(2)}) collective-permute-start(bf16[2,1,32,1024]{3,2,0,1:T(8,128)(2,1)} %reshape.103), channel_id=1, source_target_pairs={{0,16},{8,24},{16,32},{24,40},{32,48},{40,56},{48,64},{56,72},{64,... | collective-permute-start | bytes 393224 | tf_op jit(solution)/shard_map/ppermute | solution.py:22
  54.4 19.5 %collective-permute-start.4 = (bf16[2,1,32,1024]{3,2,0,1:T(8,128)(2,1)}, bf16[2,1,32,1024]{3,2,0,1:T(8,128)(2,1)S(1)}, u32[]{:S(2)}, u32[]{:S(2)}) collective-permute-start(bf16[2,1,32,1024]{3,2,0,1:T(8,128)(2,1)} %reshape.103), channel_id=1, source_target_pairs={{32,0},{40,8},{48,16},{56,24},{64,32},{72,40},{80,48},{88,56},{96,... | collective-permute-start | bytes 393224 | tf_op jit(solution)/shard_map/ppermute | solution.py:22
  65.3 8.7 %collective-permute-start.3 = (bf16[2,1,32,1024]{3,2,0,1:T(8,128)(2,1)}, bf16[2,1,32,1024]{3,2,0,1:T(8,128)(2,1)S(1)}, u32[]{:S(2)}, u32[]{:S(2)}) collective-permute-start(bf16[2,1,32,1024]{3,2,0,1:T(8,128)(2,1)} %reshape.103), channel_id=1, source_target_pairs={{16,0},{24,8},{32,16},{40,24},{48,32},{56,40},{64,48},{72,56},{80,... | collective-permute-start | bytes 393224 | tf_op jit(solution)/shard_map/ppermute | solution.py:22
  76.0 2.0 %copy-start.3 = (bf16[27,1024,64]{1,2,0:T(8,128)(2,1)S(1)}, bf16[27,1024,64]{1,2,0:T(8,128)(2,1)}, u32[]{:S(2)}) copy-start(bf16[27,1024,64]{1,2,0:T(8,128)(2,1)} %param.6) | copy-start | bytes 10616836
  76.0 2.0 %copy-start.4 = (pred[8,5]{0,1:T(8,128)(4,1)S(1)}, pred[8,5]{0,1:T(8,128)(4,1)}, u32[]{:S(2)}) copy-start(pred[8,5]{0,1:T(8,128)(4,1)} %constant.39) | copy-start | bytes 124
  78.0 3.7 %copy-start.2 = (f32[64]{0:T(128)S(1)}, f32[64]{0:T(128)}, u32[]{:S(2)}) copy-start(f32[64]{0:T(128)} %param.7) | copy-start | bytes 772
  83.1 45.9 %copy-start.1 = (bf16[2,1,32,64]{3,2,1,0:T(8,128)(2,1)S(1)}, bf16[2,1,32,64]{3,2,1,0:T(8,128)(2,1)}, u32[]{:S(2)}) copy-start(bf16[2,1,32,64]{3,2,1,0:T(8,128)(2,1)} %param.5) | copy-start | bytes 24580
  104.0 24.1 %collective-permute-start.5 = (f32[64,64]{1,0:T(8,128)S(1)}, f32[64,64]{1,0:T(8,128)S(1)}, u32[]{:S(2)}, u32[]{:S(2)}) collective-permute-start(f32[64,64]{1,0:T(8,128)S(1)} %slice_select_fusion), channel_id=1, source_target_pairs={{0,8},{8,0},{1,9},{9,1},{2,10},{10,2},{3,11},{11,3},{4,12},{12,4},... | collective-permute-start | bytes 49160 | tf_op jit(solution)/shard_map/ppermute | solution.py:32

commit v8 on v7

--- a/solution.py
+++ b/solution.py
@@ -91,7 +91,7 @@
     low, high = sums[:, :own_chan], sums[:, own_chan:]
     mine = jnp.where(half == 0, low, high)
     theirs = jnp.where(half == 0, high, low)
-    return mine + swap_halves(theirs)
+    return mine + swap_halves(theirs.astype(jnp.bfloat16)).astype(jnp.float32)
 
 
 def local(latent, conv_one, bias_one, conv_two, bias_two):

time: 131 us -> 131 us (level)
  no operation moved by 1% of the time
where the time goes in v8:
time: 131 us; the launch traced here: 130 us
  starting transfers between devices  67.2 us (51%)
  blocking collectives  24.7 us (19%)
  local copies, waits for them, and re-layouts  15.9 us (12%)
  waiting for transfers between devices  12.1 us (9%)
  other arithmetic  5.59 us (4%)
  matrix products  4.43 us (3%)
    ppermute x2, starting transfers between devices, swap_halves(): return lax.ppermute(v, 'zh', [(0, 1), (1, 0)])  46.4 us
    ppermute x4, starting transfers between devices, row_from(): return lax.ppermute(cells, ('space', 'zh'), pairs)  20.8 us
    all_gather x1, blocking collectives, gather_channels(): inner = lax.all_gather(pair, 'inner', axis=0, tiled=False)  13.2 us
    all_to_all x1, blocking collectives, reduce_channels(): sums = lax.all_to_all(blocks, 'inner', 0, 0, tiled=True).sum(0)  11.5 us
    ppermute x2, waiting for transfers between devices, swap_halves(): return lax.ppermute(v, 'zh', [(0, 1), (1, 0)])  8.69 us
    conv_general_dilated x2, matrix products, conv3(): lax.conv_general_dilated(padded[None], taps, (1, 1, 1), 'VALID', dimensio...  4.43 us
    unnamed x15, local copies, waits for them, and re-layouts  4.28 us
    ppermute x4, waiting for transfers between devices, row_from(): return lax.ppermute(cells, ('space', 'zh'), pairs)  3.44 us
  transfers between devices with their start and end apart: 6, of which 4 were waited for; matrix products, arithmetic and copies ran while one was open for 1% of the time, Pallas kernels for 0%

profile of v8, /device:TPU:24, one launch (start us, length us, event | category | flops | bytes accessed | tf_op | source)
XLA Modules:
  0.0 130.2 jit_solution(11532873929148385665)
XLA Ops:
  0.0 29.2 %collective-permute-start = (bf16[2,1,32,64]{3,2,0,1:T(8,128)(2,1)}, bf16[2,1,32,64]{3,2,0,1:T(8,128)(2,1)S(1)}, u32[]{:S(2)}, u32[]{:S(2)}) collective-permute-start(bf16[2,1,32,64]{3,2,0,1:T(8,128)(2,1)} %bitcast.52), channel_id=1, source_target_pairs={{0,8},{8,0},{1,9},{9,1},{2,10},{10,2},{3,11},{11,3},{4,12},{12,4},... | collective-permute-start | bytes 24584 | tf_op jit(solution)/shard_map/ppermute | solution.py:32
  29.2 1.9 %collective-permute-done = bf16[2,1,32,64]{3,2,0,1:T(8,128)(2,1)S(1)} collective-permute-done((bf16[2,1,32,64]{3,2,0,1:T(8,128)(2,1)}, bf16[2,1,32,64]{3,2,0,1:T(8,128)(2,1)S(1)}, u32[]{:S(2)}, u32[]{:S(2)}) %collective-permute-start) | collective-permute-done | bytes 8224 | tf_op jit(solution)/shard_map/ppermute | solution.py:32
  31.2 0.8 maximum_select_fusion
  32.0 13.2 %all_gather.4 = bf16[8,2,2,1,32,64]{5,4,3,2,1,0:T(8,128)(2,1)S(1)} all-gather(bf16[1,2,2,1,32,64]{5,4,3,2,1,0:T(8,128)(2,1)S(1)} %maximum_select_fusion), channel_id=1, replica_groups=mesh['space'=64,'zh'=2,'inner'=8] {'inner'}, dimensions={0}, use_global_device_ids=true | all-gather | bytes 147456 | tf_op jit(solution)/shard_map/all_gather | solution.py:78
  45.1 0.9 copy.25
  46.0 1.8 %reshape.103 = bf16[2,1,32,1024]{3,2,0,1:T(8,128)(2,1)} reshape(bf16[2,1,32,2,8,64]{5,4,3,2,0,1:T(8,128)(2,1)} %copy.25) | data formatting | bytes 262144 | tf_op jit(solution)/shard_map/reshape | solution.py:81
  47.8 3.6 %collective-permute-start.1 = (bf16[2,1,32,1024]{3,2,0,1:T(8,128)(2,1)}, bf16[2,1,32,1024]{3,2,0,1:T(8,128)(2,1)}, u32[]{:S(2)}, u32[]{:S(2)}) collective-permute-start(bf16[2,1,32,1024]{3,2,0,1:T(8,128)(2,1)} %reshape.103), channel_id=1, source_target_pairs={{0,32},{8,40},{16,48},{24,56},{32,64},{40,72},{48,80},{56,88},{64,... | collective-permute-start | bytes 393224 | tf_op jit(solution)/shard_map/ppermute | solution.py:22
  51.5 2.9 %collective-permute-start.2 = (bf16[2,1,32,1024]{3,2,0,1:T(8,128)(2,1)}, bf16[2,1,32,1024]{3,2,0,1:T(8,128)(2,1)S(1)}, u32[]{:S(2)}, u32[]{:S(2)}) collective-permute-start(bf16[2,1,32,1024]{3,2,0,1:T(8,128)(2,1)} %reshape.103), channel_id=1, source_target_pairs={{0,16},{8,24},{16,32},{24,40},{32,48},{40,56},{48,64},{56,72},{64,... | collective-permute-start | bytes 393224 | tf_op jit(solution)/shard_map/ppermute | solution.py:22
  54.4 10.8 %collective-permute-start.4 = (bf16[2,1,32,1024]{3,2,0,1:T(8,128)(2,1)}, bf16[2,1,32,1024]{3,2,0,1:T(8,128)(2,1)S(1)}, u32[]{:S(2)}, u32[]{:S(2)}) collective-permute-start(bf16[2,1,32,1024]{3,2,0,1:T(8,128)(2,1)} %reshape.103), channel_id=1, source_target_pairs={{32,0},{40,8},{48,16},{56,24},{64,32},{72,40},{80,48},{88,56},{96,... | collective-permute-start | bytes 393224 | tf_op jit(solution)/shard_map/ppermute | solution.py:22
  65.3 3.4 %collective-permute-start.3 = (bf16[2,1,32,1024]{3,2,0,1:T(8,128)(2,1)}, bf16[2,1,32,1024]{3,2,0,1:T(8,128)(2,1)S(1)}, u32[]{:S(2)}, u32[]{:S(2)}) collective-permute-start(bf16[2,1,32,1024]{3,2,0,1:T(8,128)(2,1)} %reshape.103), channel_id=1, source_target_pairs={{16,0},{24,8},{32,16},{40,24},{48,32},{56,40},{64,48},{72,56},{80,... | collective-permute-start | bytes 393224 | tf_op jit(solution)/shard_map/ppermute | solution.py:22
  68.7 0.9 constant_dynamic-update-slice_fusion.4
  69.8 0.9 constant_dynamic-update-slice_fusion.2
  70.7 3.2 %collective-permute-done.3 = bf16[2,1,32,1024]{3,2,0,1:T(8,128)(2,1)S(1)} collective-permute-done((bf16[2,1,32,1024]{3,2,0,1:T(8,128)(2,1)}, bf16[2,1,32,1024]{3,2,0,1:T(8,128)(2,1)S(1)}, u32[]{:S(2)}, u32[]{:S(2)}) %collective-permute-start.3) | collective-permute-done | bytes 131104 | tf_op jit(solution)/shard_map/ppermute | solution.py:22
  74.0 0.3 pad_bitcast_fusion
  74.3 1.1 copy.35
  75.3 0.7 pad.10.clone
  76.0 0.5 copy.28
  76.7 1.3 %copy-done.3 = bf16[27,1024,64]{1,2,0:T(8,128)(2,1)S(1)} copy-done((bf16[27,1024,64]{1,2,0:T(8,128)(2,1)S(1)}, bf16[27,1024,64]{1,2,0:T(8,128)(2,1)}, u32[]{:S(2)}) %copy-start.3) | copy-done | bytes 3538968
  78.0 3.7 %fusion.9 = f32[2,3,8,5,64]{4,2,3,1,0:T(8,128)S(1)} fusion(bf16[3,3,3,1024,64]{3,4,2,1,0:T(8,128)(2,1)S(1)} %bitcast.55, bf16[4,5,1,7,2,1024]{5,3,4,1,0,2:T(8,128)(2,1)S(1)} %slice.12, bf16[4,5,1,8,5,1024]{5,3,4,1,0,2:T(8,128)(2,1)S(1)} %copy.28, pred[8,5]{0,1:T(8,128)(4,1)S(1)} %copy-done.4), kind=kOutput, calls=%fused_computation.11 | convolution fusion | flops 856243200 | bytes 5812264 | tf_op jit(solution)/shard_map/conv_general_dilated | solution.py:63
  82.1 0.8 convolution_select_fusion
  82.9 0.3 copy.32
  83.2 0.8 copy.33
  84.0 1.9 %reshape_reshape_squeeze.3 = f32[64,2,8,64]{3,2,1,0:T(8,128)} reshape(f32[2,1,1,32,1024]{4,3,0,2,1:T(8,128)} %copy.33) | data formatting | bytes 524288 | tf_op jit(solution)/shard_map/reshape;reshape;squeeze | solution.py:87
  85.9 2.1 %copy.34 = f32[8,64,2,64]{3,2,1,0:T(2,128)} copy(f32[8,64,2,64]{3,0,2,1:T(8,128)} %bitcast.46) | data formatting | bytes 524288 | tf_op jit(solution)/shard_map/transpose | solution.py:87
  88.0 2.0 %reshape.106 = f32[8,64,128]{2,1,0:T(8,128)} reshape(f32[8,64,2,64]{3,2,1,0:T(2,128)} %copy.34) | data formatting | bytes 524288 | tf_op jit(solution)/shard_map/reshape | solution.py:88
  90.0 11.5 %all_to_all.5 = f32[8,64,128]{2,1,0:T(8,128)} all-to-all(f32[8,64,128]{2,1,0:T(8,128)} %reshape.106), channel_id=1, replica_groups=mesh['space'=64,'zh'=2,'inner'=8] {'inner'}, dimensions={0} | all-to-all | bytes 524288 | tf_op jit(solution)/shard_map/all_to_all | solution.py:89
  101.6 1.6 %reduce_sum.9 = f32[64,128]{1,0:T(8,128)} reduce(f32[8,64,128]{2,1,0:T(8,128)} %all_to_all.5, f32[]{:T(128)} %constant.25.clone.1), dimensions={0}, to_apply=%region_0.1 | reduce | flops 57344 | bytes 294916 | tf_op jit(solution)/shard_map/reduce_sum | solution.py:89
  103.1 0.9 select_convert_fusion
  104.0 17.2 %collective-permute-start.5 = (bf16[64,64]{1,0:T(8,128)(2,1)S(1)}, bf16[64,64]{1,0:T(8,128)(2,1)S(1)}, u32[]{:S(2)}, u32[]{:S(2)}) collective-permute-start(bf16[64,64]{1,0:T(8,128)(2,1)S(1)} %select_convert_fusion), channel_id=1, source_target_pairs={{0,8},{8,0},{1,9},{9,1},{2,10},{10,2},{3,11},{11,3},{4,12},{12,4},... | collective-permute-start | bytes 24584 | tf_op jit(solution)/shard_map/ppermute | solution.py:32
  121.2 6.8 %collective-permute-done.5 = bf16[64,64]{1,0:T(8,128)(2,1)S(1)} collective-permute-done((bf16[64,64]{1,0:T(8,128)(2,1)S(1)}, bf16[64,64]{1,0:T(8,128)(2,1)S(1)}, u32[]{:S(2)}, u32[]{:S(2)}) %collective-permute-start.5) | collective-permute-done | bytes 8224 | tf_op jit(solution)/shard_map/ppermute | solution.py:32
  128.0 0.9 convert_add_fusion
  128.9 1.3 add_convert_fusion
  (24 shorter events, 0.8 us)
Async XLA Ops:
  0.0 82.1 %copy-start = (bf16[27,64,1024]{2,1,0:T(8,128)(2,1)S(1)}, bf16[27,64,1024]{2,1,0:T(8,128)(2,1)}, u32[]{:S(2)}) copy-start(bf16[27,64,1024]{2,1,0:T(8,128)(2,1)} %param.8) | copy-start | bytes 10616836
  0.0 31.1 %collective-permute-start = (bf16[2,1,32,64]{3,2,0,1:T(8,128)(2,1)}, bf16[2,1,32,64]{3,2,0,1:T(8,128)(2,1)S(1)}, u32[]{:S(2)}, u32[]{:S(2)}) collective-permute-start(bf16[2,1,32,64]{3,2,0,1:T(8,128)(2,1)} %bitcast.52), channel_id=1, source_target_pairs={{0,8},{8,0},{1,9},{9,1},{2,10},{10,2},{3,11},{11,3},{4,12},{12,4},... | collective-permute-start | bytes 24584 | tf_op jit(solution)/shard_map/ppermute | solution.py:32
  47.8 20.8 %collective-permute-start.1 = (bf16[2,1,32,1024]{3,2,0,1:T(8,128)(2,1)}, bf16[2,1,32,1024]{3,2,0,1:T(8,128)(2,1)}, u32[]{:S(2)}, u32[]{:S(2)}) collective-permute-start(bf16[2,1,32,1024]{3,2,0,1:T(8,128)(2,1)} %reshape.103), channel_id=1, source_target_pairs={{0,32},{8,40},{16,48},{24,56},{32,64},{40,72},{48,80},{56,88},{64,... | collective-permute-start | bytes 393224 | tf_op jit(solution)/shard_map/ppermute | solution.py:22
  51.5 18.3 %collective-permute-start.2 = (bf16[2,1,32,1024]{3,2,0,1:T(8,128)(2,1)}, bf16[2,1,32,1024]{3,2,0,1:T(8,128)(2,1)S(1)}, u32[]{:S(2)}, u32[]{:S(2)}) collective-permute-start(bf16[2,1,32,1024]{3,2,0,1:T(8,128)(2,1)} %reshape.103), channel_id=1, source_target_pairs={{0,16},{8,24},{16,32},{24,40},{32,48},{40,56},{48,64},{56,72},{64,... | collective-permute-start | bytes 393224 | tf_op jit(solution)/shard_map/ppermute | solution.py:22
  54.4 19.5 %collective-permute-start.4 = (bf16[2,1,32,1024]{3,2,0,1:T(8,128)(2,1)}, bf16[2,1,32,1024]{3,2,0,1:T(8,128)(2,1)S(1)}, u32[]{:S(2)}, u32[]{:S(2)}) collective-permute-start(bf16[2,1,32,1024]{3,2,0,1:T(8,128)(2,1)} %reshape.103), channel_id=1, source_target_pairs={{32,0},{40,8},{48,16},{56,24},{64,32},{72,40},{80,48},{88,56},{96,... | collective-permute-start | bytes 393224 | tf_op jit(solution)/shard_map/ppermute | solution.py:22
  65.3 8.7 %collective-permute-start.3 = (bf16[2,1,32,1024]{3,2,0,1:T(8,128)(2,1)}, bf16[2,1,32,1024]{3,2,0,1:T(8,128)(2,1)S(1)}, u32[]{:S(2)}, u32[]{:S(2)}) collective-permute-start(bf16[2,1,32,1024]{3,2,0,1:T(8,128)(2,1)} %reshape.103), channel_id=1, source_target_pairs={{16,0},{24,8},{32,16},{40,24},{48,32},{56,40},{64,48},{72,56},{80,... | collective-permute-start | bytes 393224 | tf_op jit(solution)/shard_map/ppermute | solution.py:22
  76.0 2.0 %copy-start.3 = (bf16[27,1024,64]{1,2,0:T(8,128)(2,1)S(1)}, bf16[27,1024,64]{1,2,0:T(8,128)(2,1)}, u32[]{:S(2)}) copy-start(bf16[27,1024,64]{1,2,0:T(8,128)(2,1)} %param.6) | copy-start | bytes 10616836
  76.0 2.0 %copy-start.4 = (pred[8,5]{0,1:T(8,128)(4,1)S(1)}, pred[8,5]{0,1:T(8,128)(4,1)}, u32[]{:S(2)}) copy-start(pred[8,5]{0,1:T(8,128)(4,1)} %constant.39) | copy-start | bytes 124
  78.0 3.7 %copy-start.2 = (f32[64]{0:T(128)S(1)}, f32[64]{0:T(128)}, u32[]{:S(2)}) copy-start(f32[64]{0:T(128)} %param.7) | copy-start | bytes 772
  83.1 45.8 %copy-start.1 = (bf16[2,1,32,64]{3,2,1,0:T(8,128)(2,1)S(1)}, bf16[2,1,32,64]{3,2,1,0:T(8,128)(2,1)}, u32[]{:S(2)}) copy-start(bf16[2,1,32,64]{3,2,1,0:T(8,128)(2,1)} %param.5) | copy-start | bytes 24580
  104.0 23.9 %collective-permute-start.5 = (bf16[64,64]{1,0:T(8,128)(2,1)S(1)}, bf16[64,64]{1,0:T(8,128)(2,1)S(1)}, u32[]{:S(2)}, u32[]{:S(2)}) collective-permute-start(bf16[64,64]{1,0:T(8,128)(2,1)S(1)} %select_convert_fusion), channel_id=1, source_target_pairs={{0,8},{8,0},{1,9},{9,1},{2,10},{10,2},{3,11},{11,3},{4,12},{12,4},... | collective-permute-start | bytes 24584 | tf_op jit(solution)/shard_map/ppermute | solution.py:32

commit v9 on v7

--- a/solution.py
+++ b/solution.py
@@ -64,7 +64,7 @@
         padded[None],
         taps,
         (1, 1, 1),
-        "VALID",
+        ((1, 1), (0, 0), (1, 1)),
         dimension_numbers=("NDHWC", "DHWIO", "NDHWC"),
         preferred_element_type=jnp.float32,
     )
@@ -98,12 +98,12 @@
     frame_count, row_count, col_count, own_chan = latent.shape
     gathered = gather_channels(latent)
     extended = halo_rows(gathered, 2)
-    first = conv3(pad_sides(extended), conv_one)
+    first = conv3(extended, conv_one)
     hidden = jax.nn.relu(first + bias_one).astype(jnp.bfloat16)
     row = lax.axis_index("space") * row_count + jnp.arange(-1, row_count + 1)
     inside = (row >= 0) & (row < lax.axis_size("space") * row_count)
     hidden_ext = jnp.where(inside[None, :, None, None], hidden, jnp.zeros_like(hidden))
-    partial = conv3(pad_sides(hidden_ext), conv_two)
+    partial = conv3(hidden_ext, conv_two)
     partial = partial.reshape(frame_count * row_count * col_count, -1)
     mine = reduce_channels(partial, own_chan)
     second = mine.reshape(frame_count, row_count, col_count, own_chan)

time: 131 us -> 128 us (0.977)
  waiting for transfers between devices: 12.3 us -> 9.62 us
  local copies, waits for them, and re-layouts: 15.9 us -> 13.6 us
    ppermute x4, waiting for transfers between devices: 3.44 us -> 1.86 us  [row_from(): return lax.ppermute(cells, ('space', 'zh'), pairs)]
    unnamed x15, local copies, waits for them, and re-layouts: 4.28 us -> 2.94 us
where the time goes in v9:
time: 128 us; the launch traced here: 126 us
  starting transfers between devices  68.3 us (53%)
  blocking collectives  24.7 us (19%)
  local copies, waits for them, and re-layouts  13.6 us (11%)
  waiting for transfers between devices  9.62 us (8%)
  other arithmetic  5.48 us (4%)
  matrix products  4.38 us (3%)
    ppermute x2, starting transfers between devices, swap_halves(): return lax.ppermute(v, 'zh', [(0, 1), (1, 0)])  47.5 us
    ppermute x4, starting transfers between devices, row_from(): return lax.ppermute(cells, ('space', 'zh'), pairs)  20.8 us
    all_gather x1, blocking collectives, gather_channels(): inner = lax.all_gather(pair, 'inner', axis=0, tiled=False)  13.2 us
    all_to_all x1, blocking collectives, reduce_channels(): sums = lax.all_to_all(blocks, 'inner', 0, 0, tiled=True).sum(0)  11.5 us
    ppermute x2, waiting for transfers between devices, swap_halves(): return lax.ppermute(v, 'zh', [(0, 1), (1, 0)])  7.77 us
    conv_general_dilated x2, matrix products, conv3(): lax.conv_general_dilated(padded[None], taps, (1, 1, 1), ((1, 1), (0, 0),...  4.38 us
    unnamed x15, local copies, waits for them, and re-layouts  2.94 us
  transfers between devices with their start and end apart: 6, of which 4 were waited for; matrix products, arithmetic and copies ran while one was open for 1% of the time, Pallas kernels for 0%

profile of v9, /device:TPU:24, one launch (start us, length us, event | category | flops | bytes accessed | tf_op | source)
XLA Modules:
  0.0 126.3 jit_solution(7362377233161356405)
XLA Ops:
  0.0 29.2 %collective-permute-start = (bf16[2,1,32,64]{3,2,0,1:T(8,128)(2,1)}, bf16[2,1,32,64]{3,2,0,1:T(8,128)(2,1)S(1)}, u32[]{:S(2)}, u32[]{:S(2)}) collective-permute-start(bf16[2,1,32,64]{3,2,0,1:T(8,128)(2,1)} %bitcast.50), channel_id=1, source_target_pairs={{0,8},{8,0},{1,9},{9,1},{2,10},{10,2},{3,11},{11,3},{4,12},{12,4},... | collective-permute-start | bytes 24584 | tf_op jit(solution)/shard_map/ppermute | solution.py:32
  29.2 1.9 %collective-permute-done = bf16[2,1,32,64]{3,2,0,1:T(8,128)(2,1)S(1)} collective-permute-done((bf16[2,1,32,64]{3,2,0,1:T(8,128)(2,1)}, bf16[2,1,32,64]{3,2,0,1:T(8,128)(2,1)S(1)}, u32[]{:S(2)}, u32[]{:S(2)}) %collective-permute-start) | collective-permute-done | bytes 8224 | tf_op jit(solution)/shard_map/ppermute | solution.py:32
  31.2 0.8 maximum_select_fusion
  32.0 13.2 %all_gather.4 = bf16[8,2,2,1,32,64]{5,4,3,2,1,0:T(8,128)(2,1)S(1)} all-gather(bf16[1,2,2,1,32,64]{5,4,3,2,1,0:T(8,128)(2,1)S(1)} %maximum_select_fusion), channel_id=1, replica_groups=mesh['space'=64,'zh'=2,'inner'=8] {'inner'}, dimensions={0}, use_global_device_ids=true | all-gather | bytes 147456 | tf_op jit(solution)/shard_map/all_gather | solution.py:78
  45.1 0.9 copy.19
  46.0 1.8 %reshape.103 = bf16[2,1,32,1024]{3,2,0,1:T(8,128)(2,1)} reshape(bf16[2,1,32,2,8,64]{5,4,3,2,0,1:T(8,128)(2,1)} %copy.19) | data formatting | bytes 262144 | tf_op jit(solution)/shard_map/reshape | solution.py:81
  47.8 3.6 %collective-permute-start.1 = (bf16[2,1,32,1024]{3,2,0,1:T(8,128)(2,1)}, bf16[2,1,32,1024]{3,2,0,1:T(8,128)(2,1)}, u32[]{:S(2)}, u32[]{:S(2)}) collective-permute-start(bf16[2,1,32,1024]{3,2,0,1:T(8,128)(2,1)} %reshape.103), channel_id=1, source_target_pairs={{0,32},{8,40},{16,48},{24,56},{32,64},{40,72},{48,80},{56,88},{64,... | collective-permute-start | bytes 393224 | tf_op jit(solution)/shard_map/ppermute | solution.py:22
  51.5 2.9 %collective-permute-start.2 = (bf16[2,1,32,1024]{3,2,0,1:T(8,128)(2,1)}, bf16[2,1,32,1024]{3,2,0,1:T(8,128)(2,1)S(1)}, u32[]{:S(2)}, u32[]{:S(2)}) collective-permute-start(bf16[2,1,32,1024]{3,2,0,1:T(8,128)(2,1)} %reshape.103), channel_id=1, source_target_pairs={{0,16},{8,24},{16,32},{24,40},{32,48},{40,56},{48,64},{56,72},{64,... | collective-permute-start | bytes 393224 | tf_op jit(solution)/shard_map/ppermute | solution.py:22
  54.4 9.4 %collective-permute-start.3 = (bf16[2,1,32,1024]{3,2,0,1:T(8,128)(2,1)}, bf16[2,1,32,1024]{3,2,0,1:T(8,128)(2,1)S(1)}, u32[]{:S(2)}, u32[]{:S(2)}) collective-permute-start(bf16[2,1,32,1024]{3,2,0,1:T(8,128)(2,1)} %reshape.103), channel_id=1, source_target_pairs={{16,0},{24,8},{32,16},{40,24},{48,32},{56,40},{64,48},{72,56},{80,... | collective-permute-start | bytes 393224 | tf_op jit(solution)/shard_map/ppermute | solution.py:22
  63.8 4.8 %collective-permute-start.4 = (bf16[2,1,32,1024]{3,2,0,1:T(8,128)(2,1)}, bf16[2,1,32,1024]{3,2,0,1:T(8,128)(2,1)S(1)}, u32[]{:S(2)}, u32[]{:S(2)}) collective-permute-start(bf16[2,1,32,1024]{3,2,0,1:T(8,128)(2,1)} %reshape.103), channel_id=1, source_target_pairs={{32,0},{40,8},{48,16},{56,24},{64,32},{72,40},{80,48},{88,56},{96,... | collective-permute-start | bytes 393224 | tf_op jit(solution)/shard_map/ppermute | solution.py:22
  68.7 0.9 constant_dynamic-update-slice_fusion.4
  69.6 0.2 collective-permute-done.2
  69.8 0.9 constant_dynamic-update-slice_fusion.2
  70.7 1.7 %collective-permute-done.4 = bf16[2,1,32,1024]{3,2,0,1:T(8,128)(2,1)S(1)} collective-permute-done((bf16[2,1,32,1024]{3,2,0,1:T(8,128)(2,1)}, bf16[2,1,32,1024]{3,2,0,1:T(8,128)(2,1)S(1)}, u32[]{:S(2)}, u32[]{:S(2)}) %collective-permute-start.4) | collective-permute-done | bytes 131104 | tf_op jit(solution)/shard_map/ppermute | solution.py:22
  72.4 0.7 copy.26
  73.1 0.6 pad.clone
  73.7 0.2 copy.22
  74.0 0.4 copy-done.2
  74.4 3.6 %fusion.26 = bf16[2,3,1,8,5,64]{5,3,4,1,0,2:T(8,128)(2,1)S(1)} fusion(bf16[3,3,3,1024,64]{3,4,2,1,0:T(8,128)(2,1)S(1)} %bitcast.53, bf16[2,5,1,7,2,1024]{5,3,4,1,0,2:T(8,128)(2,1)S(1)} %slice.12, bf16[2,5,1,8,5,1024]{5,3,4,1,0,2:T(8,128)(2,1)S(1)} %copy.22, f32[64]{0:T(128)S(1)} %copy-done.3, pred[3]{0:T(512)(128)(4,1)S(1)} %compare_and_fusion, ...), kind=kOutput, calls=%fused_computation.14 | convolution fusion | flops 569763840 | bytes 4675883 | tf_op jit(solution)/shard_map/conv_general_dilated | solution.py:63
  78.1 0.8 fusion.34
  78.8 0.3 copy.23
  79.1 0.8 copy.24
  79.9 1.9 %reshape_reshape_squeeze.3 = f32[64,2,8,64]{3,2,1,0:T(8,128)} reshape(f32[2,1,1,32,1024]{4,3,0,2,1:T(8,128)} %copy.24) | data formatting | bytes 524288 | tf_op jit(solution)/shard_map/reshape;reshape;squeeze | solution.py:87
  81.8 2.1 %copy.25 = f32[8,64,2,64]{3,2,1,0:T(2,128)} copy(f32[8,64,2,64]{3,0,2,1:T(8,128)} %bitcast.45) | data formatting | bytes 524288 | tf_op jit(solution)/shard_map/transpose | solution.py:87
  83.9 2.0 %reshape.106 = f32[8,64,128]{2,1,0:T(8,128)} reshape(f32[8,64,2,64]{3,2,1,0:T(2,128)} %copy.25) | data formatting | bytes 524288 | tf_op jit(solution)/shard_map/reshape | solution.py:88
  85.9 11.5 %all_to_all.5 = f32[8,64,128]{2,1,0:T(8,128)} all-to-all(f32[8,64,128]{2,1,0:T(8,128)} %reshape.106), channel_id=1, replica_groups=mesh['space'=64,'zh'=2,'inner'=8] {'inner'}, dimensions={0} | all-to-all | bytes 524288 | tf_op jit(solution)/shard_map/all_to_all | solution.py:89
  97.5 1.6 %reduce_sum.9 = f32[64,128]{1,0:T(8,128)} reduce(f32[8,64,128]{2,1,0:T(8,128)} %all_to_all.5, f32[]{:T(128)} %constant.23.clone.1), dimensions={0}, to_apply=%region_0.1 | reduce | flops 57344 | bytes 294916 | tf_op jit(solution)/shard_map/reduce_sum | solution.py:89
  99.0 0.9 slice_select_fusion
  100.0 18.3 %collective-permute-start.5 = (f32[64,64]{1,0:T(8,128)S(1)}, f32[64,64]{1,0:T(8,128)S(1)}, u32[]{:S(2)}, u32[]{:S(2)}) collective-permute-start(f32[64,64]{1,0:T(8,128)S(1)} %slice_select_fusion), channel_id=1, source_target_pairs={{0,8},{8,0},{1,9},{9,1},{2,10},{10,2},{3,11},{11,3},{4,12},{12,4},... | collective-permute-start | bytes 49160 | tf_op jit(solution)/shard_map/ppermute | solution.py:32
  118.2 5.9 %collective-permute-done.5 = f32[64,64]{1,0:T(8,128)S(1)} collective-permute-done((f32[64,64]{1,0:T(8,128)S(1)}, f32[64,64]{1,0:T(8,128)S(1)}, u32[]{:S(2)}, u32[]{:S(2)}) %collective-permute-start.5) | collective-permute-done | bytes 16416 | tf_op jit(solution)/shard_map/ppermute | solution.py:32
  124.1 0.9 select_add_fusion
  125.0 1.3 %add_convert_fusion = bf16[2,1,32,64]{3,2,1,0:T(8,128)(2,1)} fusion(f32[2,1,32,64]{3,2,1,0:T(8,128)S(1)} %bitcast.49, bf16[2,1,32,64]{3,2,1,0:T(8,128)(2,1)S(1)} %copy-done.1, f32[64]{0:T(128)} %param.9), kind=kLoop, calls=%fused_computation.31 | loop fusion | flops 16384 | bytes 33024 | tf_op jit(solution)/shard_map/convert_element_type | solution.py:111
  (18 shorter events, 0.2 us)
Async XLA Ops:
  0.0 78.0 %copy-start = (bf16[27,64,1024]{2,1,0:T(8,128)(2,1)S(1)}, bf16[27,64,1024]{2,1,0:T(8,128)(2,1)}, u32[]{:S(2)}) copy-start(bf16[27,64,1024]{2,1,0:T(8,128)(2,1)} %param.8) | copy-start | bytes 10616836
  0.0 31.1 %collective-permute-start = (bf16[2,1,32,64]{3,2,0,1:T(8,128)(2,1)}, bf16[2,1,32,64]{3,2,0,1:T(8,128)(2,1)S(1)}, u32[]{:S(2)}, u32[]{:S(2)}) collective-permute-start(bf16[2,1,32,64]{3,2,0,1:T(8,128)(2,1)} %bitcast.50), channel_id=1, source_target_pairs={{0,8},{8,0},{1,9},{9,1},{2,10},{10,2},{3,11},{11,3},{4,12},{12,4},... | collective-permute-start | bytes 24584 | tf_op jit(solution)/shard_map/ppermute | solution.py:32
  47.8 20.8 %collective-permute-start.1 = (bf16[2,1,32,1024]{3,2,0,1:T(8,128)(2,1)}, bf16[2,1,32,1024]{3,2,0,1:T(8,128)(2,1)}, u32[]{:S(2)}, u32[]{:S(2)}) collective-permute-start(bf16[2,1,32,1024]{3,2,0,1:T(8,128)(2,1)} %reshape.103), channel_id=1, source_target_pairs={{0,32},{8,40},{16,48},{24,56},{32,64},{40,72},{48,80},{56,88},{64,... | collective-permute-start | bytes 393224 | tf_op jit(solution)/shard_map/ppermute | solution.py:22
  51.5 18.3 %collective-permute-start.2 = (bf16[2,1,32,1024]{3,2,0,1:T(8,128)(2,1)}, bf16[2,1,32,1024]{3,2,0,1:T(8,128)(2,1)S(1)}, u32[]{:S(2)}, u32[]{:S(2)}) collective-permute-start(bf16[2,1,32,1024]{3,2,0,1:T(8,128)(2,1)} %reshape.103), channel_id=1, source_target_pairs={{0,16},{8,24},{16,32},{24,40},{32,48},{40,56},{48,64},{56,72},{64,... | collective-permute-start | bytes 393224 | tf_op jit(solution)/shard_map/ppermute | solution.py:22
  54.4 16.3 %collective-permute-start.3 = (bf16[2,1,32,1024]{3,2,0,1:T(8,128)(2,1)}, bf16[2,1,32,1024]{3,2,0,1:T(8,128)(2,1)S(1)}, u32[]{:S(2)}, u32[]{:S(2)}) collective-permute-start(bf16[2,1,32,1024]{3,2,0,1:T(8,128)(2,1)} %reshape.103), channel_id=1, source_target_pairs={{16,0},{24,8},{32,16},{40,24},{48,32},{56,40},{64,48},{72,56},{80,... | collective-permute-start | bytes 393224 | tf_op jit(solution)/shard_map/ppermute | solution.py:22
  63.8 8.6 %collective-permute-start.4 = (bf16[2,1,32,1024]{3,2,0,1:T(8,128)(2,1)}, bf16[2,1,32,1024]{3,2,0,1:T(8,128)(2,1)S(1)}, u32[]{:S(2)}, u32[]{:S(2)}) collective-permute-start(bf16[2,1,32,1024]{3,2,0,1:T(8,128)(2,1)} %reshape.103), channel_id=1, source_target_pairs={{32,0},{40,8},{48,16},{56,24},{64,32},{72,40},{80,48},{88,56},{96,... | collective-permute-start | bytes 393224 | tf_op jit(solution)/shard_map/ppermute | solution.py:22
  72.4 2.0 %copy-start.2 = (bf16[27,1024,64]{1,2,0:T(8,128)(2,1)S(1)}, bf16[27,1024,64]{1,2,0:T(8,128)(2,1)}, u32[]{:S(2)}) copy-start(bf16[27,1024,64]{1,2,0:T(8,128)(2,1)} %param.6) | copy-start | bytes 10616836
  72.4 2.0 %copy-start.3 = (f32[64]{0:T(128)S(1)}, f32[64]{0:T(128)}, u32[]{:S(2)}) copy-start(f32[64]{0:T(128)} %param.7) | copy-start | bytes 772
  72.4 2.0 %copy-start.4 = (pred[8,5]{0,1:T(8,128)(4,1)S(1)}, pred[8,5]{0,1:T(8,128)(4,1)}, u32[]{:S(2)}) copy-start(pred[8,5]{0,1:T(8,128)(4,1)} %constant.33) | copy-start | bytes 124
  79.1 45.9 %copy-start.1 = (bf16[2,1,32,64]{3,2,1,0:T(8,128)(2,1)S(1)}, bf16[2,1,32,64]{3,2,1,0:T(8,128)(2,1)}, u32[]{:S(2)}) copy-start(bf16[2,1,32,64]{3,2,1,0:T(8,128)(2,1)} %param.5) | copy-start | bytes 24580
  100.0 24.1 %collective-permute-start.5 = (f32[64,64]{1,0:T(8,128)S(1)}, f32[64,64]{1,0:T(8,128)S(1)}, u32[]{:S(2)}, u32[]{:S(2)}) collective-permute-start(f32[64,64]{1,0:T(8,128)S(1)} %slice_select_fusion), channel_id=1, source_target_pairs={{0,8},{8,0},{1,9},{9,1},{2,10},{10,2},{3,11},{11,3},{4,12},{12,4},... | collective-permute-start | bytes 49160 | tf_op jit(solution)/shard_map/ppermute | solution.py:32

commit v10 on v9

--- a/solution.py
+++ b/solution.py
@@ -22,10 +22,10 @@
     return lax.ppermute(cells, ("space", "zh"), pairs)
 
 
-def halo_rows(cells, width):
+def halo_rows(cells, width, axis):
     parts = [row_from(cells, -d) for d in range(width, 0, -1)]
     parts += [cells] + [row_from(cells, d) for d in range(1, width + 1)]
-    return jnp.concatenate(parts, axis=1)
+    return jnp.concatenate(parts, axis=axis)
 
 
 def swap_halves(v):
@@ -71,12 +71,13 @@
     return out[0]
 
 
-def gather_channels(latent):
+def gather_channels(latent, width):
     other = swap_halves(latent)
     half = lax.axis_index("zh")
     pair = jnp.where(half == 0, jnp.stack([latent, other]), jnp.stack([other, latent]))
+    pair = halo_rows(pair, width, 2)
     inner = lax.all_gather(pair, "inner", axis=0, tiled=False)
-    frame_count, row_count, col_count, own_chan = latent.shape
+    frame_count, row_count, col_count, own_chan = inner.shape[2:]
     total = inner.shape[0] * HALVES * own_chan
     return jnp.transpose(inner, (2, 3, 4, 1, 0, 5)).reshape(frame_count, row_count, col_count, total)
 
@@ -96,8 +97,7 @@
 
 def local(latent, conv_one, bias_one, conv_two, bias_two):
     frame_count, row_count, col_count, own_chan = latent.shape
-    gathered = gather_channels(latent)
-    extended = halo_rows(gathered, 2)
+    extended = gather_channels(latent, 2)
     first = conv3(extended, conv_one)
     hidden = jax.nn.relu(first + bias_one).astype(jnp.bfloat16)
     row = lax.axis_index("space") * row_count + jnp.arange(-1, row_count + 1)

time: 128 us -> 136 us (1.062)
  waiting for transfers between devices: 9.62 us -> 18.4 us
  starting transfers between devices: 68.3 us -> 64.1 us
  blocking collectives: 24.7 us -> 26.2 us
    ppermute x2, waiting for transfers between devices: 7.77 us -> 12.4 us  [swap_halves(): return lax.ppermute(v, 'zh', [(0, 1), (1, 0)])]
    ppermute x2, starting transfers between devices: 47.5 us -> 43.4 us  [swap_halves(): return lax.ppermute(v, 'zh', [(0, 1), (1, 0)])]
    ppermute x4, waiting for transfers between devices: 1.86 us -> 5.97 us  [row_from(): return lax.ppermute(cells, ('space', 'zh'), pairs)]
    another operation x0 -> x2, local copies, waits for them, and re-layouts: none -> 3.41 us  [conv3(): padded[None]]
    all_gather x0 -> x1, local copies, waits for them, and re-layouts: none -> 1.94 us  [gather_channels(): inner = lax.all_gather(pair, 'inner', axis=0, tiled=False)]
    reshape x1 -> x0, local copies, waits for them, and re-layouts: 1.79 us -> none  [gather_channels(): jnp.transpose(inner, (2, 3, 4, 1, 0, 5))]
    all_gather x1, blocking collectives: 13.2 us -> 14.7 us  [gather_channels(): inner = lax.all_gather(pair, 'inner', axis=0, tiled=False)]
    unnamed x15 -> x16, local copies, waits for them, and re-layouts: 2.94 us -> 1.96 us
  transfers between devices with their start and end apart: 6 -> 6, of which waited for: 4 -> 3; matrix products, arithmetic and copies ran while one was open for 1% -> 1% of each run, Pallas kernels for 0% -> 0%
where the time goes in v10:
time: 136 us; the launch traced here: 135 us
  starting transfers between devices  64.1 us (47%)
  blocking collectives  26.2 us (19%)
  waiting for transfers between devices  18.4 us (14%)
  local copies, waits for them, and re-layouts  14.7 us (11%)
  other arithmetic  6.82 us (5%)
  matrix products  4.39 us (3%)
    ppermute x2, starting transfers between devices, swap_halves(): return lax.ppermute(v, 'zh', [(0, 1), (1, 0)])  43.4 us
    ppermute x4, starting transfers between devices, row_from(): return lax.ppermute(cells, ('space', 'zh'), pairs)  20.8 us
    all_gather x1, blocking collectives, gather_channels(): inner = lax.all_gather(pair, 'inner', axis=0, tiled=False)  14.7 us
    ppermute x2, waiting for transfers between devices, swap_halves(): return lax.ppermute(v, 'zh', [(0, 1), (1, 0)])  12.4 us
    all_to_all x1, blocking collectives, reduce_channels(): sums = lax.all_to_all(blocks, 'inner', 0, 0, tiled=True).sum(0)  11.5 us
    ppermute x4, waiting for transfers between devices, row_from(): return lax.ppermute(cells, ('space', 'zh'), pairs)  5.97 us
    conv_general_dilated x2, matrix products, conv3(): lax.conv_general_dilated(padded[None], taps, (1, 1, 1), ((1, 1), (0, 0),...  4.39 us
    another operation x2, local copies, waits for them, and re-layouts, conv3(): padded[None]  3.41 us
  transfers between devices with their start and end apart: 6, of which 3 were waited for; matrix products, arithmetic and copies ran while one was open for 1% of the time, Pallas kernels for 0%

profile of v10, /device:TPU:24, one launch (start us, length us, event | category | flops | bytes accessed | tf_op | source)
XLA Modules:
  0.0 134.8 jit_solution(12558528530644078179)
XLA Ops:
  0.0 29.2 %collective-permute-start = (bf16[2,1,32,64]{3,2,0,1:T(8,128)(2,1)}, bf16[2,1,32,64]{3,2,0,1:T(8,128)(2,1)S(1)}, u32[]{:S(2)}, u32[]{:S(2)}) collective-permute-start(bf16[2,1,32,64]{3,2,0,1:T(8,128)(2,1)} %bitcast.49), channel_id=1, source_target_pairs={{0,8},{8,0},{1,9},{9,1},{2,10},{10,2},{3,11},{11,3},{4,12},{12,4},... | collective-permute-start | bytes 24584 | tf_op jit(solution)/shard_map/ppermute | solution.py:32
  29.2 1.9 %collective-permute-done = bf16[2,1,32,64]{3,2,0,1:T(8,128)(2,1)S(1)} collective-permute-done((bf16[2,1,32,64]{3,2,0,1:T(8,128)(2,1)}, bf16[2,1,32,64]{3,2,0,1:T(8,128)(2,1)S(1)}, u32[]{:S(2)}, u32[]{:S(2)}) %collective-permute-start) | collective-permute-done | bytes 8224 | tf_op jit(solution)/shard_map/ppermute | solution.py:32
  31.2 0.8 maximum_select_fusion
  32.0 3.7 %collective-permute-start.1 = (bf16[2,2,1,32,64]{4,3,2,1,0:T(8,128)(2,1)S(1)}, bf16[2,2,1,32,64]{4,3,2,1,0:T(8,128)(2,1)S(1)}, u32[]{:S(2)}, u32[]{:S(2)}) collective-permute-start(bf16[2,2,1,32,64]{4,3,2,1,0:T(8,128)(2,1)S(1)} %maximum_select_fusion), channel_id=1, source_target_pairs={{0,32},{8,40},{16,48},{24,56},{32,64},{40,72},{48,80},{56,88},{64,... | collective-permute-start | bytes 49160 | tf_op jit(solution)/shard_map/ppermute | solution.py:22
  35.6 0.5 compare_and_fusion
  36.2 10.8 %collective-permute-start.4 = (bf16[2,2,1,32,64]{4,3,2,1,0:T(8,128)(2,1)S(1)}, bf16[2,2,1,32,64]{4,3,2,1,0:T(8,128)(2,1)S(1)}, u32[]{:S(2)}, u32[]{:S(2)}) collective-permute-start(bf16[2,2,1,32,64]{4,3,2,1,0:T(8,128)(2,1)S(1)} %maximum_select_fusion), channel_id=1, source_target_pairs={{32,0},{40,8},{48,16},{56,24},{64,32},{72,40},{80,48},{88,56},{96,... | collective-permute-start | bytes 49160 | tf_op jit(solution)/shard_map/ppermute | solution.py:22
  47.0 4.4 %collective-permute-start.3 = (bf16[2,2,1,32,64]{4,3,2,1,0:T(8,128)(2,1)S(1)}, bf16[2,2,1,32,64]{4,3,2,1,0:T(8,128)(2,1)S(1)}, u32[]{:S(2)}, u32[]{:S(2)}) collective-permute-start(bf16[2,2,1,32,64]{4,3,2,1,0:T(8,128)(2,1)S(1)} %maximum_select_fusion), channel_id=1, source_target_pairs={{16,0},{24,8},{32,16},{40,24},{48,32},{56,40},{64,48},{72,56},{80,... | collective-permute-start | bytes 49160 | tf_op jit(solution)/shard_map/ppermute | solution.py:22
  51.4 1.9 %collective-permute-start.2 = (bf16[2,2,1,32,64]{4,3,2,1,0:T(8,128)(2,1)S(1)}, bf16[2,2,1,32,64]{4,3,2,1,0:T(8,128)(2,1)S(1)}, u32[]{:S(2)}, u32[]{:S(2)}) collective-permute-start(bf16[2,2,1,32,64]{4,3,2,1,0:T(8,128)(2,1)S(1)} %maximum_select_fusion), channel_id=1, source_target_pairs={{0,16},{8,24},{16,32},{24,40},{32,48},{40,56},{48,64},{56,72},{64,... | collective-permute-start | bytes 49160 | tf_op jit(solution)/shard_map/ppermute | solution.py:22
  53.3 6.0 %collective-permute-done.2 = bf16[2,2,1,32,64]{4,3,2,1,0:T(8,128)(2,1)S(1)} collective-permute-done((bf16[2,2,1,32,64]{4,3,2,1,0:T(8,128)(2,1)S(1)}, bf16[2,2,1,32,64]{4,3,2,1,0:T(8,128)(2,1)S(1)}, u32[]{:S(2)}, u32[]{:S(2)}) %collective-permute-start.2) | collective-permute-done | bytes 16416 | tf_op jit(solution)/shard_map/ppermute | solution.py:22
  59.3 0.8 constant_dynamic-update-slice_fusion.2
  60.2 14.7 %all-gather = bf16[16,2,5,32,64]{4,3,2,1,0:T(8,128)(2,1)S(1)} all-gather(bf16[2,2,5,32,64]{4,3,2,1,0:T(8,128)(2,1)S(1)} %constant_dynamic-update-slice_fusion), channel_id=2, replica_groups=mesh['space'=64,'zh'=2,'inner'=8] {'inner'}, dimensions={0}, use_global_device_ids=true | all-gather | bytes 737280 | tf_op jit(solution)/shard_map/all_gather | solution.py:79
  74.8 1.9 %copy.28 = bf16[8,2,2,5,32,64]{5,0,1,4,3,2:T(8,128)(2,1)} copy(bf16[8,2,2,5,32,64]{5,4,3,2,1,0:T(8,128)(2,1)S(1)} %bitcast.44) | data formatting | bytes 1310720 | tf_op jit(solution)/shard_map/all_gather | solution.py:79
  76.8 2.8 %reshape.106 = bf16[2,5,1,32,1024]{4,3,1,0,2:T(8,128)(2,1)} reshape(bf16[2,5,32,2,8,64]{5,4,3,2,1,0:T(8,128)(2,1)} %bitcast.45) | data formatting | bytes 1310720 | tf_op jit(solution)/shard_map/broadcast_in_dim;reshape | solution.py:64
  79.6 1.9 %copy.26 = bf16[2,5,1,32,1024]{4,0,3,1,2:T(2,128)(2,1)S(1)} copy(bf16[2,5,1,32,1024]{4,3,1,0,2:T(8,128)(2,1)} %reshape.106) | data formatting | bytes 1310720
  81.5 0.6 pad.clone
  82.1 0.2 copy.22
  82.3 0.1 slice.12
  82.5 3.6 %fusion.26 = bf16[2,3,1,8,5,64]{5,3,4,1,0,2:T(8,128)(2,1)S(1)} fusion(bf16[3,3,3,1024,64]{3,4,2,1,0:T(8,128)(2,1)S(1)} %bitcast.55, bf16[2,5,1,7,2,1024]{5,3,4,1,0,2:T(8,128)(2,1)S(1)} %slice.12, bf16[2,5,1,8,5,1024]{5,3,4,1,0,2:T(8,128)(2,1)S(1)} %copy.22, f32[64]{0:T(128)S(1)} %copy-done.3, pred[3]{0:T(512)(128)(4,1)S(1)} %copy-done.4, ...), kind=kOutput, calls=%fused_computation.15 | convolution fusion | flops 569763840 | bytes 4675883 | tf_op jit(solution)/shard_map/conv_general_dilated | solution.py:63
  86.1 0.8 fusion.34
  86.9 0.3 copy.23
  87.1 0.0 copy-start.1
  87.2 0.8 copy.24
  88.0 1.9 %reshape_reshape_squeeze.3 = f32[64,2,8,64]{3,2,1,0:T(8,128)} reshape(f32[2,1,1,32,1024]{4,3,0,2,1:T(8,128)} %copy.24) | data formatting | bytes 524288 | tf_op jit(solution)/shard_map/reshape;reshape;squeeze | solution.py:88
  89.8 2.1 %copy.25 = f32[8,64,2,64]{3,2,1,0:T(2,128)} copy(f32[8,64,2,64]{3,0,2,1:T(8,128)} %bitcast.47) | data formatting | bytes 524288 | tf_op jit(solution)/shard_map/transpose | solution.py:88
  91.9 2.1 %reshape.94 = f32[8,64,128]{2,1,0:T(8,128)} reshape(f32[8,64,2,64]{3,2,1,0:T(2,128)} %copy.25) | data formatting | bytes 524288 | tf_op jit(solution)/shard_map/reshape | solution.py:89
  94.0 11.5 %all_to_all.5 = f32[8,64,128]{2,1,0:T(8,128)} all-to-all(f32[8,64,128]{2,1,0:T(8,128)} %reshape.94), channel_id=1, replica_groups=mesh['space'=64,'zh'=2,'inner'=8] {'inner'}, dimensions={0} | all-to-all | bytes 524288 | tf_op jit(solution)/shard_map/all_to_all | solution.py:90
  105.5 1.6 %reduce_sum.9 = f32[64,128]{1,0:T(8,128)} reduce(f32[8,64,128]{2,1,0:T(8,128)} %all_to_all.5, f32[]{:T(128)} %constant.23.clone.1), dimensions={0}, to_apply=%region_0.1 | reduce | flops 57344 | bytes 294916 | tf_op jit(solution)/shard_map/reduce_sum | solution.py:90
  107.1 0.9 slice_select_fusion
  108.0 14.1 %collective-permute-start.5 = (f32[64,64]{1,0:T(8,128)S(1)}, f32[64,64]{1,0:T(8,128)S(1)}, u32[]{:S(2)}, u32[]{:S(2)}) collective-permute-start(f32[64,64]{1,0:T(8,128)S(1)} %slice_select_fusion), channel_id=1, source_target_pairs={{0,8},{8,0},{1,9},{9,1},{2,10},{10,2},{3,11},{11,3},{4,12},{12,4},... | collective-permute-start | bytes 49160 | tf_op jit(solution)/shard_map/ppermute | solution.py:32
  122.2 10.5 %collective-permute-done.5 = f32[64,64]{1,0:T(8,128)S(1)} collective-permute-done((f32[64,64]{1,0:T(8,128)S(1)}, f32[64,64]{1,0:T(8,128)S(1)}, u32[]{:S(2)}, u32[]{:S(2)}) %collective-permute-start.5) | collective-permute-done | bytes 16416 | tf_op jit(solution)/shard_map/ppermute | solution.py:32
  132.7 0.9 select_add_fusion
  133.6 1.3 add_convert_fusion
  (20 shorter events, 0.1 us)
Async XLA Ops:
  0.0 86.1 %copy-start = (bf16[27,64,1024]{2,1,0:T(8,128)(2,1)S(1)}, bf16[27,64,1024]{2,1,0:T(8,128)(2,1)}, u32[]{:S(2)}) copy-start(bf16[27,64,1024]{2,1,0:T(8,128)(2,1)} %param.8) | copy-start | bytes 10616836
  0.0 31.1 %collective-permute-start = (bf16[2,1,32,64]{3,2,0,1:T(8,128)(2,1)}, bf16[2,1,32,64]{3,2,0,1:T(8,128)(2,1)S(1)}, u32[]{:S(2)}, u32[]{:S(2)}) collective-permute-start(bf16[2,1,32,64]{3,2,0,1:T(8,128)(2,1)} %bitcast.49), channel_id=1, source_target_pairs={{0,8},{8,0},{1,9},{9,1},{2,10},{10,2},{3,11},{11,3},{4,12},{12,4},... | collective-permute-start | bytes 24584 | tf_op jit(solution)/shard_map/ppermute | solution.py:32
  32.0 21.3 %collective-permute-start.1 = (bf16[2,2,1,32,64]{4,3,2,1,0:T(8,128)(2,1)S(1)}, bf16[2,2,1,32,64]{4,3,2,1,0:T(8,128)(2,1)S(1)}, u32[]{:S(2)}, u32[]{:S(2)}) collective-permute-start(bf16[2,2,1,32,64]{4,3,2,1,0:T(8,128)(2,1)S(1)} %maximum_select_fusion), channel_id=1, source_target_pairs={{0,32},{8,40},{16,48},{24,56},{32,64},{40,72},{48,80},{56,88},{64,... | collective-permute-start | bytes 49160 | tf_op jit(solution)/shard_map/ppermute | solution.py:22
  36.2 24.0 %collective-permute-start.4 = (bf16[2,2,1,32,64]{4,3,2,1,0:T(8,128)(2,1)S(1)}, bf16[2,2,1,32,64]{4,3,2,1,0:T(8,128)(2,1)S(1)}, u32[]{:S(2)}, u32[]{:S(2)}) collective-permute-start(bf16[2,2,1,32,64]{4,3,2,1,0:T(8,128)(2,1)S(1)} %maximum_select_fusion), channel_id=1, source_target_pairs={{32,0},{40,8},{48,16},{56,24},{64,32},{72,40},{80,48},{88,56},{96,... | collective-permute-start | bytes 49160 | tf_op jit(solution)/shard_map/ppermute | solution.py:22
  47.0 13.1 %collective-permute-start.3 = (bf16[2,2,1,32,64]{4,3,2,1,0:T(8,128)(2,1)S(1)}, bf16[2,2,1,32,64]{4,3,2,1,0:T(8,128)(2,1)S(1)}, u32[]{:S(2)}, u32[]{:S(2)}) collective-permute-start(bf16[2,2,1,32,64]{4,3,2,1,0:T(8,128)(2,1)S(1)} %maximum_select_fusion), channel_id=1, source_target_pairs={{16,0},{24,8},{32,16},{40,24},{48,32},{56,40},{64,48},{72,56},{80,... | collective-permute-start | bytes 49160 | tf_op jit(solution)/shard_map/ppermute | solution.py:22
  51.4 7.9 %collective-permute-start.2 = (bf16[2,2,1,32,64]{4,3,2,1,0:T(8,128)(2,1)S(1)}, bf16[2,2,1,32,64]{4,3,2,1,0:T(8,128)(2,1)S(1)}, u32[]{:S(2)}, u32[]{:S(2)}) collective-permute-start(bf16[2,2,1,32,64]{4,3,2,1,0:T(8,128)(2,1)S(1)} %maximum_select_fusion), channel_id=1, source_target_pairs={{0,16},{8,24},{16,32},{24,40},{32,48},{40,56},{48,64},{56,72},{64,... | collective-permute-start | bytes 49160 | tf_op jit(solution)/shard_map/ppermute | solution.py:22
  79.6 2.8 %copy-start.2 = (bf16[27,1024,64]{1,2,0:T(8,128)(2,1)S(1)}, bf16[27,1024,64]{1,2,0:T(8,128)(2,1)}, u32[]{:S(2)}) copy-start(bf16[27,1024,64]{1,2,0:T(8,128)(2,1)} %param.6) | copy-start | bytes 10616836
  79.6 2.8 %copy-start.3 = (f32[64]{0:T(128)S(1)}, f32[64]{0:T(128)}, u32[]{:S(2)}) copy-start(f32[64]{0:T(128)} %param.7) | copy-start | bytes 772
  79.6 2.8 %copy-start.4 = (pred[3]{0:T(512)(128)(4,1)S(1)}, pred[3]{0:T(512)(128)(4,1)}, u32[]{:S(2)}) copy-start(pred[3]{0:T(512)(128)(4,1)} %compare_and_fusion) | copy-start | bytes 13
  79.6 2.9 %copy-start.5 = (pred[8,5]{0,1:T(8,128)(4,1)S(1)}, pred[8,5]{0,1:T(8,128)(4,1)}, u32[]{:S(2)}) copy-start(pred[8,5]{0,1:T(8,128)(4,1)} %constant.33) | copy-start | bytes 124
  87.1 46.4 %copy-start.1 = (bf16[2,1,32,64]{3,2,1,0:T(8,128)(2,1)S(1)}, bf16[2,1,32,64]{3,2,1,0:T(8,128)(2,1)}, u32[]{:S(2)}) copy-start(bf16[2,1,32,64]{3,2,1,0:T(8,128)(2,1)} %param.5) | copy-start | bytes 24580
  108.0 24.6 %collective-permute-start.5 = (f32[64,64]{1,0:T(8,128)S(1)}, f32[64,64]{1,0:T(8,128)S(1)}, u32[]{:S(2)}, u32[]{:S(2)}) collective-permute-start(f32[64,64]{1,0:T(8,128)S(1)} %slice_select_fusion), channel_id=1, source_target_pairs={{0,8},{8,0},{1,9},{9,1},{2,10},{10,2},{3,11},{11,3},{4,12},{12,4},... | collective-permute-start | bytes 49160 | tf_op jit(solution)/shard_map/ppermute | solution.py:32

commit v11 on v9

--- a/solution.py
+++ b/solution.py
@@ -72,9 +72,7 @@
 
 
 def gather_channels(latent):
-    other = swap_halves(latent)
-    half = lax.axis_index("zh")
-    pair = jnp.where(half == 0, jnp.stack([latent, other]), jnp.stack([other, latent]))
+    pair = lax.all_gather(latent, "zh", axis=0, tiled=False)
     inner = lax.all_gather(pair, "inner", axis=0, tiled=False)
     frame_count, row_count, col_count, own_chan = latent.shape
     total = inner.shape[0] * HALVES * own_chan

time: 128 us -> 126 us (0.984)
  starting transfers between devices: 68.3 us -> 42.9 us
  blocking collectives: 24.7 us -> 43 us
  waiting for transfers between devices: 9.62 us -> 13.8 us
  local copies, waits for them, and re-layouts: 13.6 us -> 16.3 us
    all_gather x0 -> x1, blocking collectives: none -> 29.8 us  [gather_channels(): pair = lax.all_gather(latent, 'zh', axis=0, tiled=False)]
    ppermute x2 -> x1, starting transfers between devices: 47.5 us -> 18.1 us  [swap_halves(): return lax.ppermute(v, 'zh', [(0, 1), (1, 0)])]
    all_to_all x1 -> x0, blocking collectives: 11.5 us -> none  [reduce_channels(): sums = lax.all_to_all(blocks, 'inner', 0, 0, tiled=True).sum(0)]
    all_to_all x0 -> x1, waiting for transfers between devices: none -> 7.5 us  [reduce_channels(): sums = lax.all_to_all(blocks, 'inner', 0, 0, tiled=True).sum(0)]
    all_to_all x0 -> x1, starting transfers between devices: none -> 4.06 us  [reduce_channels(): sums = lax.all_to_all(blocks, 'inner', 0, 0, tiled=True).sum(0)]
    unnamed x15, local copies, waits for them, and re-layouts: 2.94 us -> 4.75 us
    ppermute x2 -> x1, waiting for transfers between devices: 7.77 us -> 6.03 us  [swap_halves(): return lax.ppermute(v, 'zh', [(0, 1), (1, 0)])]
    ppermute x4, waiting for transfers between devices: 1.86 us -> 0.3 us  [row_from(): return lax.ppermute(cells, ('space', 'zh'), pairs)]
  transfers between devices with their start and end apart: 6 -> 6, of which waited for: 4 -> 3; matrix products, arithmetic and copies ran while one was open for 1% -> 3% of each run, Pallas kernels for 0% -> 0%
where the time goes in v11:
time: 126 us; the launch traced here: 125 us
  blocking collectives  43 us (34%)
  starting transfers between devices  42.9 us (34%)
  local copies, waits for them, and re-layouts  16.3 us (13%)
  waiting for transfers between devices  13.8 us (11%)
  other arithmetic  4.68 us (4%)
  matrix products  4.38 us (3%)
    all_gather x1, blocking collectives, gather_channels(): pair = lax.all_gather(latent, 'zh', axis=0, tiled=False)  29.8 us
    ppermute x4, starting transfers between devices, row_from(): return lax.ppermute(cells, ('space', 'zh'), pairs)  20.8 us
    ppermute x1, starting transfers between devices, swap_halves(): return lax.ppermute(v, 'zh', [(0, 1), (1, 0)])  18.1 us
    all_gather x1, blocking collectives, gather_channels(): inner = lax.all_gather(pair, 'inner', axis=0, tiled=False)  13.2 us
    all_to_all x1, waiting for transfers between devices, reduce_channels(): sums = lax.all_to_all(blocks, 'inner', 0, 0, tiled=True).sum(0)  7.5 us
    ppermute x1, waiting for transfers between devices, swap_halves(): return lax.ppermute(v, 'zh', [(0, 1), (1, 0)])  6.03 us
    unnamed x15, local copies, waits for them, and re-layouts  4.75 us
    conv_general_dilated x2, matrix products, conv3(): lax.conv_general_dilated(padded[None], taps, (1, 1, 1), ((1, 1), (0, 0),...  4.38 us
  transfers between devices with their start and end apart: 6, of which 3 were waited for; matrix products, arithmetic and copies ran while one was open for 3% of the time, Pallas kernels for 0%

profile of v11, /device:TPU:24, one launch (start us, length us, event | category | flops | bytes accessed | tf_op | source)
XLA Modules:
  0.0 125.3 jit_solution(6163053280483651424)
XLA Ops:
  0.0 29.8 %all-gather = bf16[4,1,32,64]{3,2,1,0:T(8,128)(2,1)S(1)} all-gather(bf16[2,1,32,64]{3,2,1,0:T(8,128)(2,1)} %param.5), channel_id=2, replica_groups=mesh['space'=64,'zh'=2,'inner'=8] {'zh'}, dimensions={0}, use_global_device_ids=true | all-gather | bytes 24576 | tf_op jit(solution)/shard_map/all_gather | solution.py:75
  29.8 13.2 %all-gather.1 = bf16[16,2,1,32,64]{4,3,2,1,0:T(8,128)(2,1)S(1)} all-gather(bf16[2,2,1,32,64]{4,3,2,1,0:T(8,128)(2,1)S(1)} %bitcast.51), channel_id=3, replica_groups=mesh['space'=64,'zh'=2,'inner'=8] {'inner'}, dimensions={0}, use_global_device_ids=true | all-gather | bytes 147456 | tf_op jit(solution)/shard_map/all_gather | solution.py:76
  43.0 0.9 copy.18
  43.9 1.8 %reshape.27 = bf16[2,1,32,1024]{3,2,0,1:T(8,128)(2,1)} reshape(bf16[2,1,32,2,8,64]{5,4,3,2,0,1:T(8,128)(2,1)} %copy.18) | data formatting | bytes 262144 | tf_op jit(solution)/shard_map/reshape | solution.py:79
  45.7 3.6 %collective-permute-start = (bf16[2,1,32,1024]{3,2,0,1:T(8,128)(2,1)}, bf16[2,1,32,1024]{3,2,0,1:T(8,128)(2,1)}, u32[]{:S(2)}, u32[]{:S(2)}) collective-permute-start(bf16[2,1,32,1024]{3,2,0,1:T(8,128)(2,1)} %reshape.27), channel_id=1, source_target_pairs={{0,32},{8,40},{16,48},{24,56},{32,64},{40,72},{48,80},{56,88},{64,... | collective-permute-start | bytes 393224 | tf_op jit(solution)/shard_map/ppermute | solution.py:22
  49.3 2.9 %collective-permute-start.1 = (bf16[2,1,32,1024]{3,2,0,1:T(8,128)(2,1)}, bf16[2,1,32,1024]{3,2,0,1:T(8,128)(2,1)}, u32[]{:S(2)}, u32[]{:S(2)}) collective-permute-start(bf16[2,1,32,1024]{3,2,0,1:T(8,128)(2,1)} %reshape.27), channel_id=1, source_target_pairs={{0,16},{8,24},{16,32},{24,40},{32,48},{40,56},{48,64},{56,72},{64,... | collective-permute-start | bytes 393224 | tf_op jit(solution)/shard_map/ppermute | solution.py:22
  52.2 9.4 %collective-permute-start.2 = (bf16[2,1,32,1024]{3,2,0,1:T(8,128)(2,1)}, bf16[2,1,32,1024]{3,2,0,1:T(8,128)(2,1)}, u32[]{:S(2)}, u32[]{:S(2)}) collective-permute-start(bf16[2,1,32,1024]{3,2,0,1:T(8,128)(2,1)} %reshape.27), channel_id=1, source_target_pairs={{16,0},{24,8},{32,16},{40,24},{48,32},{56,40},{64,48},{72,56},{80,... | collective-permute-start | bytes 393224 | tf_op jit(solution)/shard_map/ppermute | solution.py:22
  61.6 4.8 %collective-permute-start.3 = (bf16[2,1,32,1024]{3,2,0,1:T(8,128)(2,1)}, bf16[2,1,32,1024]{3,2,0,1:T(8,128)(2,1)}, u32[]{:S(2)}, u32[]{:S(2)}) collective-permute-start(bf16[2,1,32,1024]{3,2,0,1:T(8,128)(2,1)} %reshape.27), channel_id=1, source_target_pairs={{32,0},{40,8},{48,16},{56,24},{64,32},{72,40},{80,48},{88,56},{96,... | collective-permute-start | bytes 393224 | tf_op jit(solution)/shard_map/ppermute | solution.py:22
  66.5 0.9 constant_dynamic-update-slice_fusion.4
  67.4 0.3 collective-permute-done.1
  67.7 0.9 constant_dynamic-update-slice_fusion.3
  68.6 0.9 constant_dynamic-update-slice_fusion.2
  69.6 0.9 constant_dynamic-update-slice_fusion.1
  70.5 0.9 constant_dynamic-update-slice_fusion
  71.4 0.7 copy.25
  72.1 0.6 pad.clone
  73.0 0.4 copy-done.2
  73.4 3.6 %fusion.26 = bf16[2,3,1,8,5,64]{5,3,4,1,0,2:T(8,128)(2,1)S(1)} fusion(bf16[3,3,3,1024,64]{3,4,2,1,0:T(8,128)(2,1)S(1)} %bitcast.53, bf16[2,5,1,7,2,1024]{5,3,4,1,0,2:T(8,128)(2,1)S(1)} %slice.12, bf16[2,5,1,8,5,1024]{5,3,4,1,0,2:T(8,128)(2,1)S(1)} %copy.21, f32[64]{0:T(128)S(1)} %copy-done.3, pred[3]{0:T(512)(128)(4,1)S(1)} %compare_and_fusion, ...), kind=kOutput, calls=%fused_computation.14 | convolution fusion | flops 569763840 | bytes 4675883 | tf_op jit(solution)/shard_map/conv_general_dilated | solution.py:63
  77.1 0.8 fusion.34
  77.8 0.3 copy.22
  78.1 0.8 copy.23
  78.9 1.9 %reshape_reshape_squeeze.3 = f32[64,2,8,64]{3,2,1,0:T(8,128)} reshape(f32[2,1,1,32,1024]{4,3,0,2,1:T(8,128)} %copy.23) | data formatting | bytes 524288 | tf_op jit(solution)/shard_map/reshape;reshape;squeeze | solution.py:85
  80.8 2.1 %copy.24 = f32[8,64,2,64]{3,2,1,0:T(2,128)} copy(f32[8,64,2,64]{3,0,2,1:T(8,128)} %bitcast.47) | data formatting | bytes 524288 | tf_op jit(solution)/shard_map/transpose | solution.py:85
  82.9 2.0 %reshape.30 = f32[8,64,128]{2,1,0:T(8,128)} reshape(f32[8,64,2,64]{3,2,1,0:T(2,128)} %copy.24) | data formatting | bytes 524288 | tf_op jit(solution)/shard_map/reshape | solution.py:86
  84.9 4.1 %all-to-all-start = ((f32[8,64,128]{2,1,0:T(8,128)}), f32[8,64,128]{2,1,0:T(8,128)}, u32[]{:S(2)}, u32[]{:S(2)}) async-start(f32[8,64,128]{2,1,0:T(8,128)} %reshape.30), calls=%async_computation | async-start | bytes 524288 | tf_op jit(solution)/shard_map/all_to_all | solution.py:87
  89.0 7.5 %all-to-all-done = f32[8,64,128]{2,1,0:T(8,128)} async-done(((f32[8,64,128]{2,1,0:T(8,128)}), f32[8,64,128]{2,1,0:T(8,128)}, u32[]{:S(2)}, u32[]{:S(2)}) %all-to-all-start) | async-done | bytes 262176 | tf_op jit(solution)/shard_map/all_to_all | solution.py:87
  96.5 1.6 %reduce_sum.9 = f32[64,128]{1,0:T(8,128)} reduce(f32[8,64,128]{2,1,0:T(8,128)} %all-to-all-done, f32[]{:T(128)} %constant.23.clone.1), dimensions={0}, to_apply=%region_0.1 | reduce | flops 57344 | bytes 294916 | tf_op jit(solution)/shard_map/reduce_sum | solution.py:87
  98.1 0.9 slice_select_fusion
  99.0 18.1 %collective-permute-start.4 = (f32[64,64]{1,0:T(8,128)S(1)}, f32[64,64]{1,0:T(8,128)S(1)}, u32[]{:S(2)}, u32[]{:S(2)}) collective-permute-start(f32[64,64]{1,0:T(8,128)S(1)} %slice_select_fusion), channel_id=1, source_target_pairs={{0,8},{8,0},{1,9},{9,1},{2,10},{10,2},{3,11},{11,3},{4,12},{12,4},... | collective-permute-start | bytes 49160 | tf_op jit(solution)/shard_map/ppermute | solution.py:32
  117.1 6.0 %collective-permute-done.4 = f32[64,64]{1,0:T(8,128)S(1)} collective-permute-done((f32[64,64]{1,0:T(8,128)S(1)}, f32[64,64]{1,0:T(8,128)S(1)}, u32[]{:S(2)}, u32[]{:S(2)}) %collective-permute-start.4) | collective-permute-done | bytes 16416 | tf_op jit(solution)/shard_map/ppermute | solution.py:32
  123.1 0.9 select_add_fusion
  124.0 1.3 %add_convert_fusion = bf16[2,1,32,64]{3,2,1,0:T(8,128)(2,1)} fusion(f32[2,1,32,64]{3,2,1,0:T(8,128)S(1)} %bitcast.52, bf16[2,1,32,64]{3,2,1,0:T(8,128)(2,1)S(1)} %copy-done.1, f32[64]{0:T(128)} %param.9), kind=kLoop, calls=%fused_computation.30 | loop fusion | flops 16384 | bytes 33024 | tf_op jit(solution)/shard_map/convert_element_type | solution.py:109
  (17 shorter events, 0.4 us)
Async XLA Ops:
  0.0 77.0 %copy-start = (bf16[27,64,1024]{2,1,0:T(8,128)(2,1)S(1)}, bf16[27,64,1024]{2,1,0:T(8,128)(2,1)}, u32[]{:S(2)}) copy-start(bf16[27,64,1024]{2,1,0:T(8,128)(2,1)} %param.8) | copy-start | bytes 10616836
  45.7 20.8 %collective-permute-start = (bf16[2,1,32,1024]{3,2,0,1:T(8,128)(2,1)}, bf16[2,1,32,1024]{3,2,0,1:T(8,128)(2,1)}, u32[]{:S(2)}, u32[]{:S(2)}) collective-permute-start(bf16[2,1,32,1024]{3,2,0,1:T(8,128)(2,1)} %reshape.27), channel_id=1, source_target_pairs={{0,32},{8,40},{16,48},{24,56},{32,64},{40,72},{48,80},{56,88},{64,... | collective-permute-start | bytes 393224 | tf_op jit(solution)/shard_map/ppermute | solution.py:22
  49.3 18.4 %collective-permute-start.1 = (bf16[2,1,32,1024]{3,2,0,1:T(8,128)(2,1)}, bf16[2,1,32,1024]{3,2,0,1:T(8,128)(2,1)}, u32[]{:S(2)}, u32[]{:S(2)}) collective-permute-start(bf16[2,1,32,1024]{3,2,0,1:T(8,128)(2,1)} %reshape.27), channel_id=1, source_target_pairs={{0,16},{8,24},{16,32},{24,40},{32,48},{40,56},{48,64},{56,72},{64,... | collective-permute-start | bytes 393224 | tf_op jit(solution)/shard_map/ppermute | solution.py:22
  52.2 17.3 %collective-permute-start.2 = (bf16[2,1,32,1024]{3,2,0,1:T(8,128)(2,1)}, bf16[2,1,32,1024]{3,2,0,1:T(8,128)(2,1)}, u32[]{:S(2)}, u32[]{:S(2)}) collective-permute-start(bf16[2,1,32,1024]{3,2,0,1:T(8,128)(2,1)} %reshape.27), channel_id=1, source_target_pairs={{16,0},{24,8},{32,16},{40,24},{48,32},{56,40},{64,48},{72,56},{80,... | collective-permute-start | bytes 393224 | tf_op jit(solution)/shard_map/ppermute | solution.py:22
  61.6 8.8 %collective-permute-start.3 = (bf16[2,1,32,1024]{3,2,0,1:T(8,128)(2,1)}, bf16[2,1,32,1024]{3,2,0,1:T(8,128)(2,1)}, u32[]{:S(2)}, u32[]{:S(2)}) collective-permute-start(bf16[2,1,32,1024]{3,2,0,1:T(8,128)(2,1)} %reshape.27), channel_id=1, source_target_pairs={{32,0},{40,8},{48,16},{56,24},{64,32},{72,40},{80,48},{88,56},{96,... | collective-permute-start | bytes 393224 | tf_op jit(solution)/shard_map/ppermute | solution.py:22
  71.4 2.0 %copy-start.2 = (bf16[27,1024,64]{1,2,0:T(8,128)(2,1)S(1)}, bf16[27,1024,64]{1,2,0:T(8,128)(2,1)}, u32[]{:S(2)}) copy-start(bf16[27,1024,64]{1,2,0:T(8,128)(2,1)} %param.6) | copy-start | bytes 10616836
  71.4 2.0 %copy-start.3 = (f32[64]{0:T(128)S(1)}, f32[64]{0:T(128)}, u32[]{:S(2)}) copy-start(f32[64]{0:T(128)} %param.7) | copy-start | bytes 772
  71.4 2.0 %copy-start.4 = (pred[8,5]{0,1:T(8,128)(4,1)S(1)}, pred[8,5]{0,1:T(8,128)(4,1)}, u32[]{:S(2)}) copy-start(pred[8,5]{0,1:T(8,128)(4,1)} %constant.33) | copy-start | bytes 124
  78.1 45.9 %copy-start.1 = (bf16[2,1,32,64]{3,2,1,0:T(8,128)(2,1)S(1)}, bf16[2,1,32,64]{3,2,1,0:T(8,128)(2,1)}, u32[]{:S(2)}) copy-start(bf16[2,1,32,64]{3,2,1,0:T(8,128)(2,1)} %param.5) | copy-start | bytes 24580
  84.9 11.6 %all-to-all-start = ((f32[8,64,128]{2,1,0:T(8,128)}), f32[8,64,128]{2,1,0:T(8,128)}, u32[]{:S(2)}, u32[]{:S(2)}) async-start(f32[8,64,128]{2,1,0:T(8,128)} %reshape.30), calls=%async_computation | async-start | bytes 524288 | tf_op jit(solution)/shard_map/all_to_all | solution.py:87
  99.0 24.1 %collective-permute-start.4 = (f32[64,64]{1,0:T(8,128)S(1)}, f32[64,64]{1,0:T(8,128)S(1)}, u32[]{:S(2)}, u32[]{:S(2)}) collective-permute-start(f32[64,64]{1,0:T(8,128)S(1)} %slice_select_fusion), channel_id=1, source_target_pairs={{0,8},{8,0},{1,9},{9,1},{2,10},{10,2},{3,11},{11,3},{4,12},{12,4},... | collective-permute-start | bytes 49160 | tf_op jit(solution)/shard_map/ppermute | solution.py:32

commit v12 on v11

--- a/solution.py
+++ b/solution.py
@@ -89,7 +89,8 @@
     low, high = sums[:, :own_chan], sums[:, own_chan:]
     mine = jnp.where(half == 0, low, high)
     theirs = jnp.where(half == 0, high, low)
-    return mine + swap_halves(theirs)
+    both = lax.all_gather(theirs, "zh", axis=0, tiled=False)
+    return mine + jnp.where(half == 0, both[1], both[0])
 
 
 def local(latent, conv_one, bias_one, conv_two, bias_two):

time: 126 us -> 125 us (level)
  blocking collectives: 43 us -> 65.9 us
  starting transfers between devices: 42.9 us -> 24.8 us
  waiting for transfers between devices: 13.8 us -> 7.8 us
    all_gather x0 -> x1, blocking collectives: none -> 22.9 us  [reduce_channels(): both = lax.all_gather(theirs, 'zh', axis=0, tiled=False)]
    ppermute x1 -> x0, starting transfers between devices: 18.1 us -> none  [swap_halves(): return lax.ppermute(v, 'zh', [(0, 1), (1, 0)])]
    ppermute x1 -> x0, waiting for transfers between devices: 6.03 us -> none  [swap_halves(): return lax.ppermute(v, 'zh', [(0, 1), (1, 0)])]
  transfers between devices with their start and end apart: 6 -> 5, of which waited for: 3 -> 2; matrix products, arithmetic and copies ran while one was open for 3% -> 3% of each run, Pallas kernels for 0% -> 0%
where the time goes in v12:
time: 125 us; the launch traced here: 124 us
  blocking collectives  65.9 us (53%)
  starting transfers between devices  24.8 us (20%)
  local copies, waits for them, and re-layouts  16.3 us (13%)
  waiting for transfers between devices  7.8 us (6%)
  other arithmetic  4.67 us (4%)
  matrix products  4.38 us (4%)
    all_gather x1, blocking collectives, gather_channels(): pair = lax.all_gather(latent, 'zh', axis=0, tiled=False)  29.8 us
    all_gather x1, blocking collectives, reduce_channels(): both = lax.all_gather(theirs, 'zh', axis=0, tiled=False)  22.9 us
    ppermute x4, starting transfers between devices, row_from(): return lax.ppermute(cells, ('space', 'zh'), pairs)  20.8 us
    all_gather x1, blocking collectives, gather_channels(): inner = lax.all_gather(pair, 'inner', axis=0, tiled=False)  13.2 us
    all_to_all x1, waiting for transfers between devices, reduce_channels(): sums = lax.all_to_all(blocks, 'inner', 0, 0, tiled=True).sum(0)  7.5 us
    unnamed x15, local copies, waits for them, and re-layouts  4.75 us
    conv_general_dilated x2, matrix products, conv3(): lax.conv_general_dilated(padded[None], taps, (1, 1, 1), ((1, 1), (0, 0),...  4.38 us
    all_to_all x1, starting transfers between devices, reduce_channels(): sums = lax.all_to_all(blocks, 'inner', 0, 0, tiled=True).sum(0)  4.05 us
  transfers between devices with their start and end apart: 5, of which 2 were waited for; matrix products, arithmetic and copies ran while one was open for 3% of the time, Pallas kernels for 0%

profile of v12, /device:TPU:24, one launch (start us, length us, event | category | flops | bytes accessed | tf_op | source)
XLA Modules:
  0.0 124.0 jit_solution(11793975361550683967)
XLA Ops:
  0.0 29.8 %all-gather = bf16[4,1,32,64]{3,2,1,0:T(8,128)(2,1)S(1)} all-gather(bf16[2,1,32,64]{3,2,1,0:T(8,128)(2,1)} %param.5), channel_id=2, replica_groups=mesh['space'=64,'zh'=2,'inner'=8] {'zh'}, dimensions={0}, use_global_device_ids=true | all-gather | bytes 24576 | tf_op jit(solution)/shard_map/all_gather | solution.py:75
  29.8 13.2 %all-gather.1 = bf16[16,2,1,32,64]{4,3,2,1,0:T(8,128)(2,1)S(1)} all-gather(bf16[2,2,1,32,64]{4,3,2,1,0:T(8,128)(2,1)S(1)} %bitcast.52), channel_id=3, replica_groups=mesh['space'=64,'zh'=2,'inner'=8] {'inner'}, dimensions={0}, use_global_device_ids=true | all-gather | bytes 147456 | tf_op jit(solution)/shard_map/all_gather | solution.py:76
  43.0 0.9 copy.18
  43.8 1.8 %reshape.29 = bf16[2,1,32,1024]{3,2,0,1:T(8,128)(2,1)} reshape(bf16[2,1,32,2,8,64]{5,4,3,2,0,1:T(8,128)(2,1)} %copy.18) | data formatting | bytes 262144 | tf_op jit(solution)/shard_map/reshape | solution.py:79
  45.6 3.6 %collective-permute-start = (bf16[2,1,32,1024]{3,2,0,1:T(8,128)(2,1)}, bf16[2,1,32,1024]{3,2,0,1:T(8,128)(2,1)}, u32[]{:S(2)}, u32[]{:S(2)}) collective-permute-start(bf16[2,1,32,1024]{3,2,0,1:T(8,128)(2,1)} %reshape.29), channel_id=1, source_target_pairs={{0,32},{8,40},{16,48},{24,56},{32,64},{40,72},{48,80},{56,88},{64,... | collective-permute-start | bytes 393224 | tf_op jit(solution)/shard_map/ppermute | solution.py:22
  49.3 2.9 %collective-permute-start.1 = (bf16[2,1,32,1024]{3,2,0,1:T(8,128)(2,1)}, bf16[2,1,32,1024]{3,2,0,1:T(8,128)(2,1)}, u32[]{:S(2)}, u32[]{:S(2)}) collective-permute-start(bf16[2,1,32,1024]{3,2,0,1:T(8,128)(2,1)} %reshape.29), channel_id=1, source_target_pairs={{0,16},{8,24},{16,32},{24,40},{32,48},{40,56},{48,64},{56,72},{64,... | collective-permute-start | bytes 393224 | tf_op jit(solution)/shard_map/ppermute | solution.py:22
  52.2 9.4 %collective-permute-start.2 = (bf16[2,1,32,1024]{3,2,0,1:T(8,128)(2,1)}, bf16[2,1,32,1024]{3,2,0,1:T(8,128)(2,1)}, u32[]{:S(2)}, u32[]{:S(2)}) collective-permute-start(bf16[2,1,32,1024]{3,2,0,1:T(8,128)(2,1)} %reshape.29), channel_id=1, source_target_pairs={{16,0},{24,8},{32,16},{40,24},{48,32},{56,40},{64,48},{72,56},{80,... | collective-permute-start | bytes 393224 | tf_op jit(solution)/shard_map/ppermute | solution.py:22
  61.6 4.8 %collective-permute-start.3 = (bf16[2,1,32,1024]{3,2,0,1:T(8,128)(2,1)}, bf16[2,1,32,1024]{3,2,0,1:T(8,128)(2,1)}, u32[]{:S(2)}, u32[]{:S(2)}) collective-permute-start(bf16[2,1,32,1024]{3,2,0,1:T(8,128)(2,1)} %reshape.29), channel_id=1, source_target_pairs={{32,0},{40,8},{48,16},{56,24},{64,32},{72,40},{80,48},{88,56},{96,... | collective-permute-start | bytes 393224 | tf_op jit(solution)/shard_map/ppermute | solution.py:22
  66.5 0.9 constant_dynamic-update-slice_fusion.4
  67.4 0.3 collective-permute-done.1
  67.7 0.9 constant_dynamic-update-slice_fusion.3
  68.6 0.9 constant_dynamic-update-slice_fusion.2
  69.5 0.9 constant_dynamic-update-slice_fusion.1
  70.5 0.9 constant_dynamic-update-slice_fusion
  71.4 0.7 copy.25
  72.1 0.6 pad.clone
  72.7 0.2 copy.21
  73.0 0.4 copy-done.2
  73.4 3.6 %fusion.26 = bf16[2,3,1,8,5,64]{5,3,4,1,0,2:T(8,128)(2,1)S(1)} fusion(bf16[3,3,3,1024,64]{3,4,2,1,0:T(8,128)(2,1)S(1)} %bitcast.53, bf16[2,5,1,7,2,1024]{5,3,4,1,0,2:T(8,128)(2,1)S(1)} %slice.22, bf16[2,5,1,8,5,1024]{5,3,4,1,0,2:T(8,128)(2,1)S(1)} %copy.21, f32[64]{0:T(128)S(1)} %copy-done.3, pred[3]{0:T(512)(128)(4,1)S(1)} %compare_and_fusion, ...), kind=kOutput, calls=%fused_computation.14 | convolution fusion | flops 569763840 | bytes 4675883 | tf_op jit(solution)/shard_map/conv_general_dilated | solution.py:63
  77.0 0.8 fusion.34
  77.8 0.3 copy.22
  78.1 0.8 copy.23
  78.9 1.9 %reshape_reshape_squeeze.3 = f32[64,2,8,64]{3,2,1,0:T(8,128)} reshape(f32[2,1,1,32,1024]{4,3,0,2,1:T(8,128)} %copy.23) | data formatting | bytes 524288 | tf_op jit(solution)/shard_map/reshape;reshape;squeeze | solution.py:85
  80.8 2.1 %copy.24 = f32[8,64,2,64]{3,2,1,0:T(2,128)} copy(f32[8,64,2,64]{3,0,2,1:T(8,128)} %bitcast.47) | data formatting | bytes 524288 | tf_op jit(solution)/shard_map/transpose | solution.py:85
  82.9 2.0 %reshape.32 = f32[8,64,128]{2,1,0:T(8,128)} reshape(f32[8,64,2,64]{3,2,1,0:T(2,128)} %copy.24) | data formatting | bytes 524288 | tf_op jit(solution)/shard_map/reshape | solution.py:86
  84.9 4.0 %all-to-all-start = ((f32[8,64,128]{2,1,0:T(8,128)}), f32[8,64,128]{2,1,0:T(8,128)}, u32[]{:S(2)}, u32[]{:S(2)}) async-start(f32[8,64,128]{2,1,0:T(8,128)} %reshape.32), calls=%async_computation | async-start | bytes 524288 | tf_op jit(solution)/shard_map/all_to_all | solution.py:87
  89.0 7.5 %all-to-all-done = f32[8,64,128]{2,1,0:T(8,128)} async-done(((f32[8,64,128]{2,1,0:T(8,128)}), f32[8,64,128]{2,1,0:T(8,128)}, u32[]{:S(2)}, u32[]{:S(2)}) %all-to-all-start) | async-done | bytes 262176 | tf_op jit(solution)/shard_map/all_to_all | solution.py:87
  96.5 1.6 %reduce_sum.9 = f32[64,128]{1,0:T(8,128)} reduce(f32[8,64,128]{2,1,0:T(8,128)} %all-to-all-done, f32[]{:T(128)} %constant.23.clone.1), dimensions={0}, to_apply=%region_0.1 | reduce | flops 57344 | bytes 294916 | tf_op jit(solution)/shard_map/reduce_sum | solution.py:87
  98.1 0.9 slice_select_fusion.1
  99.0 22.9 %all-gather.2 = f32[128,64]{1,0:T(8,128)S(1)} all-gather(f32[64,64]{1,0:T(8,128)S(1)} %slice_select_fusion.1), channel_id=4, replica_groups=mesh['space'=64,'zh'=2,'inner'=8] {'zh'}, dimensions={0}, use_global_device_ids=true | all-gather | bytes 49152 | tf_op jit(solution)/shard_map/all_gather | solution.py:92
  121.9 0.9 fusion.44
  122.8 1.3 %add_convert_fusion = bf16[2,1,32,64]{3,2,1,0:T(8,128)(2,1)} fusion(f32[2,1,32,64]{3,2,1,0:T(8,128)S(1)} %bitcast.51, bf16[2,1,32,64]{3,2,1,0:T(8,128)(2,1)S(1)} %copy-done.1, f32[64]{0:T(128)} %param.9), kind=kLoop, calls=%fused_computation.32 | loop fusion | flops 16384 | bytes 33024 | tf_op jit(solution)/shard_map/convert_element_type | solution.py:110
  (16 shorter events, 0.2 us)
Async XLA Ops:
  0.0 77.0 %copy-start = (bf16[27,64,1024]{2,1,0:T(8,128)(2,1)S(1)}, bf16[27,64,1024]{2,1,0:T(8,128)(2,1)}, u32[]{:S(2)}) copy-start(bf16[27,64,1024]{2,1,0:T(8,128)(2,1)} %param.8) | copy-start | bytes 10616836
  45.6 20.8 %collective-permute-start = (bf16[2,1,32,1024]{3,2,0,1:T(8,128)(2,1)}, bf16[2,1,32,1024]{3,2,0,1:T(8,128)(2,1)}, u32[]{:S(2)}, u32[]{:S(2)}) collective-permute-start(bf16[2,1,32,1024]{3,2,0,1:T(8,128)(2,1)} %reshape.29), channel_id=1, source_target_pairs={{0,32},{8,40},{16,48},{24,56},{32,64},{40,72},{48,80},{56,88},{64,... | collective-permute-start | bytes 393224 | tf_op jit(solution)/shard_map/ppermute | solution.py:22
  49.3 18.4 %collective-permute-start.1 = (bf16[2,1,32,1024]{3,2,0,1:T(8,128)(2,1)}, bf16[2,1,32,1024]{3,2,0,1:T(8,128)(2,1)}, u32[]{:S(2)}, u32[]{:S(2)}) collective-permute-start(bf16[2,1,32,1024]{3,2,0,1:T(8,128)(2,1)} %reshape.29), channel_id=1, source_target_pairs={{0,16},{8,24},{16,32},{24,40},{32,48},{40,56},{48,64},{56,72},{64,... | collective-permute-start | bytes 393224 | tf_op jit(solution)/shard_map/ppermute | solution.py:22
  52.2 17.3 %collective-permute-start.2 = (bf16[2,1,32,1024]{3,2,0,1:T(8,128)(2,1)}, bf16[2,1,32,1024]{3,2,0,1:T(8,128)(2,1)}, u32[]{:S(2)}, u32[]{:S(2)}) collective-permute-start(bf16[2,1,32,1024]{3,2,0,1:T(8,128)(2,1)} %reshape.29), channel_id=1, source_target_pairs={{16,0},{24,8},{32,16},{40,24},{48,32},{56,40},{64,48},{72,56},{80,... | collective-permute-start | bytes 393224 | tf_op jit(solution)/shard_map/ppermute | solution.py:22
  61.6 8.8 %collective-permute-start.3 = (bf16[2,1,32,1024]{3,2,0,1:T(8,128)(2,1)}, bf16[2,1,32,1024]{3,2,0,1:T(8,128)(2,1)}, u32[]{:S(2)}, u32[]{:S(2)}) collective-permute-start(bf16[2,1,32,1024]{3,2,0,1:T(8,128)(2,1)} %reshape.29), channel_id=1, source_target_pairs={{32,0},{40,8},{48,16},{56,24},{64,32},{72,40},{80,48},{88,56},{96,... | collective-permute-start | bytes 393224 | tf_op jit(solution)/shard_map/ppermute | solution.py:22
  71.4 2.0 %copy-start.2 = (bf16[27,1024,64]{1,2,0:T(8,128)(2,1)S(1)}, bf16[27,1024,64]{1,2,0:T(8,128)(2,1)}, u32[]{:S(2)}) copy-start(bf16[27,1024,64]{1,2,0:T(8,128)(2,1)} %param.6) | copy-start | bytes 10616836
  71.4 2.0 %copy-start.3 = (f32[64]{0:T(128)S(1)}, f32[64]{0:T(128)}, u32[]{:S(2)}) copy-start(f32[64]{0:T(128)} %param.7) | copy-start | bytes 772
  71.4 2.0 %copy-start.4 = (pred[8,5]{0,1:T(8,128)(4,1)S(1)}, pred[8,5]{0,1:T(8,128)(4,1)}, u32[]{:S(2)}) copy-start(pred[8,5]{0,1:T(8,128)(4,1)} %constant.33) | copy-start | bytes 124
  78.1 44.7 %copy-start.1 = (bf16[2,1,32,64]{3,2,1,0:T(8,128)(2,1)S(1)}, bf16[2,1,32,64]{3,2,1,0:T(8,128)(2,1)}, u32[]{:S(2)}) copy-start(bf16[2,1,32,64]{3,2,1,0:T(8,128)(2,1)} %param.5) | copy-start | bytes 24580
  84.9 11.6 %all-to-all-start = ((f32[8,64,128]{2,1,0:T(8,128)}), f32[8,64,128]{2,1,0:T(8,128)}, u32[]{:S(2)}, u32[]{:S(2)}) async-start(f32[8,64,128]{2,1,0:T(8,128)} %reshape.32), calls=%async_computation | async-start | bytes 524288 | tf_op jit(solution)/shard_map/all_to_all | solution.py:87

commit v13 on v12

--- a/solution.py
+++ b/solution.py
@@ -4,8 +4,10 @@
 from jax.sharding import Mesh
 from jax.sharding import PartitionSpec as P
 
-CHAN = ("zh", "inner")
+CHAN = ("zh", "x", "core")
+INNER = ("x", "core")
 HALVES = 2
+CORES = 2
 RUN = 16
 
 
@@ -73,18 +75,20 @@
 
 def gather_channels(latent):
     pair = lax.all_gather(latent, "zh", axis=0, tiled=False)
-    inner = lax.all_gather(pair, "inner", axis=0, tiled=False)
+    chip = lax.all_gather(pair, "core", axis=0, tiled=False)
+    inner = lax.all_gather(chip, "x", axis=0, tiled=False)
+    inner = inner.reshape((-1,) + inner.shape[2:])
     frame_count, row_count, col_count, own_chan = latent.shape
     total = inner.shape[0] * HALVES * own_chan
     return jnp.transpose(inner, (2, 3, 4, 1, 0, 5)).reshape(frame_count, row_count, col_count, total)
 
 
 def reduce_channels(partial, own_chan):
-    inner_count = lax.axis_size("inner")
+    inner_count = lax.axis_size(INNER)
     cells = partial.shape[0]
     blocks = partial.reshape(cells, HALVES, inner_count, own_chan).transpose(2, 0, 1, 3)
     blocks = blocks.reshape(inner_count, cells, HALVES * own_chan)
-    sums = lax.all_to_all(blocks, "inner", 0, 0, tiled=True).sum(0)
+    sums = lax.all_to_all(blocks, INNER, 0, 0, tiled=True).sum(0)
     half = lax.axis_index("zh")
     low, high = sums[:, :own_chan], sums[:, own_chan:]
     mine = jnp.where(half == 0, low, high)
@@ -112,7 +116,9 @@
 
 def solution(mesh):
     space, chan = mesh.shape["space"], mesh.shape["chan"]
-    split = Mesh(mesh.devices.reshape(space, HALVES, chan // HALVES), ("space",) + CHAN)
+    split = Mesh(
+        mesh.devices.reshape(space, HALVES, chan // (HALVES * CORES), CORES), ("space",) + CHAN
+    )
     in_specs = (
         P(None, "space", None, CHAN),
         P(None, None, CHAN),

time: 125 us -> 126 us (level)
    all_gather x1 -> x2, blocking collectives: 13.2 us -> 14.4 us  [the longest x1 12.6 us: gather_channels(): inner = lax.all_gather(chip, 'x', axis=0, tiled=False)]
where the time goes in v13:
time: 126 us
  blocking collectives  67.1 us (53%)
  starting transfers between devices  24.8 us (20%)
  local copies, waits for them, and re-layouts  16.3 us (13%)
  waiting for transfers between devices  8 us (6%)
  other arithmetic  4.67 us (4%)
  matrix products  4.38 us (3%)
    all_gather x1, blocking collectives, gather_channels(): pair = lax.all_gather(latent, 'zh', axis=0, tiled=False)  29.8 us
    all_gather x1, blocking collectives, reduce_channels(): both = lax.all_gather(theirs, 'zh', axis=0, tiled=False)  22.9 us
    ppermute x4, starting transfers between devices, row_from(): return lax.ppermute(cells, ('space', 'zh'), pairs)  20.8 us
    all_gather x1, blocking collectives, gather_channels(): inner = lax.all_gather(chip, 'x', axis=0, tiled=False)  12.6 us
    all_to_all x1, waiting for transfers between devices, reduce_channels(): sums = lax.all_to_all(blocks, INNER, 0, 0, tiled=True).sum(0)  7.5 us
    unnamed x15, local copies, waits for them, and re-layouts  4.75 us
    conv_general_dilated x2, matrix products, conv3(): lax.conv_general_dilated(padded[None], taps, (1, 1, 1), ((1, 1), (0, 0),...  4.38 us
    all_to_all x1, starting transfers between devices, reduce_channels(): sums = lax.all_to_all(blocks, INNER, 0, 0, tiled=True).sum(0)  4.05 us
  transfers between devices with their start and end apart: 5, of which 2 were waited for; matrix products, arithmetic and copies ran while one was open for 3% of the time, Pallas kernels for 0%

profile of v13, /device:TPU:24, one launch (start us, length us, event | category | flops | bytes accessed | tf_op | source)
XLA Modules:
  0.0 125.5 jit_solution(9029518978425879851)
XLA Ops:
  0.0 29.8 %all-gather = bf16[4,1,32,64]{3,2,1,0:T(8,128)(2,1)S(1)} all-gather(bf16[2,1,32,64]{3,2,1,0:T(8,128)(2,1)} %param.5), channel_id=2, replica_groups=mesh['space'=64,'zh'=2,'x'=4,'core'=2] {'zh'}, dimensions={0}, use_global_device_ids=true | all-gather | bytes 24576 | tf_op jit(solution)/shard_map/all_gather | solution.py:77
  29.8 1.8 %all-gather.1 = bf16[4,2,1,32,64]{4,3,2,1,0:T(8,128)(2,1)S(1)} all-gather(bf16[2,2,1,32,64]{4,3,2,1,0:T(8,128)(2,1)S(1)} %bitcast.54), channel_id=3, replica_groups=mesh['space'=64,'zh'=2,'x'=4,'core'=2] {'core'}, dimensions={0}, use_global_device_ids=true | all-gather | bytes 49152 | tf_op jit(solution)/shard_map/all_gather | solution.py:78
  31.6 12.6 %all-gather.2 = bf16[8,2,2,1,32,64]{5,4,3,2,1,0:T(8,128)(2,1)S(1)} all-gather(bf16[2,2,2,1,32,64]{5,4,3,2,1,0:T(8,128)(2,1)S(1)} %bitcast.52), channel_id=4, replica_groups=mesh['space'=64,'zh'=2,'x'=4,'core'=2] {'x'}, dimensions={0}, use_global_device_ids=true | all-gather | bytes 163840 | tf_op jit(solution)/shard_map/all_gather | solution.py:79
  44.2 0.9 copy.19
  45.1 1.8 %reshape.33 = bf16[2,1,32,1024]{3,2,0,1:T(8,128)(2,1)} reshape(bf16[2,1,32,2,8,64]{5,4,3,2,0,1:T(8,128)(2,1)} %copy.19) | data formatting | bytes 262144 | tf_op jit(solution)/shard_map/reshape | solution.py:83
  46.9 3.6 %collective-permute-start = (bf16[2,1,32,1024]{3,2,0,1:T(8,128)(2,1)}, bf16[2,1,32,1024]{3,2,0,1:T(8,128)(2,1)}, u32[]{:S(2)}, u32[]{:S(2)}) collective-permute-start(bf16[2,1,32,1024]{3,2,0,1:T(8,128)(2,1)} %reshape.33), channel_id=1, source_target_pairs={{0,32},{8,40},{16,48},{24,56},{32,64},{40,72},{48,80},{56,88},{64,... | collective-permute-start | bytes 393224 | tf_op jit(solution)/shard_map/ppermute | solution.py:24
  50.5 2.9 %collective-permute-start.1 = (bf16[2,1,32,1024]{3,2,0,1:T(8,128)(2,1)}, bf16[2,1,32,1024]{3,2,0,1:T(8,128)(2,1)}, u32[]{:S(2)}, u32[]{:S(2)}) collective-permute-start(bf16[2,1,32,1024]{3,2,0,1:T(8,128)(2,1)} %reshape.33), channel_id=1, source_target_pairs={{0,16},{8,24},{16,32},{24,40},{32,48},{40,56},{48,64},{56,72},{64,... | collective-permute-start | bytes 393224 | tf_op jit(solution)/shard_map/ppermute | solution.py:24
  53.5 9.4 %collective-permute-start.2 = (bf16[2,1,32,1024]{3,2,0,1:T(8,128)(2,1)}, bf16[2,1,32,1024]{3,2,0,1:T(8,128)(2,1)}, u32[]{:S(2)}, u32[]{:S(2)}) collective-permute-start(bf16[2,1,32,1024]{3,2,0,1:T(8,128)(2,1)} %reshape.33), channel_id=1, source_target_pairs={{16,0},{24,8},{32,16},{40,24},{48,32},{56,40},{64,48},{72,56},{80,... | collective-permute-start | bytes 393224 | tf_op jit(solution)/shard_map/ppermute | solution.py:24
  62.9 4.8 %collective-permute-start.3 = (bf16[2,1,32,1024]{3,2,0,1:T(8,128)(2,1)}, bf16[2,1,32,1024]{3,2,0,1:T(8,128)(2,1)}, u32[]{:S(2)}, u32[]{:S(2)}) collective-permute-start(bf16[2,1,32,1024]{3,2,0,1:T(8,128)(2,1)} %reshape.33), channel_id=1, source_target_pairs={{32,0},{40,8},{48,16},{56,24},{64,32},{72,40},{80,48},{88,56},{96,... | collective-permute-start | bytes 393224 | tf_op jit(solution)/shard_map/ppermute | solution.py:24
  67.7 0.9 constant_dynamic-update-slice_fusion.4
  68.7 0.9 constant_dynamic-update-slice_fusion.3
  69.6 0.9 constant_dynamic-update-slice_fusion.2
  70.5 0.9 constant_dynamic-update-slice_fusion.1
  71.4 0.5 collective-permute-done.3
  71.9 0.9 constant_dynamic-update-slice_fusion
  72.9 0.7 copy.26
  73.6 0.6 pad.clone
  74.5 0.4 copy-done.2
  74.9 3.6 %fusion.26 = bf16[2,3,1,8,5,64]{5,3,4,1,0,2:T(8,128)(2,1)S(1)} fusion(bf16[3,3,3,1024,64]{3,4,2,1,0:T(8,128)(2,1)S(1)} %bitcast.55, bf16[2,5,1,7,2,1024]{5,3,4,1,0,2:T(8,128)(2,1)S(1)} %slice.22, bf16[2,5,1,8,5,1024]{5,3,4,1,0,2:T(8,128)(2,1)S(1)} %copy.22, f32[64]{0:T(128)S(1)} %copy-done.3, pred[3]{0:T(512)(128)(4,1)S(1)} %compare_and_fusion, ...), kind=kOutput, calls=%fused_computation.14 | convolution fusion | flops 569763840 | bytes 4675883 | tf_op jit(solution)/shard_map/conv_general_dilated | solution.py:65
  78.5 0.8 fusion.34
  79.3 0.3 copy.23
  79.6 0.8 copy.24
  80.4 1.9 %reshape_reshape_squeeze.3 = f32[64,2,8,64]{3,2,1,0:T(8,128)} reshape(f32[2,1,1,32,1024]{4,3,0,2,1:T(8,128)} %copy.24) | data formatting | bytes 524288 | tf_op jit(solution)/shard_map/reshape;reshape;squeeze | solution.py:89
  82.3 2.1 %copy.25 = f32[8,64,2,64]{3,2,1,0:T(2,128)} copy(f32[8,64,2,64]{3,0,2,1:T(8,128)} %bitcast.48) | data formatting | bytes 524288 | tf_op jit(solution)/shard_map/transpose | solution.py:89
  84.3 2.0 %reshape.36 = f32[8,64,128]{2,1,0:T(8,128)} reshape(f32[8,64,2,64]{3,2,1,0:T(2,128)} %copy.25) | data formatting | bytes 524288 | tf_op jit(solution)/shard_map/reshape | solution.py:90
  86.4 4.0 %all-to-all-start = ((f32[8,64,128]{2,1,0:T(8,128)}), f32[8,64,128]{2,1,0:T(8,128)}, u32[]{:S(2)}, u32[]{:S(2)}) async-start(f32[8,64,128]{2,1,0:T(8,128)} %reshape.36), calls=%async_computation | async-start | bytes 524288 | tf_op jit(solution)/shard_map/all_to_all | solution.py:91
  90.5 7.5 %all-to-all-done = f32[8,64,128]{2,1,0:T(8,128)} async-done(((f32[8,64,128]{2,1,0:T(8,128)}), f32[8,64,128]{2,1,0:T(8,128)}, u32[]{:S(2)}, u32[]{:S(2)}) %all-to-all-start) | async-done | bytes 262176 | tf_op jit(solution)/shard_map/all_to_all | solution.py:91
  98.0 1.6 %reduce_sum.9 = f32[64,128]{1,0:T(8,128)} reduce(f32[8,64,128]{2,1,0:T(8,128)} %all-to-all-done, f32[]{:T(128)} %constant.23.clone.1), dimensions={0}, to_apply=%region_0.1 | reduce | flops 57344 | bytes 294916 | tf_op jit(solution)/shard_map/reduce_sum | solution.py:91
  99.5 0.9 slice_select_fusion.1
  100.4 22.9 %all-gather.3 = f32[128,64]{1,0:T(8,128)S(1)} all-gather(f32[64,64]{1,0:T(8,128)S(1)} %slice_select_fusion.1), channel_id=5, replica_groups=mesh['space'=64,'zh'=2,'x'=4,'core'=2] {'zh'}, dimensions={0}, use_global_device_ids=true | all-gather | bytes 49152 | tf_op jit(solution)/shard_map/all_gather | solution.py:96
  123.3 0.9 fusion.44
  124.2 1.3 %add_convert_fusion = bf16[2,1,32,64]{3,2,1,0:T(8,128)(2,1)} fusion(f32[2,1,32,64]{3,2,1,0:T(8,128)S(1)} %bitcast.53, bf16[2,1,32,64]{3,2,1,0:T(8,128)(2,1)S(1)} %copy-done.1, f32[64]{0:T(128)} %param.9), kind=kLoop, calls=%fused_computation.32 | loop fusion | flops 16384 | bytes 33024 | tf_op jit(solution)/shard_map/convert_element_type | solution.py:114
  (17 shorter events, 0.4 us)
Async XLA Ops:
  0.0 78.5 %copy-start = (bf16[27,64,1024]{2,1,0:T(8,128)(2,1)S(1)}, bf16[27,64,1024]{2,1,0:T(8,128)(2,1)}, u32[]{:S(2)}) copy-start(bf16[27,64,1024]{2,1,0:T(8,128)(2,1)} %param.8) | copy-start | bytes 10616836
  46.9 20.8 %collective-permute-start = (bf16[2,1,32,1024]{3,2,0,1:T(8,128)(2,1)}, bf16[2,1,32,1024]{3,2,0,1:T(8,128)(2,1)}, u32[]{:S(2)}, u32[]{:S(2)}) collective-permute-start(bf16[2,1,32,1024]{3,2,0,1:T(8,128)(2,1)} %reshape.33), channel_id=1, source_target_pairs={{0,32},{8,40},{16,48},{24,56},{32,64},{40,72},{48,80},{56,88},{64,... | collective-permute-start | bytes 393224 | tf_op jit(solution)/shard_map/ppermute | solution.py:24
  50.5 18.1 %collective-permute-start.1 = (bf16[2,1,32,1024]{3,2,0,1:T(8,128)(2,1)}, bf16[2,1,32,1024]{3,2,0,1:T(8,128)(2,1)}, u32[]{:S(2)}, u32[]{:S(2)}) collective-permute-start(bf16[2,1,32,1024]{3,2,0,1:T(8,128)(2,1)} %reshape.33), channel_id=1, source_target_pairs={{0,16},{8,24},{16,32},{24,40},{32,48},{40,56},{48,64},{56,72},{64,... | collective-permute-start | bytes 393224 | tf_op jit(solution)/shard_map/ppermute | solution.py:24
  53.5 17.0 %collective-permute-start.2 = (bf16[2,1,32,1024]{3,2,0,1:T(8,128)(2,1)}, bf16[2,1,32,1024]{3,2,0,1:T(8,128)(2,1)}, u32[]{:S(2)}, u32[]{:S(2)}) collective-permute-start(bf16[2,1,32,1024]{3,2,0,1:T(8,128)(2,1)} %reshape.33), channel_id=1, source_target_pairs={{16,0},{24,8},{32,16},{40,24},{48,32},{56,40},{64,48},{72,56},{80,... | collective-permute-start | bytes 393224 | tf_op jit(solution)/shard_map/ppermute | solution.py:24
  62.9 9.0 %collective-permute-start.3 = (bf16[2,1,32,1024]{3,2,0,1:T(8,128)(2,1)}, bf16[2,1,32,1024]{3,2,0,1:T(8,128)(2,1)}, u32[]{:S(2)}, u32[]{:S(2)}) collective-permute-start(bf16[2,1,32,1024]{3,2,0,1:T(8,128)(2,1)} %reshape.33), channel_id=1, source_target_pairs={{32,0},{40,8},{48,16},{56,24},{64,32},{72,40},{80,48},{88,56},{96,... | collective-permute-start | bytes 393224 | tf_op jit(solution)/shard_map/ppermute | solution.py:24
  72.8 2.0 %copy-start.2 = (bf16[27,1024,64]{1,2,0:T(8,128)(2,1)S(1)}, bf16[27,1024,64]{1,2,0:T(8,128)(2,1)}, u32[]{:S(2)}) copy-start(bf16[27,1024,64]{1,2,0:T(8,128)(2,1)} %param.6) | copy-start | bytes 10616836
  72.9 2.0 %copy-start.3 = (f32[64]{0:T(128)S(1)}, f32[64]{0:T(128)}, u32[]{:S(2)}) copy-start(f32[64]{0:T(128)} %param.7) | copy-start | bytes 772
  72.9 2.0 %copy-start.4 = (pred[8,5]{0,1:T(8,128)(4,1)S(1)}, pred[8,5]{0,1:T(8,128)(4,1)}, u32[]{:S(2)}) copy-start(pred[8,5]{0,1:T(8,128)(4,1)} %constant.33) | copy-start | bytes 124
  79.6 44.7 %copy-start.1 = (bf16[2,1,32,64]{3,2,1,0:T(8,128)(2,1)S(1)}, bf16[2,1,32,64]{3,2,1,0:T(8,128)(2,1)}, u32[]{:S(2)}) copy-start(bf16[2,1,32,64]{3,2,1,0:T(8,128)(2,1)} %param.5) | copy-start | bytes 24580
  86.4 11.6 %all-to-all-start = ((f32[8,64,128]{2,1,0:T(8,128)}), f32[8,64,128]{2,1,0:T(8,128)}, u32[]{:S(2)}, u32[]{:S(2)}) async-start(f32[8,64,128]{2,1,0:T(8,128)} %reshape.36), calls=%async_computation | async-start | bytes 524288 | tf_op jit(solution)/shard_map/all_to_all | solution.py:91

commit v14 on v12

--- a/solution.py
+++ b/solution.py
@@ -89,7 +89,8 @@
     low, high = sums[:, :own_chan], sums[:, own_chan:]
     mine = jnp.where(half == 0, low, high)
     theirs = jnp.where(half == 0, high, low)
-    both = lax.all_gather(theirs, "zh", axis=0, tiled=False)
+    dense = theirs.reshape(-1, 2 * theirs.shape[1])
+    both = lax.all_gather(dense, "zh", axis=0, tiled=False).reshape((HALVES,) + theirs.shape)
     return mine + jnp.where(half == 0, both[1], both[0])
 
 

time: 125 us -> 127 us (1.016)
  local copies, waits for them, and re-layouts: 16.3 us -> 17.8 us
    unnamed x15 -> x13, local copies, waits for them, and re-layouts: 4.75 us -> 4.74 us
where the time goes in v14:
time: 127 us; the launch traced here: 126 us
  blocking collectives  65.7 us (52%)
  starting transfers between devices  24.8 us (20%)
  local copies, waits for them, and re-layouts  17.8 us (14%)
  waiting for transfers between devices  7.8 us (6%)
  other arithmetic  5.36 us (4%)
  matrix products  4.39 us (3%)
    all_gather x1, blocking collectives, gather_channels(): pair = lax.all_gather(latent, 'zh', axis=0, tiled=False)  29.8 us
    all_gather x1, blocking collectives, reduce_channels(): lax.all_gather(dense, 'zh', axis=0, tiled=False)  22.7 us
    ppermute x4, starting transfers between devices, row_from(): return lax.ppermute(cells, ('space', 'zh'), pairs)  20.8 us
    all_gather x1, blocking collectives, gather_channels(): inner = lax.all_gather(pair, 'inner', axis=0, tiled=False)  13.2 us
    all_to_all x1, waiting for transfers between devices, reduce_channels(): sums = lax.all_to_all(blocks, 'inner', 0, 0, tiled=True).sum(0)  7.5 us
    unnamed x13, local copies, waits for them, and re-layouts  4.74 us
    conv_general_dilated x2, matrix products, conv3(): lax.conv_general_dilated(padded[None], taps, (1, 1, 1), ((1, 1), (0, 0),...  4.39 us
    all_to_all x1, starting transfers between devices, reduce_channels(): sums = lax.all_to_all(blocks, 'inner', 0, 0, tiled=True).sum(0)  4.04 us
  transfers between devices with their start and end apart: 5, of which 2 were waited for; matrix products, arithmetic and copies ran while one was open for 3% of the time, Pallas kernels for 0%

profile of v14, /device:TPU:24, one launch (start us, length us, event | category | flops | bytes accessed | tf_op | source)
XLA Modules:
  0.0 126.1 jit_solution(2267215505229678723)
XLA Ops:
  0.0 29.8 %all-gather = bf16[4,1,32,64]{3,2,1,0:T(8,128)(2,1)S(1)} all-gather(bf16[2,1,32,64]{3,2,1,0:T(8,128)(2,1)} %param.5), channel_id=2, replica_groups=mesh['space'=64,'zh'=2,'inner'=8] {'zh'}, dimensions={0}, use_global_device_ids=true | all-gather | bytes 24576 | tf_op jit(solution)/shard_map/all_gather | solution.py:75
  29.8 13.2 %all-gather.1 = bf16[16,2,1,32,64]{4,3,2,1,0:T(8,128)(2,1)S(1)} all-gather(bf16[2,2,1,32,64]{4,3,2,1,0:T(8,128)(2,1)S(1)} %bitcast.51), channel_id=3, replica_groups=mesh['space'=64,'zh'=2,'inner'=8] {'inner'}, dimensions={0}, use_global_device_ids=true | all-gather | bytes 147456 | tf_op jit(solution)/shard_map/all_gather | solution.py:76
  43.0 0.9 copy.18
  43.8 1.8 %reshape.34 = bf16[2,1,32,1024]{3,2,0,1:T(8,128)(2,1)} reshape(bf16[2,1,32,2,8,64]{5,4,3,2,0,1:T(8,128)(2,1)} %copy.18) | data formatting | bytes 262144 | tf_op jit(solution)/shard_map/reshape | solution.py:79
  45.6 3.6 %collective-permute-start = (bf16[2,1,32,1024]{3,2,0,1:T(8,128)(2,1)}, bf16[2,1,32,1024]{3,2,0,1:T(8,128)(2,1)}, u32[]{:S(2)}, u32[]{:S(2)}) collective-permute-start(bf16[2,1,32,1024]{3,2,0,1:T(8,128)(2,1)} %reshape.34), channel_id=1, source_target_pairs={{0,32},{8,40},{16,48},{24,56},{32,64},{40,72},{48,80},{56,88},{64,... | collective-permute-start | bytes 393224 | tf_op jit(solution)/shard_map/ppermute | solution.py:22
  49.3 2.9 %collective-permute-start.1 = (bf16[2,1,32,1024]{3,2,0,1:T(8,128)(2,1)}, bf16[2,1,32,1024]{3,2,0,1:T(8,128)(2,1)}, u32[]{:S(2)}, u32[]{:S(2)}) collective-permute-start(bf16[2,1,32,1024]{3,2,0,1:T(8,128)(2,1)} %reshape.34), channel_id=1, source_target_pairs={{0,16},{8,24},{16,32},{24,40},{32,48},{40,56},{48,64},{56,72},{64,... | collective-permute-start | bytes 393224 | tf_op jit(solution)/shard_map/ppermute | solution.py:22
  52.2 9.4 %collective-permute-start.2 = (bf16[2,1,32,1024]{3,2,0,1:T(8,128)(2,1)}, bf16[2,1,32,1024]{3,2,0,1:T(8,128)(2,1)}, u32[]{:S(2)}, u32[]{:S(2)}) collective-permute-start(bf16[2,1,32,1024]{3,2,0,1:T(8,128)(2,1)} %reshape.34), channel_id=1, source_target_pairs={{16,0},{24,8},{32,16},{40,24},{48,32},{56,40},{64,48},{72,56},{80,... | collective-permute-start | bytes 393224 | tf_op jit(solution)/shard_map/ppermute | solution.py:22
  61.6 4.8 %collective-permute-start.3 = (bf16[2,1,32,1024]{3,2,0,1:T(8,128)(2,1)}, bf16[2,1,32,1024]{3,2,0,1:T(8,128)(2,1)}, u32[]{:S(2)}, u32[]{:S(2)}) collective-permute-start(bf16[2,1,32,1024]{3,2,0,1:T(8,128)(2,1)} %reshape.34), channel_id=1, source_target_pairs={{32,0},{40,8},{48,16},{56,24},{64,32},{72,40},{80,48},{88,56},{96,... | collective-permute-start | bytes 393224 | tf_op jit(solution)/shard_map/ppermute | solution.py:22
  66.5 0.9 constant_dynamic-update-slice_fusion.4
  67.4 0.3 collective-permute-done.1
  67.7 0.9 constant_dynamic-update-slice_fusion.3
  68.6 0.9 constant_dynamic-update-slice_fusion.2
  69.5 0.9 constant_dynamic-update-slice_fusion.1
  70.4 0.9 constant_dynamic-update-slice_fusion
  71.4 0.7 copy.25
  72.1 0.6 pad.clone
  73.0 0.4 copy-done.1
  73.4 3.6 %fusion.26 = bf16[2,3,1,8,5,64]{5,3,4,1,0,2:T(8,128)(2,1)S(1)} fusion(bf16[3,3,3,1024,64]{3,4,2,1,0:T(8,128)(2,1)S(1)} %bitcast.53, bf16[2,5,1,7,2,1024]{5,3,4,1,0,2:T(8,128)(2,1)S(1)} %slice.22, bf16[2,5,1,8,5,1024]{5,3,4,1,0,2:T(8,128)(2,1)S(1)} %copy.21, f32[64]{0:T(128)S(1)} %copy-done.2, pred[3]{0:T(512)(128)(4,1)S(1)} %compare_and_fusion, ...), kind=kOutput, calls=%fused_computation.14 | convolution fusion | flops 569763840 | bytes 4675883 | tf_op jit(solution)/shard_map/conv_general_dilated | solution.py:63
  77.0 0.8 fusion.34
  78.1 0.8 copy.23
  78.9 1.9 %reshape_reshape_squeeze.3 = f32[64,2,8,64]{3,2,1,0:T(8,128)} reshape(f32[2,1,1,32,1024]{4,3,0,2,1:T(8,128)} %copy.23) | data formatting | bytes 524288 | tf_op jit(solution)/shard_map/reshape;reshape;squeeze | solution.py:85
  80.8 2.1 %copy.24 = f32[8,64,2,64]{3,2,1,0:T(2,128)} copy(f32[8,64,2,64]{3,0,2,1:T(8,128)} %bitcast.47) | data formatting | bytes 524288 | tf_op jit(solution)/shard_map/transpose | solution.py:85
  82.9 2.1 %reshape.37 = f32[8,64,128]{2,1,0:T(8,128)} reshape(f32[8,64,2,64]{3,2,1,0:T(2,128)} %copy.24) | data formatting | bytes 524288 | tf_op jit(solution)/shard_map/reshape | solution.py:86
  84.9 4.0 %all-to-all-start = ((f32[8,64,128]{2,1,0:T(8,128)}), f32[8,64,128]{2,1,0:T(8,128)}, u32[]{:S(2)}, u32[]{:S(2)}) async-start(f32[8,64,128]{2,1,0:T(8,128)} %reshape.37), calls=%async_computation | async-start | bytes 524288 | tf_op jit(solution)/shard_map/all_to_all | solution.py:87
  89.0 7.5 %all-to-all-done = f32[8,64,128]{2,1,0:T(8,128)} async-done(((f32[8,64,128]{2,1,0:T(8,128)}), f32[8,64,128]{2,1,0:T(8,128)}, u32[]{:S(2)}, u32[]{:S(2)}) %all-to-all-start) | async-done | bytes 262176 | tf_op jit(solution)/shard_map/all_to_all | solution.py:87
  96.5 1.6 %reduce_sum.9 = f32[64,128]{1,0:T(8,128)} reduce(f32[8,64,128]{2,1,0:T(8,128)} %all-to-all-done, f32[]{:T(128)} %constant.23.clone.1), dimensions={0}, to_apply=%region_0.1 | reduce | flops 57344 | bytes 294916 | tf_op jit(solution)/shard_map/reduce_sum | solution.py:87
  98.1 1.5 %slice_select_fusion = f32[64,64]{1,0:T(8,128)} fusion(f32[64,128]{1,0:T(8,128)} %reduce_sum.9, pred[]{:T(512)S(6)} %eq.2), kind=kLoop, calls=%fused_computation.32 | loop fusion | flops 4096 | bytes 49153 | tf_op jit(solution)/shard_map/jit(_where)/select_n | solution.py:91
  99.6 0.8 all_gather_reshape.3
  100.4 22.7 %all_gather.19 = f32[2,32,128]{2,1,0:T(8,128)S(1)} all-gather(f32[1,32,128]{2,1,0:T(8,128)S(1)} %all_gather_reshape.3), channel_id=1, replica_groups=mesh['space'=64,'zh'=2,'inner'=8] {'zh'}, dimensions={0}, use_global_device_ids=true | all-gather | bytes 49152 | tf_op jit(solution)/shard_map/all_gather | solution.py:93
  123.2 0.7 select_n.32
  123.8 0.9 select_add_fusion
  124.7 1.3 %add_convert_fusion = bf16[2,1,32,64]{3,2,1,0:T(8,128)(2,1)} fusion(f32[2,1,32,64]{3,2,1,0:T(8,128)S(1)} %bitcast.52, bf16[2,1,32,64]{3,2,1,0:T(8,128)(2,1)} %param.5, f32[64]{0:T(128)} %param.9), kind=kLoop, calls=%fused_computation.30 | loop fusion | flops 16384 | bytes 33024 | tf_op jit(solution)/shard_map/convert_element_type | solution.py:111
  (17 shorter events, 0.6 us)
Async XLA Ops:
  0.0 77.0 %copy-start = (bf16[27,64,1024]{2,1,0:T(8,128)(2,1)S(1)}, bf16[27,64,1024]{2,1,0:T(8,128)(2,1)}, u32[]{:S(2)}) copy-start(bf16[27,64,1024]{2,1,0:T(8,128)(2,1)} %param.8) | copy-start | bytes 10616836
  45.6 20.8 %collective-permute-start = (bf16[2,1,32,1024]{3,2,0,1:T(8,128)(2,1)}, bf16[2,1,32,1024]{3,2,0,1:T(8,128)(2,1)}, u32[]{:S(2)}, u32[]{:S(2)}) collective-permute-start(bf16[2,1,32,1024]{3,2,0,1:T(8,128)(2,1)} %reshape.34), channel_id=1, source_target_pairs={{0,32},{8,40},{16,48},{24,56},{32,64},{40,72},{48,80},{56,88},{64,... | collective-permute-start | bytes 393224 | tf_op jit(solution)/shard_map/ppermute | solution.py:22
  49.3 18.4 %collective-permute-start.1 = (bf16[2,1,32,1024]{3,2,0,1:T(8,128)(2,1)}, bf16[2,1,32,1024]{3,2,0,1:T(8,128)(2,1)}, u32[]{:S(2)}, u32[]{:S(2)}) collective-permute-start(bf16[2,1,32,1024]{3,2,0,1:T(8,128)(2,1)} %reshape.34), channel_id=1, source_target_pairs={{0,16},{8,24},{16,32},{24,40},{32,48},{40,56},{48,64},{56,72},{64,... | collective-permute-start | bytes 393224 | tf_op jit(solution)/shard_map/ppermute | solution.py:22
  52.2 17.3 %collective-permute-start.2 = (bf16[2,1,32,1024]{3,2,0,1:T(8,128)(2,1)}, bf16[2,1,32,1024]{3,2,0,1:T(8,128)(2,1)}, u32[]{:S(2)}, u32[]{:S(2)}) collective-permute-start(bf16[2,1,32,1024]{3,2,0,1:T(8,128)(2,1)} %reshape.34), channel_id=1, source_target_pairs={{16,0},{24,8},{32,16},{40,24},{48,32},{56,40},{64,48},{72,56},{80,... | collective-permute-start | bytes 393224 | tf_op jit(solution)/shard_map/ppermute | solution.py:22
  61.6 8.8 %collective-permute-start.3 = (bf16[2,1,32,1024]{3,2,0,1:T(8,128)(2,1)}, bf16[2,1,32,1024]{3,2,0,1:T(8,128)(2,1)}, u32[]{:S(2)}, u32[]{:S(2)}) collective-permute-start(bf16[2,1,32,1024]{3,2,0,1:T(8,128)(2,1)} %reshape.34), channel_id=1, source_target_pairs={{32,0},{40,8},{48,16},{56,24},{64,32},{72,40},{80,48},{88,56},{96,... | collective-permute-start | bytes 393224 | tf_op jit(solution)/shard_map/ppermute | solution.py:22
  71.4 2.0 %copy-start.1 = (bf16[27,1024,64]{1,2,0:T(8,128)(2,1)S(1)}, bf16[27,1024,64]{1,2,0:T(8,128)(2,1)}, u32[]{:S(2)}) copy-start(bf16[27,1024,64]{1,2,0:T(8,128)(2,1)} %param.6) | copy-start | bytes 10616836
  71.4 2.0 %copy-start.2 = (f32[64]{0:T(128)S(1)}, f32[64]{0:T(128)}, u32[]{:S(2)}) copy-start(f32[64]{0:T(128)} %param.7) | copy-start | bytes 772
  71.4 2.0 %copy-start.3 = (pred[8,5]{0,1:T(8,128)(4,1)S(1)}, pred[8,5]{0,1:T(8,128)(4,1)}, u32[]{:S(2)}) copy-start(pred[8,5]{0,1:T(8,128)(4,1)} %constant.33) | copy-start | bytes 124
  84.9 11.6 %all-to-all-start = ((f32[8,64,128]{2,1,0:T(8,128)}), f32[8,64,128]{2,1,0:T(8,128)}, u32[]{:S(2)}, u32[]{:S(2)}) async-start(f32[8,64,128]{2,1,0:T(8,128)} %reshape.37), calls=%async_computation | async-start | bytes 524288 | tf_op jit(solution)/shard_map/all_to_all | solution.py:87
